TPU v7x, 256 devices: a whole 4x4x8 slice. The times are simulated.
256 devices in a mesh: lat: 16 (over z, y_hi), lon: 16 (over y_lo, x, core).
Axes of the slice: x: 4, y: 4 (y_hi: 2, y_lo: 2; y = y_hi * 2 + y_lo), z: 8, core: 2. Of those that a mesh axis runs over, the one named last changes fastest.
Arguments:
- meridian_slab_data: bfloat16 [512, 96, 4096], P('lat', None, 'lon'), may hold values from -6 to 6
- smoothing_filter_taps: bfloat16 [3, 3, 96, 128], replicated, may hold values from -0.21875 to 0.21875
- smoothing_offset_entries: float32 [128], replicated, may hold values from -3 to 3
- opening_coarsen_taps: bfloat16 [4, 4, 128, 256], replicated, may hold values from -0.125 to 0.125
- opening_coarsen_offset: float32 [256], replicated, may hold values from -3 to 3
- closing_coarsen_taps: bfloat16 [4, 4, 256, 256], replicated, may hold values from -0.09375 to 0.09375
- closing_coarsen_offset: float32 [256], replicated, may hold values from -3 to 3
- layernorm_multiplier: float32 [256], replicated, may hold values from 0.25 to 1.75
- triple_mapping_matrix: bfloat16 [256, 768], replicated, may hold values from -0.375 to 0.375
- logit_sharpness: float32 [8], replicated, may hold values from 2.5 to 40, as said below
- mixing_return_matrix: bfloat16 [256, 256], replicated, may hold values from -0.375 to 0.375
Outputs:
- encoded: bfloat16 [128, 1024, 256], P('lat', 'lon')
Inputs may be any that keep to these rules, and one draw needn't show every extreme that they name: `logit_sharpness`: per-head score scales.
All inputs are finite; a program needn't handle non-finite values.
Results may differ from a plain program's by a relative error of at most 0.034.
Values may be sent and summed in bfloat16 or wider, within the bound.
No kernel may reach another device: no remote copies, remote signals or barrier semaphores. Data moves between devices by JAX's collectives and lax.ppermute only.
A program may use at most 128 MiB of HBM per device.

v0:
```python
import jax
import jax.numpy as jnp
from jax import lax
from jax.sharding import PartitionSpec as P

HEADS = 8
HALO = 4


def extend_lat(value, width):
    size, length = lax.axis_size("lat"), value.shape[0]
    up = [(i, i + 1) for i in range(size - 1)]
    down = [(i + 1, i) for i in range(size - 1)]
    before = lax.ppermute(value[length - width :], "lat", up)
    after = lax.ppermute(value[:width], "lat", down)
    return jnp.concatenate([before, value, after], axis=0)


def extend_lon(value, width, dim):
    size, length = lax.axis_size("lon"), value.shape[dim]
    up = [(i, (i + 1) % size) for i in range(size)]
    down = [(j, i) for i, j in up]
    last = lax.slice_in_dim(value, length - width, length, axis=dim)
    initial = lax.slice_in_dim(value, 0, width, axis=dim)
    before = lax.ppermute(last, "lon", up)
    after = lax.ppermute(initial, "lon", down)
    return jnp.concatenate([before, value, after], axis=dim)


def clear_outside(value, start, total):
    count = value.shape[0]
    rows = start + jnp.arange(count)
    keep = (rows >= 0) & (rows < total)
    shape = (count,) + (1,) * (value.ndim - 1)
    return jnp.where(keep.reshape(shape), value, jnp.zeros_like(value))


def first_conv(extended, kernel, bias):
    total = lax.conv_general_dilated(
        extended[None],
        kernel,
        (1, 1),
        "VALID",
        dimension_numbers=("NHCW", "HWIO", "NHWC"),
        preferred_element_type=jnp.float32,
    )[0]
    return jax.nn.silu(total + bias).astype(jnp.bfloat16)


def halving_filter(extended, kernel, bias):
    total = lax.conv_general_dilated(
        extended[None],
        kernel,
        (2, 2),
        "VALID",
        dimension_numbers=("NHWC", "HWIO", "NHWC"),
        preferred_element_type=jnp.float32,
    )[0]
    return jax.nn.silu(total + bias).astype(jnp.bfloat16)


def on_device(
    meridian_slab_data,
    smoothing_filter_taps,
    smoothing_offset_entries,
    opening_coarsen_taps,
    opening_coarsen_offset,
    closing_coarsen_taps,
    closing_coarsen_offset,
    layernorm_multiplier,
    triple_mapping_matrix,
    logit_sharpness,
    mixing_return_matrix,
):
    band = meridian_slab_data.shape[0]
    lat_total = band * lax.axis_size("lat")
    base = lax.axis_index("lat") * band
    extended = extend_lat(meridian_slab_data, HALO)
    extended = extend_lon(extended, HALO, 2)
    opening_halved = first_conv(extended, smoothing_filter_taps, smoothing_offset_entries)
    opening_halved = clear_outside(opening_halved, base - HALO + 1, lat_total)
    closing_halved = halving_filter(opening_halved, opening_coarsen_taps, opening_coarsen_offset)
    closing_halved = clear_outside(closing_halved, base // 2 - 1, lat_total // 2)
    closing_halved = lax.optimization_barrier(closing_halved)
    activation_maps = halving_filter(
        closing_halved, closing_coarsen_taps, closing_coarsen_offset
    )
    rows, tokens, widths = activation_maps.shape
    per_group_channel_count = widths // HEADS
    upcast = activation_maps.astype(jnp.float32)
    mean = jnp.mean(upcast, axis=-1, keepdims=True)
    centred = upcast - mean
    variance = jnp.mean(centred * centred, axis=-1, keepdims=True)
    normed = (centred * lax.rsqrt(variance + 1e-05) * layernorm_multiplier).astype(jnp.bfloat16)
    projected = jnp.dot(normed, triple_mapping_matrix, preferred_element_type=jnp.float32)
    shape = (rows, tokens, HEADS, per_group_channel_count)
    logit_multiplier = (logit_sharpness / jnp.sqrt(jnp.float32(per_group_channel_count)))[:, None]
    query = (projected[..., :widths].reshape(shape) * logit_multiplier).astype(jnp.bfloat16)
    key = projected[..., widths : 2 * widths].reshape(shape).astype(jnp.bfloat16)
    value = projected[..., 2 * widths :].reshape(shape).astype(jnp.bfloat16)

    sectors = lax.axis_size("lon")
    items = rows * HEADS
    per_device = items // sectors
    trio = jnp.concatenate([query, key, value], axis=-1)
    trio = jnp.transpose(trio, (0, 2, 1, 3)).reshape(sectors, per_device, tokens, 3 * per_group_channel_count)
    trio = lax.all_to_all(trio, "lon", 0, 0, tiled=True)
    trio = jnp.transpose(trio, (1, 0, 2, 3)).reshape(per_device, sectors * tokens, 3 * per_group_channel_count)
    q_items = trio[..., :per_group_channel_count]
    k_items = trio[..., per_group_channel_count : 2 * per_group_channel_count]
    v_items = trio[..., 2 * per_group_channel_count :]
    scores = jnp.einsum("isd,itd->ist", q_items, k_items, preferred_element_type=jnp.float32)
    best = jnp.max(scores, axis=-1, keepdims=True)
    weights = jnp.exp(scores - best)
    total = jnp.sum(weights, axis=-1, keepdims=True)
    summed = jnp.einsum(
        "ist,itd->isd", weights.astype(jnp.bfloat16), v_items, preferred_element_type=jnp.float32
    )
    attended = (summed / total).astype(jnp.bfloat16)
    attended = attended.reshape(per_device, sectors, tokens, per_group_channel_count)
    attended = jnp.transpose(attended, (1, 0, 2, 3))
    attended = lax.all_to_all(attended, "lon", 0, 0, tiled=True)
    attended = attended.reshape(rows, HEADS, tokens, per_group_channel_count)
    joined = jnp.transpose(attended, (0, 2, 1, 3)).reshape(rows, tokens, widths)
    mixed_out = jnp.dot(joined, mixing_return_matrix, preferred_element_type=jnp.float32)
    return (upcast + mixed_out).astype(jnp.bfloat16)


def solution(mesh):
    return jax.shard_map(
        on_device,
        mesh=mesh,
        in_specs=(P("lat", None, "lon"), P(), P(), P(), P(), P(), P(), P(), P(), P(), P()),
        out_specs=P("lat", "lon", None),
        check_vma=False,
    )
```

profile of v0, /device:TPU:112, one launch (start us, length us, event | category | flops | bytes accessed | tf_op | source)
XLA Modules:
  0.0 122.5 jit_solution(3448078387444277257)
XLA Ops:
  0.0 4.6 %copy.13 = bf16[32,96,256]{1,0,2:T(8,128)(2,1)} copy(bf16[32,96,256]{2,1,0:T(8,128)(2,1)} %param.11) | data formatting | bytes 3145728 | tf_op args[0]
  4.6 1.4 %fusion.98 = (bf16[4,96,256]{1,0,2:T(4,128)(2,1)S(1)}, bf16[4,96,256]{1,0,2:T(4,128)(2,1)S(1)}) fusion(bf16[32,96,256]{1,0,2:T(8,128)(2,1)} %copy.13), kind=kLoop, calls=%fused_computation.90 | loop fusion | bytes 786432 | tf_op jit(solution)/shard_map/slice | solution.py:14
  6.0 4.8 %collective-permute-start = (bf16[4,96,256]{1,0,2:T(4,128)(2,1)S(1)}, bf16[4,96,256]{1,0,2:T(4,128)(2,1)S(1)}, u32[]{:S(2)}, u32[]{:S(2)}) collective-permute-start(bf16[4,96,256]{1,0,2:T(4,128)(2,1)S(1)} %get-tuple-element.9), channel_id=1, source_target_pairs={{0,16},{16,32},{32,48},{48,64},{64,80},{80,96},{96,112},{112,128},... | collective-permute-start | bytes 589832 | tf_op jit(solution)/shard_map/ppermute | solution.py:14
  10.9 2.5 %collective-permute-start.1 = (bf16[4,96,256]{1,0,2:T(4,128)(2,1)S(1)}, bf16[4,96,256]{1,0,2:T(4,128)(2,1)S(1)}, u32[]{:S(2)}, u32[]{:S(2)}) collective-permute-start(bf16[4,96,256]{1,0,2:T(4,128)(2,1)S(1)} %get-tuple-element.10), channel_id=1, source_target_pairs={{16,0},{32,16},{48,32},{64,48},{80,64},{96,80},{112,96},{128,112},... | collective-permute-start | bytes 589832 | tf_op jit(solution)/shard_map/ppermute | solution.py:15
  13.5 4.0 %collective-permute-done = bf16[4,96,256]{1,0,2:T(4,128)(2,1)S(1)} collective-permute-done((bf16[4,96,256]{1,0,2:T(4,128)(2,1)S(1)}, bf16[4,96,256]{1,0,2:T(4,128)(2,1)S(1)}, u32[]{:S(2)}, u32[]{:S(2)}) %collective-permute-start) | collective-permute-done | bytes 196640 | tf_op jit(solution)/shard_map/ppermute | solution.py:14
  17.5 6.6 %collective-permute-done.1 = bf16[4,96,256]{1,0,2:T(4,128)(2,1)S(1)} collective-permute-done((bf16[4,96,256]{1,0,2:T(4,128)(2,1)S(1)}, bf16[4,96,256]{1,0,2:T(4,128)(2,1)S(1)}, u32[]{:S(2)}, u32[]{:S(2)}) %collective-permute-start.1) | collective-permute-done | bytes 196640 | tf_op jit(solution)/shard_map/ppermute | solution.py:15
  24.1 0.8 pad_maximum_fusion.3
  25.0 3.8 %collective-permute-start.3 = (bf16[40,96,4]{1,0,2:T(8,128)(2,1)S(1)}, bf16[40,96,4]{1,0,2:T(8,128)(2,1)S(1)}, u32[]{:S(2)}, u32[]{:S(2)}) collective-permute-start(bf16[40,96,4]{1,0,2:T(8,128)(2,1)S(1)} %get-tuple-element.8), channel_id=1, source_target_pairs={{1,0},{2,1},{3,2},{4,3},{5,4},{6,5},{7,6},{8,7},{9,8},{10,9},{11,1... | collective-permute-start | bytes 92168 | tf_op jit(solution)/shard_map/ppermute | solution.py:26
  28.9 1.7 %collective-permute-done.2 = bf16[40,96,4]{1,0,2:T(8,128)(2,1)S(1)} collective-permute-done((bf16[40,96,4]{1,0,2:T(8,128)(2,1)S(1)}, bf16[40,96,4]{1,0,2:T(8,128)(2,1)S(1)}, u32[]{:S(2)}, u32[]{:S(2)}) %collective-permute-start.2) | collective-permute-done | bytes 30752 | tf_op jit(solution)/shard_map/ppermute | solution.py:25
  30.6 3.5 %pad_maximum_fusion = bf16[40,96,264]{1,0,2:T(8,128)(2,1)S(1)} fusion(bf16[40,96,4]{1,0,2:T(8,128)(2,1)S(1)} %collective-permute-done.3, bf16[4,96,256]{1,0,2:T(4,128)(2,1)S(1)} %collective-permute-done.1, bf16[32,96,256]{1,0,2:T(8,128)(2,1)S(1)} %copy-done.1, bf16[4,96,256]{1,0,2:T(4,128)(2,1)S(1)} %collective-permute-done, ...), kind=kLoop, calls=%fused_computation.23 | loop fusion | flops 10137600 | bytes 4055040 | tf_op jit(solution)/shard_map/concatenate | solution.py:27
  34.1 0.4 copy.17
  34.5 0.5 copy-done.8
  35.0 6.2 %select_select_fusion = bf16[38,8,33,128]{3,1,2,0:T(8,128)(2,1)S(1)} fusion(f32[128]{0:T(128)S(1)} %copy-done.10, pred[38]{0:T(512)(128)(4,1)S(1)} %compare_and_fusion, pred[8,33]{0,1:T(8,128)(4,1)S(1)} %copy-done.11, bf16[3,3,96,128]{3,2,1,0:T(8,128)(2,1)S(1)} %copy-done.8, bf16[40,96,1,7,2]{1,3,4,0,2:T(8,128)(2,1)S(1)} %slice.49, ...), kind=kOutput, calls=%fused_computation.24 | convolution fusion | flops 2236925952 | bytes 4925230 | tf_op jit(solution)/shard_map/conv_general_dilated | solution.py:39
  41.2 0.4 copy.18
  41.6 0.5 pad.1
  42.1 0.7 copy.20
  42.8 0.5 copy-done.7
  43.3 2.9 %fusion.8 = f32[18,8,17,256]{3,1,2,0:T(8,128)S(1)} fusion(bf16[4,4,128,256]{3,2,1,0:T(8,128)(2,1)S(1)} %copy-done.7, bf16[38,1,7,3,128]{4,2,3,0,1:T(8,128)(2,1)S(1)} %slice.50, bf16[38,1,8,34,128]{4,2,3,0,1:T(8,128)(2,1)S(1)} %copy.20), kind=kOutput, calls=%fused_computation.13 | convolution fusion | flops 2575552512 | bytes 6405632 | tf_op jit(solution)/shard_map/conv_general_dilated | solution.py:51
  46.2 2.7 %copy.21 = f32[18,8,17,256]{3,2,1,0:T(8,128)} copy(f32[18,8,17,256]{3,1,2,0:T(8,128)S(1)} %fusion.8) | data formatting | bytes 5013504 | tf_op jit(solution)/shard_map/conv_general_dilated | solution.py:51
  48.9 4.2 %reshape.76 = f32[18,1,136,256]{3,2,0,1:T(8,128)} reshape(f32[18,8,17,256]{3,2,1,0:T(8,128)} %copy.21) | data formatting | bytes 5013504 | tf_op jit(solution)/shard_map/conv_general_dilated | solution.py:51
  53.1 2.5 %fusion.38 = bf16[18,130,256]{2,1,0:T(8,128)(2,1)S(1)} fusion(f32[256]{0:T(256)S(1)} %copy-done.4, f32[18,1,136,256]{3,2,0,1:T(8,128)} %reshape.76, pred[18]{0:T(512)(128)(4,1)S(1)} %compare_and_fusion.1), kind=kLoop, calls=%fused_computation.38 | loop fusion | flops 4193280 | bytes 3595282 | tf_op jit(solution)/shard_map/jit(_where)/select_n | solution.py:35
  55.6 0.1 pad.3
  55.7 1.4 %reshape.79 = bf16[18,1,8,18,256]{4,3,2,0,1:T(8,128)(2,1)} reshape(bf16[18,1,144,256]{3,2,0,1:T(8,128)(2,1)S(1)} %pad.3) | data formatting | bytes 2654208 | tf_op jit(solution)/shard_map/conv_general_dilated | solution.py:51
  57.2 1.8 %copy.23 = bf16[18,1,8,18,256]{4,2,3,0,1:T(8,128)(2,1)S(1)} copy(bf16[18,1,8,18,256]{4,3,2,0,1:T(8,128)(2,1)} %reshape.79) | data formatting | bytes 2654208 | tf_op jit(solution)/shard_map/conv_general_dilated | solution.py:51
  59.0 1.4 %fusion.39 = f32[8,8,9,256]{3,1,2,0:T(8,128)S(1)} fusion(bf16[4,4,256,256]{3,2,1,0:T(8,128)(2,1)S(1)} %copy-done, bf16[18,1,7,3,256]{4,2,3,0,1:T(8,128)(2,1)S(1)} %slice.52, bf16[18,1,8,18,256]{4,2,3,0,1:T(8,128)(2,1)S(1)} %copy.23, pred[8,9]{0,1:T(8,128)(4,1)S(1)} %copy-done.12), kind=kOutput, calls=%fused_computation.40 | convolution fusion | flops 1212751872 | bytes 4207688 | tf_op jit(solution)/shard_map/conv_general_dilated | solution.py:51
  60.5 0.2 copy.24
  60.7 0.3 convert_reduce_fusion
  61.0 0.3 fusion.77
  61.3 0.1 copy-done.2
  61.4 1.3 %fusion.100 = (bf16[8,64,768]{2,1,0:T(8,128)(2,1)}, f32[8,64,768]{2,1,0:T(8,128)S(1)}) fusion(bf16[256,768]{1,0:T(8,128)(2,1)S(1)} %copy-done.2, bf16[8,64,256]{2,1,0:T(8,128)(2,1)S(1)} %get-tuple-element.6, f32[256]{0:T(256)S(1)} %copy-done.6, f32[8,64]{1,0:T(8,128)S(1)} %add_rsqrt_fusion, f32[8,64]{1,0:T(8,128)S(1)} %broadcast_multiply_fusion), kind=kOutput, calls=%fused_computation.92 | convolution fusion | flops 202375168 | bytes 3019776 | tf_op jit(solution)/shard_map/dot_general | solution.py:95
  62.8 0.8 slice.54
  63.6 1.4 %copy.26 = f32[8,64,256]{1,2,0:T(8,128)S(1)} copy(f32[8,64,256]{2,1,0:T(8,128)} %slice.54) | data formatting | bytes 1048576 | tf_op jit(solution)/shard_map/slice | solution.py:98
  65.0 1.9 %fusion.99 = (bf16[8,64,256]{2,1,0:T(8,128)(2,1)}, bf16[8,64,256]{2,1,0:T(8,128)(2,1)}) fusion(bf16[8,64,768]{2,1,0:T(8,128)(2,1)} %get-tuple-element.13), kind=kLoop, calls=%fused_computation.91 | loop fusion | bytes 1048576 | tf_op jit(solution)/shard_map/slice | solution.py:99
  66.9 2.0 %copy.27 = bf16[8,64,256]{1,2,0:T(8,128)(2,1)} copy(bf16[8,64,256]{2,1,0:T(8,128)(2,1)} %get-tuple-element.11) | data formatting | bytes 524288 | tf_op jit(solution)/shard_map/slice | solution.py:99
  68.8 2.0 %copy.28 = bf16[8,64,256]{1,2,0:T(8,128)(2,1)} copy(bf16[8,64,256]{2,1,0:T(8,128)(2,1)} %get-tuple-element.12) | data formatting | bytes 524288 | tf_op jit(solution)/shard_map/slice | solution.py:100
  70.8 0.2 multiply_convert_fusion.2
  71.0 2.7 %maximum_bitcast_fusion = bf16[8,8,64,96]{2,3,1,0:T(8,128)(2,1)} fusion(bf16[8,64,8,32]{1,3,2,0:T(8,128)(2,1)} %bitcast.84, bf16[8,64,8,32]{1,3,2,0:T(8,128)(2,1)} %bitcast.83, bf16[8,64,8,32]{1,3,2,0:T(8,128)(2,1)S(1)} %multiply_convert_fusion.2), kind=kLoop, calls=%fused_computation.29 | loop fusion | flops 2359296 | bytes 1572864 | tf_op jit(solution)/shard_map/transpose | solution.py:106
  73.6 1.8 %copy.29 = bf16[8,8,64,96]{3,2,1,0:T(8,128)(2,1)S(1)} copy(bf16[8,8,64,96]{2,3,1,0:T(8,128)(2,1)} %maximum_bitcast_fusion) | data formatting | bytes 1572864 | tf_op jit(solution)/shard_map/transpose | solution.py:106
  75.5 22.2 %all_to_all.10 = bf16[16,4,64,96]{3,2,1,0:T(8,128)(2,1)S(1)} all-to-all(bf16[16,4,64,96]{3,2,1,0:T(8,128)(2,1)S(1)} %bitcast.78), channel_id=1, replica_groups=mesh['lat'=16,'lon'=16] {'lon'}, dimensions={0} | all-to-all | bytes 1572864 | tf_op jit(solution)/shard_map/all_to_all | solution.py:107
  97.7 0.1 copy.30
  97.7 4.6 %fusion.101 = f32[4,1024]{1,0:T(4,128)S(1)} fusion(bf16[4,1024,96]{2,1,0:T(8,128)(2,1)S(1)} %bitcast.85), kind=kOutput, calls=%fused_computation.93 | convolution fusion | flops 276825088 | bytes 2113536 | tf_op jit(solution)/shard_map/sub | solution.py:114
  102.4 6.4 %fusion.51 = bf16[4,1024,32]{1,2,0:T(8,128)(2,1)} fusion(bf16[4,1024,96]{2,1,0:T(8,128)(2,1)S(1)} %bitcast.86, f32[4,1024]{1,0:T(4,128)S(1)} %fusion.101), kind=kOutput, calls=%fused_computation.45 | convolution fusion | flops 545526784 | bytes 3424256 | tf_op jit(solution)/shard_map/ist,itd->isd/dot_general | solution.py:116
  108.8 1.4 %reshape.60 = bf16[4,16,64,32]{2,1,3,0:T(8,128)(2,1)S(1)} reshape(bf16[4,1024,32]{1,2,0:T(8,128)(2,1)} %fusion.51) | data formatting | bytes 524288 | tf_op jit(solution)/shard_map/reshape | solution.py:120
  110.2 0.1 copy.52
  110.3 0.4 reshape.104
  110.7 10.4 %all_to_all.11 = bf16[16,2,4096]{2,1,0:T(2,128)(2,1)S(1)} all-to-all(bf16[16,2,4096]{2,1,0:T(2,128)(2,1)S(1)} %reshape.104), channel_id=1, replica_groups=mesh['lat'=16,'lon'=16] {'lon'}, dimensions={0} | all-to-all | bytes 524288 | tf_op jit(solution)/shard_map/all_to_all | solution.py:122
  121.2 0.3 reshape.105
  121.5 1.0 fusion.42
  (34 shorter events, 0.4 us)
Async XLA Ops:
  0.0 59.0 %copy-start = (bf16[4,4,256,256]{3,2,1,0:T(8,128)(2,1)S(1)}, bf16[4,4,256,256]{3,2,1,0:T(8,128)(2,1)}, u32[]{:S(2)}) copy-start(bf16[4,4,256,256]{3,2,1,0:T(8,128)(2,1)} %param.16) | copy-start | bytes 6291460
  0.0 13.4 %copy-start.9 = (f32[8]{0:T(128)S(1)}, f32[8]{0:T(128)}, u32[]{:S(2)}) copy-start(f32[8]{0:T(128)} %param.20) | copy-start | bytes 100
  6.0 11.4 %collective-permute-start = (bf16[4,96,256]{1,0,2:T(4,128)(2,1)S(1)}, bf16[4,96,256]{1,0,2:T(4,128)(2,1)S(1)}, u32[]{:S(2)}, u32[]{:S(2)}) collective-permute-start(bf16[4,96,256]{1,0,2:T(4,128)(2,1)S(1)} %get-tuple-element.9), channel_id=1, source_target_pairs={{0,16},{16,32},{32,48},{48,64},{64,80},{80,96},{96,112},{112,128},... | collective-permute-start | bytes 589832 | tf_op jit(solution)/shard_map/ppermute | solution.py:14
  10.9 13.3 %collective-permute-start.1 = (bf16[4,96,256]{1,0,2:T(4,128)(2,1)S(1)}, bf16[4,96,256]{1,0,2:T(4,128)(2,1)S(1)}, u32[]{:S(2)}, u32[]{:S(2)}) collective-permute-start(bf16[4,96,256]{1,0,2:T(4,128)(2,1)S(1)} %get-tuple-element.10), channel_id=1, source_target_pairs={{16,0},{32,16},{48,32},{64,48},{80,64},{96,80},{112,96},{128,112},... | collective-permute-start | bytes 589832 | tf_op jit(solution)/shard_map/ppermute | solution.py:15
  13.4 17.1 %copy-start.1 = (bf16[32,96,256]{1,0,2:T(8,128)(2,1)S(1)}, bf16[32,96,256]{1,0,2:T(8,128)(2,1)}, u32[]{:S(2)}) copy-start(bf16[32,96,256]{1,0,2:T(8,128)(2,1)} %copy.13) | copy-start | bytes 4718596
  24.9 5.6 %collective-permute-start.2 = (bf16[40,96,4]{1,0,2:T(8,128)(2,1)S(1)}, bf16[40,96,4]{1,0,2:T(8,128)(2,1)S(1)}, u32[]{:S(2)}, u32[]{:S(2)}) collective-permute-start(bf16[40,96,4]{1,0,2:T(8,128)(2,1)S(1)} %get-tuple-element.7), channel_id=1, source_target_pairs={{0,1},{1,2},{2,3},{3,4},{4,5},{5,6},{6,7},{7,8},{8,9},{9,10},{10,1... | collective-permute-start | bytes 92168 | tf_op jit(solution)/shard_map/ppermute | solution.py:25
  25.0 5.5 %collective-permute-start.3 = (bf16[40,96,4]{1,0,2:T(8,128)(2,1)S(1)}, bf16[40,96,4]{1,0,2:T(8,128)(2,1)S(1)}, u32[]{:S(2)}, u32[]{:S(2)}) collective-permute-start(bf16[40,96,4]{1,0,2:T(8,128)(2,1)S(1)} %get-tuple-element.8), channel_id=1, source_target_pairs={{1,0},{2,1},{3,2},{4,3},{5,4},{6,5},{7,6},{8,7},{9,8},{10,9},{11,1... | collective-permute-start | bytes 92168 | tf_op jit(solution)/shard_map/ppermute | solution.py:26
  34.1 0.9 copy-start.8
  34.1 0.9 copy-start.10
  34.1 0.9 copy-start.11
  42.1 1.2 %copy-start.7 = (bf16[4,4,128,256]{3,2,1,0:T(8,128)(2,1)S(1)}, bf16[4,4,128,256]{3,2,1,0:T(8,128)(2,1)}, u32[]{:S(2)}) copy-start(bf16[4,4,128,256]{3,2,1,0:T(8,128)(2,1)} %param.14) | copy-start | bytes 3145732
  48.9 4.2 %copy-start.4 = (f32[256]{0:T(256)S(1)}, f32[256]{0:T(256)}, u32[]{:S(2)}) copy-start(f32[256]{0:T(256)} %param.15) | copy-start | bytes 3076
  55.7 3.3 %copy-start.12 = (pred[8,9]{0,1:T(8,128)(4,1)S(1)}, pred[8,9]{0,1:T(8,128)(4,1)}, u32[]{:S(2)}) copy-start(pred[8,9]{0,1:T(8,128)(4,1)} %constant.67) | copy-start | bytes 220
  59.0 1.7 %copy-start.5 = (f32[256]{0:T(256)S(1)}, f32[256]{0:T(256)}, u32[]{:S(2)}) copy-start(f32[256]{0:T(256)} %param.17) | copy-start | bytes 3076
  60.4 1.0 copy-start.2
  60.4 1.0 copy-start.6
  108.8 12.7 %copy-start.3 = (bf16[256,256]{1,0:T(8,128)(2,1)S(1)}, bf16[256,256]{1,0:T(8,128)(2,1)}, u32[]{:S(2)}) copy-start(bf16[256,256]{1,0:T(8,128)(2,1)} %param.21) | copy-start | bytes 393220
where the time goes:
time: 124 us; the launch traced here: 123 us
  blocking collectives  32.6 us (26%)
  local copies, waits for them, and re-layouts  31.8 us (26%)
  matrix products  23.9 us (19%)
  waiting for transfers between devices  12.3 us (10%)
  starting transfers between devices  11.3 us (9%)
  other arithmetic  10.2 us (8%)
    all_to_all x1, blocking collectives, on_device(): trio = lax.all_to_all(trio, 'lon', 0, 0, tiled=True)  22.2 us
    all_to_all x1, blocking collectives, on_device(): attended = lax.all_to_all(attended, 'lon', 0, 0, tiled=True)  10.4 us
    conv_general_dilated x7, local copies, waits for them, and re-layouts, halving_filter(): lax.conv_general_dilated(extended[None], kernel, (2, 2), 'VALID', dimensi...  10.4 us
    ppermute x1, waiting for transfers between devices, extend_lat(): after = lax.ppermute(value[:width], 'lat', down)  6.65 us
    unnamed x29, local copies, waits for them, and re-layouts  6.49 us
    dot_general x1, matrix products, on_device(): jnp.einsum('ist,itd->isd', weights.astype(jnp.bfloat16), v_items, preferr...  6.41 us
    conv_general_dilated x1, matrix products, first_conv(): lax.conv_general_dilated(extended[None], kernel, (1, 1), 'VALID', dimensi...  6.18 us
    ppermute x1, starting transfers between devices, extend_lat(): before = lax.ppermute(value[length - width:], 'lat', up)  4.81 us
  transfers between devices with their start and end apart: 4, of which 3 were waited for; matrix products, arithmetic and copies ran while one was open for 0% of the time, Pallas kernels for 0%

commit v1 on v0

--- a/solution.py
+++ b/solution.py
@@ -92,23 +92,24 @@
     centred = upcast - mean
     variance = jnp.mean(centred * centred, axis=-1, keepdims=True)
     normed = (centred * lax.rsqrt(variance + 1e-05) * layernorm_multiplier).astype(jnp.bfloat16)
-    projected = jnp.dot(normed, triple_mapping_matrix, preferred_element_type=jnp.float32)
-    shape = (rows, tokens, HEADS, per_group_channel_count)
-    logit_multiplier = (logit_sharpness / jnp.sqrt(jnp.float32(per_group_channel_count)))[:, None]
-    query = (projected[..., :widths].reshape(shape) * logit_multiplier).astype(jnp.bfloat16)
-    key = projected[..., widths : 2 * widths].reshape(shape).astype(jnp.bfloat16)
-    value = projected[..., 2 * widths :].reshape(shape).astype(jnp.bfloat16)
+    d = widths // HEADS
+    logit_multiplier = logit_sharpness / jnp.sqrt(jnp.float32(d))
 
     sectors = lax.axis_size("lon")
-    items = rows * HEADS
-    per_device = items // sectors
-    trio = jnp.concatenate([query, key, value], axis=-1)
-    trio = jnp.transpose(trio, (0, 2, 1, 3)).reshape(sectors, per_device, tokens, 3 * per_group_channel_count)
-    trio = lax.all_to_all(trio, "lon", 0, 0, tiled=True)
-    trio = jnp.transpose(trio, (1, 0, 2, 3)).reshape(per_device, sectors * tokens, 3 * per_group_channel_count)
-    q_items = trio[..., :per_group_channel_count]
-    k_items = trio[..., per_group_channel_count : 2 * per_group_channel_count]
-    v_items = trio[..., 2 * per_group_channel_count :]
+    per_row = sectors // rows
+    heads_here = HEADS // per_row
+    half = lax.axis_index("lon") % per_row
+    row_copies = jnp.repeat(normed, per_row, axis=0)
+    gathered = lax.all_to_all(row_copies, "lon", 0, 0, tiled=True)
+    row_tokens = gathered.reshape(sectors * tokens, widths)
+    mapping = triple_mapping_matrix.reshape(widths, 3, HEADS, d)
+    mapping = lax.dynamic_slice_in_dim(mapping, half * heads_here, heads_here, axis=2)
+    projected = jnp.einsum("tc,cjhd->jhtd", row_tokens, mapping, preferred_element_type=jnp.float32)
+    multiplier = lax.dynamic_slice_in_dim(logit_multiplier, half * heads_here, heads_here)
+    q_items = (projected[0] * multiplier[:, None, None]).astype(jnp.bfloat16)
+    k_items = projected[1].astype(jnp.bfloat16)
+    v_items = projected[2].astype(jnp.bfloat16)
+    per_device = heads_here
     scores = jnp.einsum("isd,itd->ist", q_items, k_items, preferred_element_type=jnp.float32)
     best = jnp.max(scores, axis=-1, keepdims=True)
     weights = jnp.exp(scores - best)

time: 124 us -> 107 us (0.86)
  blocking collectives: 32.6 us -> 10.4 us
  waiting for transfers between devices: 12.3 us -> 21.9 us
  local copies, waits for them, and re-layouts: 31.8 us -> 22.9 us
  starting transfers between devices: 11.3 us -> 17.2 us
  other arithmetic: 10.2 us -> 7.65 us
    all_to_all x1 -> x0, blocking collectives: 22.2 us -> none  [on_device(): trio = lax.all_to_all(trio, 'lon', 0, 0, tiled=True)]
    all_to_all x0 -> x1, waiting for transfers between devices: none -> 9.54 us  [on_device(): gathered = lax.all_to_all(row_copies, 'lon', 0, 0, tiled=True)]
    slice x5 -> x0, local copies, waits for them, and re-layouts: 7.99 us -> none  [the longest x2 3.82 us: on_device(): key = projected[..., widths:2 * widths].reshape(shape).astype(jnp.bfloat16)]
    all_to_all x0 -> x1, starting transfers between devices: none -> 5.95 us  [on_device(): gathered = lax.all_to_all(row_copies, 'lon', 0, 0, tiled=True)]
    transpose x1 -> x0, other arithmetic: 2.69 us -> none  [on_device(): jnp.transpose(trio, (0, 2, 1, 3))]
    transpose x2 -> x0, local copies, waits for them, and re-layouts: 1.88 us -> none  [the longest x1 1.8 us: on_device(): jnp.transpose(trio, (0, 2, 1, 3))]
    unnamed x29 -> x28, local copies, waits for them, and re-layouts: 6.49 us -> 7.51 us
  transfers between devices with their start and end apart: 4 -> 5, of which waited for: 3 -> 4; matrix products, arithmetic and copies ran while one was open for 0% -> 1% of each run, Pallas kernels for 0% -> 0%
where the time goes in v1:
time: 107 us; the launch traced here: 105 us
  matrix products  24.9 us (23%)
  local copies, waits for them, and re-layouts  22.9 us (21%)
  waiting for transfers between devices  21.9 us (20%)
  starting transfers between devices  17.2 us (16%)
  blocking collectives  10.4 us (10%)
  other arithmetic  7.65 us (7%)
    all_to_all x1, blocking collectives, on_device(): attended = lax.all_to_all(attended, 'lon', 0, 0, tiled=True)  10.4 us
    conv_general_dilated x7, local copies, waits for them, and re-layouts, halving_filter(): lax.conv_general_dilated(extended[None], kernel, (2, 2), 'VALID', dimensi...  10.4 us
    all_to_all x1, waiting for transfers between devices, on_device(): gathered = lax.all_to_all(row_copies, 'lon', 0, 0, tiled=True)  9.54 us
    unnamed x28, local copies, waits for them, and re-layouts  7.51 us
    ppermute x1, waiting for transfers between devices, extend_lat(): after = lax.ppermute(value[:width], 'lat', down)  6.65 us
    dot_general x1, matrix products, on_device(): jnp.einsum('ist,itd->isd', weights.astype(jnp.bfloat16), v_items, preferr...  6.59 us
    conv_general_dilated x1, matrix products, first_conv(): lax.conv_general_dilated(extended[None], kernel, (1, 1), 'VALID', dimensi...  6.18 us
    all_to_all x1, starting transfers between devices, on_device(): gathered = lax.all_to_all(row_copies, 'lon', 0, 0, tiled=True)  5.95 us
  transfers between devices with their start and end apart: 5, of which 4 were waited for; matrix products, arithmetic and copies ran while one was open for 1% of the time, Pallas kernels for 0%

profile of v1, /device:TPU:112, one launch (start us, length us, event | category | flops | bytes accessed | tf_op | source)
XLA Modules:
  0.0 105.4 jit_solution(811022146684691199)
XLA Ops:
  0.0 4.6 %copy.14 = bf16[32,96,256]{1,0,2:T(8,128)(2,1)} copy(bf16[32,96,256]{2,1,0:T(8,128)(2,1)} %param.11) | data formatting | bytes 3145728 | tf_op args[0]
  4.6 1.4 %fusion.77 = (bf16[4,96,256]{1,0,2:T(4,128)(2,1)S(1)}, bf16[4,96,256]{1,0,2:T(4,128)(2,1)S(1)}) fusion(bf16[32,96,256]{1,0,2:T(8,128)(2,1)} %copy.14), kind=kLoop, calls=%fused_computation.84 | loop fusion | bytes 786432 | tf_op jit(solution)/shard_map/slice | solution.py:14
  6.0 4.8 %collective-permute-start = (bf16[4,96,256]{1,0,2:T(4,128)(2,1)S(1)}, bf16[4,96,256]{1,0,2:T(4,128)(2,1)S(1)}, u32[]{:S(2)}, u32[]{:S(2)}) collective-permute-start(bf16[4,96,256]{1,0,2:T(4,128)(2,1)S(1)} %get-tuple-element.9), channel_id=1, source_target_pairs={{0,16},{16,32},{32,48},{48,64},{64,80},{80,96},{96,112},{112,128},... | collective-permute-start | bytes 589832 | tf_op jit(solution)/shard_map/ppermute | solution.py:14
  10.8 2.5 %collective-permute-start.1 = (bf16[4,96,256]{1,0,2:T(4,128)(2,1)S(1)}, bf16[4,96,256]{1,0,2:T(4,128)(2,1)S(1)}, u32[]{:S(2)}, u32[]{:S(2)}) collective-permute-start(bf16[4,96,256]{1,0,2:T(4,128)(2,1)S(1)} %get-tuple-element.10), channel_id=1, source_target_pairs={{16,0},{32,16},{48,32},{64,48},{80,64},{96,80},{112,96},{128,112},... | collective-permute-start | bytes 589832 | tf_op jit(solution)/shard_map/ppermute | solution.py:15
  13.4 4.0 %collective-permute-done = bf16[4,96,256]{1,0,2:T(4,128)(2,1)S(1)} collective-permute-done((bf16[4,96,256]{1,0,2:T(4,128)(2,1)S(1)}, bf16[4,96,256]{1,0,2:T(4,128)(2,1)S(1)}, u32[]{:S(2)}, u32[]{:S(2)}) %collective-permute-start) | collective-permute-done | bytes 196640 | tf_op jit(solution)/shard_map/ppermute | solution.py:14
  17.5 6.6 %collective-permute-done.1 = bf16[4,96,256]{1,0,2:T(4,128)(2,1)S(1)} collective-permute-done((bf16[4,96,256]{1,0,2:T(4,128)(2,1)S(1)}, bf16[4,96,256]{1,0,2:T(4,128)(2,1)S(1)}, u32[]{:S(2)}, u32[]{:S(2)}) %collective-permute-start.1) | collective-permute-done | bytes 196640 | tf_op jit(solution)/shard_map/ppermute | solution.py:15
  24.1 0.8 pad_maximum_fusion.3
  24.9 0.1 collective-permute-start.2
  25.0 3.8 %collective-permute-start.3 = (bf16[40,96,4]{1,0,2:T(8,128)(2,1)S(1)}, bf16[40,96,4]{1,0,2:T(8,128)(2,1)S(1)}, u32[]{:S(2)}, u32[]{:S(2)}) collective-permute-start(bf16[40,96,4]{1,0,2:T(8,128)(2,1)S(1)} %get-tuple-element.8), channel_id=1, source_target_pairs={{1,0},{2,1},{3,2},{4,3},{5,4},{6,5},{7,6},{8,7},{9,8},{10,9},{11,1... | collective-permute-start | bytes 92168 | tf_op jit(solution)/shard_map/ppermute | solution.py:26
  28.9 1.7 %collective-permute-done.2 = bf16[40,96,4]{1,0,2:T(8,128)(2,1)S(1)} collective-permute-done((bf16[40,96,4]{1,0,2:T(8,128)(2,1)S(1)}, bf16[40,96,4]{1,0,2:T(8,128)(2,1)S(1)}, u32[]{:S(2)}, u32[]{:S(2)}) %collective-permute-start.2) | collective-permute-done | bytes 30752 | tf_op jit(solution)/shard_map/ppermute | solution.py:25
  30.6 3.5 %pad_maximum_fusion = bf16[40,96,264]{1,0,2:T(8,128)(2,1)S(1)} fusion(bf16[40,96,4]{1,0,2:T(8,128)(2,1)S(1)} %collective-permute-done.3, bf16[4,96,256]{1,0,2:T(4,128)(2,1)S(1)} %collective-permute-done.1, bf16[32,96,256]{1,0,2:T(8,128)(2,1)S(1)} %copy-done.1, bf16[4,96,256]{1,0,2:T(4,128)(2,1)S(1)} %collective-permute-done, ...), kind=kLoop, calls=%fused_computation.23 | loop fusion | flops 10137600 | bytes 4055040 | tf_op jit(solution)/shard_map/concatenate | solution.py:27
  34.1 0.0 copy-start.10
  34.1 0.4 copy.18
  34.5 0.5 copy-done.7
  35.0 6.2 %select_select_fusion = bf16[38,8,33,128]{3,1,2,0:T(8,128)(2,1)S(1)} fusion(f32[128]{0:T(128)S(1)} %copy-done.8, pred[38]{0:T(512)(128)(4,1)S(1)} %compare_and_fusion, pred[8,33]{0,1:T(8,128)(4,1)S(1)} %copy-done.10, bf16[3,3,96,128]{3,2,1,0:T(8,128)(2,1)S(1)} %copy-done.7, bf16[40,96,1,7,2]{1,3,4,0,2:T(8,128)(2,1)S(1)} %slice.37, ...), kind=kOutput, calls=%fused_computation.24 | convolution fusion | flops 2236925952 | bytes 4925230 | tf_op jit(solution)/shard_map/conv_general_dilated | solution.py:39
  41.2 0.4 copy.19
  41.6 0.5 pad.1
  42.1 0.7 copy.21
  42.8 0.1 slice.38
  42.8 0.5 copy-done.6
  43.3 2.9 %fusion.8 = f32[18,8,17,256]{3,1,2,0:T(8,128)S(1)} fusion(bf16[4,4,128,256]{3,2,1,0:T(8,128)(2,1)S(1)} %copy-done.6, bf16[38,1,7,3,128]{4,2,3,0,1:T(8,128)(2,1)S(1)} %slice.38, bf16[38,1,8,34,128]{4,2,3,0,1:T(8,128)(2,1)S(1)} %copy.21), kind=kOutput, calls=%fused_computation.13 | convolution fusion | flops 2575552512 | bytes 6405632 | tf_op jit(solution)/shard_map/conv_general_dilated | solution.py:51
  46.2 2.7 %copy.22 = f32[18,8,17,256]{3,2,1,0:T(8,128)} copy(f32[18,8,17,256]{3,1,2,0:T(8,128)S(1)} %fusion.8) | data formatting | bytes 5013504 | tf_op jit(solution)/shard_map/conv_general_dilated | solution.py:51
  48.9 4.2 %reshape.74 = f32[18,1,136,256]{3,2,0,1:T(8,128)} reshape(f32[18,8,17,256]{3,2,1,0:T(8,128)} %copy.22) | data formatting | bytes 5013504 | tf_op jit(solution)/shard_map/conv_general_dilated | solution.py:51
  53.1 2.5 %fusion.38 = bf16[18,130,256]{2,1,0:T(8,128)(2,1)S(1)} fusion(f32[256]{0:T(256)S(1)} %copy-done.3, f32[18,1,136,256]{3,2,0,1:T(8,128)} %reshape.74, pred[18]{0:T(512)(128)(4,1)S(1)} %compare_and_fusion.1), kind=kLoop, calls=%fused_computation.38 | loop fusion | flops 4193280 | bytes 3595282 | tf_op jit(solution)/shard_map/jit(_where)/select_n | solution.py:35
  55.6 0.1 pad.3
  55.7 1.4 %reshape.77 = bf16[18,1,8,18,256]{4,3,2,0,1:T(8,128)(2,1)} reshape(bf16[18,1,144,256]{3,2,0,1:T(8,128)(2,1)S(1)} %pad.3) | data formatting | bytes 2654208 | tf_op jit(solution)/shard_map/conv_general_dilated | solution.py:51
  57.2 1.8 %copy.24 = bf16[18,1,8,18,256]{4,2,3,0,1:T(8,128)(2,1)S(1)} copy(bf16[18,1,8,18,256]{4,3,2,0,1:T(8,128)(2,1)} %reshape.77) | data formatting | bytes 2654208 | tf_op jit(solution)/shard_map/conv_general_dilated | solution.py:51
  58.9 0.1 slice.40
  59.0 1.4 %fusion.39 = f32[8,8,9,256]{3,1,2,0:T(8,128)S(1)} fusion(bf16[4,4,256,256]{3,2,1,0:T(8,128)(2,1)S(1)} %copy-done, bf16[18,1,7,3,256]{4,2,3,0,1:T(8,128)(2,1)S(1)} %slice.40, bf16[18,1,8,18,256]{4,2,3,0,1:T(8,128)(2,1)S(1)} %copy.24, pred[8,9]{0,1:T(8,128)(4,1)S(1)} %copy-done.11), kind=kOutput, calls=%fused_computation.40 | convolution fusion | flops 1212751872 | bytes 4207688 | tf_op jit(solution)/shard_map/conv_general_dilated | solution.py:51
  60.4 0.2 copy.25
  60.7 0.3 convert_reduce_fusion
  61.0 0.3 fusion.56
  61.3 0.2 fusion.58
  61.5 0.8 broadcast_in_dim.47
  62.4 5.9 %all-to-all-start = ((bf16[16,64,256]{2,1,0:T(8,128)(2,1)}), bf16[16,64,256]{2,1,0:T(8,128)(2,1)S(1)}, u32[]{:S(2)}, u32[]{:S(2)}) async-start(bf16[16,64,256]{2,1,0:T(8,128)(2,1)} %bitcast.11), calls=%async_computation | async-start | bytes 1048576 | tf_op jit(solution)/shard_map/all_to_all | solution.py:103
  68.3 1.2 %copy.27 = bf16[256,768]{0,1:T(8,128)(2,1)S(1)} copy(bf16[256,768]{1,0:T(8,128)(2,1)} %param.19) | data formatting | bytes 786432 | tf_op args[8]
  69.5 0.1 dynamic_slice.7
  69.6 9.5 %all-to-all-done = bf16[16,64,256]{2,1,0:T(8,128)(2,1)S(1)} async-done(((bf16[16,64,256]{2,1,0:T(8,128)(2,1)}), bf16[16,64,256]{2,1,0:T(8,128)(2,1)S(1)}, u32[]{:S(2)}, u32[]{:S(2)}) %all-to-all-start) | async-done | bytes 524320 | tf_op jit(solution)/shard_map/all_to_all | solution.py:103
  79.1 1.3 %fusion.78 = (bf16[3,4,1024,32]{2,3,1,0:T(8,128)(2,1)}, f32[3,4,1024,32]{2,3,1,0:T(8,128)S(1)}) fusion(bf16[1024,256,1,1]{1,0,3,2:T(8,128)(2,1)S(1)} %bitcast.98, bf16[256,3,8,32]{0,3,2,1:T(8,128)(2,1)S(1)} %bitcast.101, s32[]{:T(128)S(6)} %select_n.28), kind=kOutput, calls=%fused_computation.85 | convolution fusion | flops 201719808 | bytes 3080196 | tf_op jit(solution)/shard_map/tc,cjhd->jhtd/dot_general | solution.py:107
  80.4 0.1 fusion.60
  80.5 5.5 %fusion.79 = f32[4,1024]{1,0:T(4,128)S(1)} fusion(bf16[4,1024,32]{1,2,0:T(8,128)(2,1)S(1)} %fusion.60, bf16[3,4,1024,32]{2,3,1,0:T(8,128)(2,1)} %get-tuple-element.11), kind=kOutput, calls=%fused_computation.86 | convolution fusion | flops 276825088 | bytes 540672 | tf_op jit(solution)/shard_map/sub | solution.py:115
  86.0 6.6 %fusion.48 = bf16[4,1024,32]{1,2,0:T(8,128)(2,1)S(1)} fusion(bf16[4,1024,32]{1,2,0:T(8,128)(2,1)S(1)} %fusion.60, bf16[3,4,1024,32]{2,3,1,0:T(8,128)(2,1)} %get-tuple-element.11, f32[4,1024]{1,0:T(4,128)S(1)} %fusion.79), kind=kOutput, calls=%fused_computation.43 | convolution fusion | flops 545526784 | bytes 1064960 | tf_op jit(solution)/shard_map/ist,itd->isd/dot_general | solution.py:117
  92.6 0.3 reshape.58
  93.0 0.1 copy.44
  93.1 0.4 reshape.102
  93.5 10.4 %all_to_all.10 = bf16[16,2,4096]{2,1,0:T(2,128)(2,1)S(1)} all-to-all(bf16[16,2,4096]{2,1,0:T(2,128)(2,1)S(1)} %reshape.102), channel_id=1, replica_groups=mesh['lat'=16,'lon'=16] {'lon'}, dimensions={0} | all-to-all | bytes 524288 | tf_op jit(solution)/shard_map/all_to_all | solution.py:123
  104.0 0.3 reshape.103
  104.3 1.0 fusion.42
  (29 shorter events, 0.2 us)
Async XLA Ops:
  0.0 59.0 %copy-start = (bf16[4,4,256,256]{3,2,1,0:T(8,128)(2,1)S(1)}, bf16[4,4,256,256]{3,2,1,0:T(8,128)(2,1)}, u32[]{:S(2)}) copy-start(bf16[4,4,256,256]{3,2,1,0:T(8,128)(2,1)} %param.16) | copy-start | bytes 6291460
  6.0 11.4 %collective-permute-start = (bf16[4,96,256]{1,0,2:T(4,128)(2,1)S(1)}, bf16[4,96,256]{1,0,2:T(4,128)(2,1)S(1)}, u32[]{:S(2)}, u32[]{:S(2)}) collective-permute-start(bf16[4,96,256]{1,0,2:T(4,128)(2,1)S(1)} %get-tuple-element.9), channel_id=1, source_target_pairs={{0,16},{16,32},{32,48},{48,64},{64,80},{80,96},{96,112},{112,128},... | collective-permute-start | bytes 589832 | tf_op jit(solution)/shard_map/ppermute | solution.py:14
  10.8 13.3 %collective-permute-start.1 = (bf16[4,96,256]{1,0,2:T(4,128)(2,1)S(1)}, bf16[4,96,256]{1,0,2:T(4,128)(2,1)S(1)}, u32[]{:S(2)}, u32[]{:S(2)}) collective-permute-start(bf16[4,96,256]{1,0,2:T(4,128)(2,1)S(1)} %get-tuple-element.10), channel_id=1, source_target_pairs={{16,0},{32,16},{48,32},{64,48},{80,64},{96,80},{112,96},{128,112},... | collective-permute-start | bytes 589832 | tf_op jit(solution)/shard_map/ppermute | solution.py:15
  13.4 17.1 %copy-start.1 = (bf16[32,96,256]{1,0,2:T(8,128)(2,1)S(1)}, bf16[32,96,256]{1,0,2:T(8,128)(2,1)}, u32[]{:S(2)}) copy-start(bf16[32,96,256]{1,0,2:T(8,128)(2,1)} %copy.14) | copy-start | bytes 4718596
  24.9 5.6 %collective-permute-start.2 = (bf16[40,96,4]{1,0,2:T(8,128)(2,1)S(1)}, bf16[40,96,4]{1,0,2:T(8,128)(2,1)S(1)}, u32[]{:S(2)}, u32[]{:S(2)}) collective-permute-start(bf16[40,96,4]{1,0,2:T(8,128)(2,1)S(1)} %get-tuple-element.7), channel_id=1, source_target_pairs={{0,1},{1,2},{2,3},{3,4},{4,5},{5,6},{6,7},{7,8},{8,9},{9,10},{10,1... | collective-permute-start | bytes 92168 | tf_op jit(solution)/shard_map/ppermute | solution.py:25
  25.0 5.5 %collective-permute-start.3 = (bf16[40,96,4]{1,0,2:T(8,128)(2,1)S(1)}, bf16[40,96,4]{1,0,2:T(8,128)(2,1)S(1)}, u32[]{:S(2)}, u32[]{:S(2)}) collective-permute-start(bf16[40,96,4]{1,0,2:T(8,128)(2,1)S(1)} %get-tuple-element.8), channel_id=1, source_target_pairs={{1,0},{2,1},{3,2},{4,3},{5,4},{6,5},{7,6},{8,7},{9,8},{10,9},{11,1... | collective-permute-start | bytes 92168 | tf_op jit(solution)/shard_map/ppermute | solution.py:26
  34.0 0.9 copy-start.7
  34.1 0.9 copy-start.8
  34.1 0.9 copy-start.10
  42.1 1.2 %copy-start.6 = (bf16[4,4,128,256]{3,2,1,0:T(8,128)(2,1)S(1)}, bf16[4,4,128,256]{3,2,1,0:T(8,128)(2,1)}, u32[]{:S(2)}) copy-start(bf16[4,4,128,256]{3,2,1,0:T(8,128)(2,1)} %param.14) | copy-start | bytes 3145732
  48.9 4.2 %copy-start.3 = (f32[256]{0:T(256)S(1)}, f32[256]{0:T(256)}, u32[]{:S(2)}) copy-start(f32[256]{0:T(256)} %param.15) | copy-start | bytes 3076
  55.7 3.3 %copy-start.11 = (pred[8,9]{0,1:T(8,128)(4,1)S(1)}, pred[8,9]{0,1:T(8,128)(4,1)}, u32[]{:S(2)}) copy-start(pred[8,9]{0,1:T(8,128)(4,1)} %constant.83) | copy-start | bytes 220
  59.0 1.7 %copy-start.4 = (f32[256]{0:T(256)S(1)}, f32[256]{0:T(256)}, u32[]{:S(2)}) copy-start(f32[256]{0:T(256)} %param.17) | copy-start | bytes 3076
  60.4 0.9 copy-start.5
  60.6 8.9 %copy-start.9 = (f32[8]{0:T(128)S(1)}, f32[8]{0:T(128)}, u32[]{:S(2)}) copy-start(f32[8]{0:T(128)} %param.20) | copy-start | bytes 100
  62.4 16.8 %all-to-all-start = ((bf16[16,64,256]{2,1,0:T(8,128)(2,1)}), bf16[16,64,256]{2,1,0:T(8,128)(2,1)S(1)}, u32[]{:S(2)}, u32[]{:S(2)}) async-start(bf16[16,64,256]{2,1,0:T(8,128)(2,1)} %bitcast.11), calls=%async_computation | async-start | bytes 1048576 | tf_op jit(solution)/shard_map/all_to_all | solution.py:103
  92.6 11.7 %copy-start.2 = (bf16[256,256]{1,0:T(8,128)(2,1)S(1)}, bf16[256,256]{1,0:T(8,128)(2,1)}, u32[]{:S(2)}) copy-start(bf16[256,256]{1,0:T(8,128)(2,1)} %param.21) | copy-start | bytes 393220

commit v2 on v1

--- a/solution.py
+++ b/solution.py
@@ -25,6 +25,37 @@
     before = lax.ppermute(last, "lon", up)
     after = lax.ppermute(initial, "lon", down)
     return jnp.concatenate([before, value, after], axis=dim)
+
+
+def extend_both(value, width):
+    n_lat, n_lon = lax.axis_size("lat"), lax.axis_size("lon")
+    h, w = value.shape[0], value.shape[2]
+
+    def shifted(piece, da, db):
+        pairs = []
+        for a in range(n_lat):
+            if 0 <= a + da < n_lat:
+                for b in range(n_lon):
+                    pairs.append((a * n_lon + b, (a + da) * n_lon + (b + db) % n_lon))
+        return lax.ppermute(piece, ("lat", "lon"), pairs)
+
+    low_rows, high_rows = value[h - width :], value[:width]
+    top = lax.ppermute(low_rows, "lat", [(i, i + 1) for i in range(n_lat - 1)])
+    bottom = lax.ppermute(high_rows, "lat", [(i + 1, i) for i in range(n_lat - 1)])
+    left = lax.ppermute(value[:, :, w - width :], "lon", [(i, (i + 1) % n_lon) for i in range(n_lon)])
+    right = lax.ppermute(value[:, :, :width], "lon", [((i + 1) % n_lon, i) for i in range(n_lon)])
+    top_left = shifted(low_rows[:, :, w - width :], 1, 1)
+    top_right = shifted(low_rows[:, :, :width], 1, -1)
+    bottom_left = shifted(high_rows[:, :, w - width :], -1, 1)
+    bottom_right = shifted(high_rows[:, :, :width], -1, -1)
+    return jnp.concatenate(
+        [
+            jnp.concatenate([top_left, top, top_right], axis=2),
+            jnp.concatenate([left, value, right], axis=2),
+            jnp.concatenate([bottom_left, bottom, bottom_right], axis=2),
+        ],
+        axis=0,
+    )
 
 
 def clear_outside(value, start, total):
@@ -75,8 +106,7 @@
     band = meridian_slab_data.shape[0]
     lat_total = band * lax.axis_size("lat")
     base = lax.axis_index("lat") * band
-    extended = extend_lat(meridian_slab_data, HALO)
-    extended = extend_lon(extended, HALO, 2)
+    extended = extend_both(meridian_slab_data, HALO)
     opening_halved = first_conv(extended, smoothing_filter_taps, smoothing_offset_entries)
     opening_halved = clear_outside(opening_halved, base - HALO + 1, lat_total)
     closing_halved = halving_filter(opening_halved, opening_coarsen_taps, opening_coarsen_offset)

time: 107 us -> 121 us (1.13)
  the two profiles are of different devices: /device:TPU:112 before, /device:TPU:144 now
where the time goes in v2:
time: 121 us; the launch traced here: 120 us
  starting transfers between devices  37.7 us (31%)
  matrix products  25.1 us (21%)
  local copies, waits for them, and re-layouts  24.4 us (20%)
  waiting for transfers between devices  11.1 us (9%)
  other arithmetic  10.8 us (9%)
  blocking collectives  10.4 us (9%)
    ppermute x4, starting transfers between devices, shifted(): return lax.ppermute(piece, ('lat', 'lon'), pairs)  18.5 us
    all_to_all x1, blocking collectives, on_device(): attended = lax.all_to_all(attended, 'lon', 0, 0, tiled=True)  10.4 us
    conv_general_dilated x7, local copies, waits for them, and re-layouts, halving_filter(): lax.conv_general_dilated(extended[None], kernel, (2, 2), 'VALID', dimensi...  10.4 us
    all_to_all x1, waiting for transfers between devices, on_device(): gathered = lax.all_to_all(row_copies, 'lon', 0, 0, tiled=True)  9.53 us
    unnamed x26, local copies, waits for them, and re-layouts  7.49 us
    concatenate x1, other arithmetic, extend_both(): jnp.concatenate([jnp.concatenate([top_left, top, top_right], axis=2), jnp...  7.49 us
    all_to_all x1, starting transfers between devices, on_device(): gathered = lax.all_to_all(row_copies, 'lon', 0, 0, tiled=True)  7.47 us
    dot_general x1, matrix products, on_device(): jnp.einsum('ist,itd->isd', weights.astype(jnp.bfloat16), v_items, preferr...  6.59 us
  transfers between devices with their start and end apart: 9, of which 2 were waited for; matrix products, arithmetic and copies ran while one was open for 3% of the time, Pallas kernels for 0%

profile of v2, /device:TPU:144, one launch (start us, length us, event | category | flops | bytes accessed | tf_op | source)
XLA Modules:
  0.0 120.1 jit_solution(14689419393322371984)
XLA Ops:
  0.0 4.6 %copy.14 = bf16[32,96,256]{1,0,2:T(8,128)(2,1)} copy(bf16[32,96,256]{2,1,0:T(8,128)(2,1)} %param.11) | data formatting | bytes 3145728 | tf_op args[0]
  4.6 0.8 fusion.77
  5.3 2.1 %collective-permute-start = (bf16[4,96,4]{1,0,2:T(4,128)(2,1)S(1)}, bf16[4,96,4]{1,0,2:T(4,128)(2,1)S(1)}, u32[]{:S(2)}, u32[]{:S(2)}) collective-permute-start(bf16[4,96,4]{1,0,2:T(4,128)(2,1)S(1)} %get-tuple-element.7), channel_id=1, source_target_pairs={{0,17},{1,18},{2,19},{3,20},{4,21},{5,22},{6,23},{7,24},{8,25},{9,... | collective-permute-start | bytes 9224 | tf_op jit(solution)/shard_map/ppermute | solution.py:40
  7.5 6.0 %collective-permute-start.2 = (bf16[4,96,4]{1,0,2:T(4,128)(2,1)S(1)}, bf16[4,96,4]{1,0,2:T(4,128)(2,1)S(1)}, u32[]{:S(2)}, u32[]{:S(2)}) collective-permute-start(bf16[4,96,4]{1,0,2:T(4,128)(2,1)S(1)} %get-tuple-element.10), channel_id=1, source_target_pairs={{0,31},{1,16},{2,17},{3,18},{4,19},{5,20},{6,21},{7,22},{8,23},{9,... | collective-permute-start | bytes 9224 | tf_op jit(solution)/shard_map/ppermute | solution.py:40
  13.5 1.9 %collective-permute-start.5 = (bf16[4,96,4]{1,0,2:T(4,128)(2,1)S(1)}, bf16[4,96,4]{1,0,2:T(4,128)(2,1)S(1)}, u32[]{:S(2)}, u32[]{:S(2)}) collective-permute-start(bf16[4,96,4]{1,0,2:T(4,128)(2,1)S(1)} %get-tuple-element.9), channel_id=1, source_target_pairs={{16,1},{17,2},{18,3},{19,4},{20,5},{21,6},{22,7},{23,8},{24,9},{25... | collective-permute-start | bytes 9224 | tf_op jit(solution)/shard_map/ppermute | solution.py:40
  15.4 1.4 %fusion.78 = (bf16[4,96,256]{1,0,2:T(4,128)(2,1)S(1)}, bf16[4,96,256]{1,0,2:T(4,128)(2,1)S(1)}) fusion(bf16[32,96,256]{1,0,2:T(8,128)(2,1)} %copy.14), kind=kLoop, calls=%fused_computation.82 | loop fusion | bytes 786432 | tf_op jit(solution)/shard_map/slice | solution.py:42
  16.8 5.2 %collective-permute-start.1 = (bf16[4,96,256]{1,0,2:T(4,128)(2,1)S(1)}, bf16[4,96,256]{1,0,2:T(4,128)(2,1)S(1)}, u32[]{:S(2)}, u32[]{:S(2)}) collective-permute-start(bf16[4,96,256]{1,0,2:T(4,128)(2,1)S(1)} %get-tuple-element.11), channel_id=1, source_target_pairs={{0,16},{16,32},{32,48},{48,64},{64,80},{80,96},{96,112},{112,128},... | collective-permute-start | bytes 589832 | tf_op jit(solution)/shard_map/ppermute | solution.py:43
  22.0 2.7 %collective-permute-start.6 = (bf16[4,96,256]{1,0,2:T(4,128)(2,1)S(1)}, bf16[4,96,256]{1,0,2:T(4,128)(2,1)S(1)}, u32[]{:S(2)}, u32[]{:S(2)}) collective-permute-start(bf16[4,96,256]{1,0,2:T(4,128)(2,1)S(1)} %get-tuple-element.12), channel_id=1, source_target_pairs={{16,0},{32,16},{48,32},{64,48},{80,64},{96,80},{112,96},{128,112},... | collective-permute-start | bytes 589832 | tf_op jit(solution)/shard_map/ppermute | solution.py:44
  24.7 0.8 fusion.79
  25.5 8.5 %collective-permute-start.7 = (bf16[4,96,4]{1,0,2:T(4,128)(2,1)S(1)}, bf16[4,96,4]{1,0,2:T(4,128)(2,1)S(1)}, u32[]{:S(2)}, u32[]{:S(2)}) collective-permute-start(bf16[4,96,4]{1,0,2:T(4,128)(2,1)S(1)} %get-tuple-element.8), channel_id=1, source_target_pairs={{16,15},{17,0},{18,1},{19,2},{20,3},{21,4},{22,5},{23,6},{24,7},{2... | collective-permute-start | bytes 9224 | tf_op jit(solution)/shard_map/ppermute | solution.py:40
  34.0 0.1 collective-permute-start.3
  34.1 3.8 %collective-permute-start.4 = (bf16[32,96,4]{1,0,2:T(8,128)(2,1)S(1)}, bf16[32,96,4]{1,0,2:T(8,128)(2,1)S(1)}, u32[]{:S(2)}, u32[]{:S(2)}) collective-permute-start(bf16[32,96,4]{1,0,2:T(8,128)(2,1)S(1)} %get-tuple-element.14), channel_id=1, source_target_pairs={{1,0},{2,1},{3,2},{4,3},{5,4},{6,5},{7,6},{8,7},{9,8},{10,9},{11,1... | collective-permute-start | bytes 73736 | tf_op jit(solution)/shard_map/ppermute | solution.py:46
  37.9 1.6 %collective-permute-done.3 = bf16[32,96,4]{1,0,2:T(8,128)(2,1)S(1)} collective-permute-done((bf16[32,96,4]{1,0,2:T(8,128)(2,1)S(1)}, bf16[32,96,4]{1,0,2:T(8,128)(2,1)S(1)}, u32[]{:S(2)}, u32[]{:S(2)}) %collective-permute-start.3) | collective-permute-done | bytes 24608 | tf_op jit(solution)/shard_map/ppermute | solution.py:45
  39.5 7.5 %maximum_maximum_fusion = bf16[40,96,264]{1,0,2:T(8,128)(2,1)S(1)} fusion(bf16[4,96,4]{1,0,2:T(4,128)(2,1)S(1)} %collective-permute-done.7, bf16[4,96,256]{1,0,2:T(4,128)(2,1)S(1)} %collective-permute-done.6, bf16[4,96,4]{1,0,2:T(4,128)(2,1)S(1)} %collective-permute-done.5, bf16[32,96,4]{1,0,2:T(8,128)(2,1)S(1)} %collective-permute-done.4, ...), kind=kLoop, calls=%fused_computation.23 | loop fusion | flops 18247680 | bytes 4055040 | tf_op jit(solution)/shard_map/concatenate | solution.py:51
  47.1 0.4 copy.24
  47.5 0.5 copy-done.6
  48.0 6.4 %select_select_fusion = bf16[38,8,33,128]{3,1,2,0:T(8,128)(2,1)S(1)} fusion(f32[128]{0:T(128)S(1)} %copy-done.7, pred[38]{0:T(512)(128)(4,1)S(1)} %compare_and_fusion, pred[8,33]{0,1:T(8,128)(4,1)S(1)} %copy-done.9, bf16[3,3,96,128]{3,2,1,0:T(8,128)(2,1)S(1)} %copy-done.6, bf16[40,96,1,7,2]{1,3,4,0,2:T(8,128)(2,1)S(1)} %slice.63, ...), kind=kOutput, calls=%fused_computation.24 | convolution fusion | flops 2236925952 | bytes 4925230 | tf_op jit(solution)/shard_map/conv_general_dilated | solution.py:70
  54.3 0.4 copy.25
  54.7 0.5 pad.1
  55.2 0.7 copy.27
  56.0 0.5 copy-done.5
  56.5 2.9 %fusion.8 = f32[18,8,17,256]{3,1,2,0:T(8,128)S(1)} fusion(bf16[4,4,128,256]{3,2,1,0:T(8,128)(2,1)S(1)} %copy-done.5, bf16[38,1,7,3,128]{4,2,3,0,1:T(8,128)(2,1)S(1)} %slice.64, bf16[38,1,8,34,128]{4,2,3,0,1:T(8,128)(2,1)S(1)} %copy.27), kind=kOutput, calls=%fused_computation.13 | convolution fusion | flops 2575552512 | bytes 6405632 | tf_op jit(solution)/shard_map/conv_general_dilated | solution.py:82
  59.4 2.7 %copy.28 = f32[18,8,17,256]{3,2,1,0:T(8,128)} copy(f32[18,8,17,256]{3,1,2,0:T(8,128)S(1)} %fusion.8) | data formatting | bytes 5013504 | tf_op jit(solution)/shard_map/conv_general_dilated | solution.py:82
  62.1 4.2 %reshape.74 = f32[18,1,136,256]{3,2,0,1:T(8,128)} reshape(f32[18,8,17,256]{3,2,1,0:T(8,128)} %copy.28) | data formatting | bytes 5013504 | tf_op jit(solution)/shard_map/conv_general_dilated | solution.py:82
  66.3 2.5 %fusion.38 = bf16[18,130,256]{2,1,0:T(8,128)(2,1)S(1)} fusion(f32[256]{0:T(256)S(1)} %copy-done.2, f32[18,1,136,256]{3,2,0,1:T(8,128)} %reshape.74, pred[18]{0:T(512)(128)(4,1)S(1)} %compare_and_fusion.1), kind=kLoop, calls=%fused_computation.38 | loop fusion | flops 4193280 | bytes 3595282 | tf_op jit(solution)/shard_map/jit(_where)/select_n | solution.py:66
  68.8 0.1 pad.3
  68.9 1.4 %reshape.77 = bf16[18,1,8,18,256]{4,3,2,0,1:T(8,128)(2,1)} reshape(bf16[18,1,144,256]{3,2,0,1:T(8,128)(2,1)S(1)} %pad.3) | data formatting | bytes 2654208 | tf_op jit(solution)/shard_map/conv_general_dilated | solution.py:82
  70.3 1.8 %copy.30 = bf16[18,1,8,18,256]{4,2,3,0,1:T(8,128)(2,1)S(1)} copy(bf16[18,1,8,18,256]{4,3,2,0,1:T(8,128)(2,1)} %reshape.77) | data formatting | bytes 2654208 | tf_op jit(solution)/shard_map/conv_general_dilated | solution.py:82
  72.2 1.4 %fusion.39 = f32[8,8,9,256]{3,1,2,0:T(8,128)S(1)} fusion(bf16[4,4,256,256]{3,2,1,0:T(8,128)(2,1)S(1)} %copy-done, bf16[18,1,7,3,256]{4,2,3,0,1:T(8,128)(2,1)S(1)} %slice.66, bf16[18,1,8,18,256]{4,2,3,0,1:T(8,128)(2,1)S(1)} %copy.30, pred[8,9]{0,1:T(8,128)(4,1)S(1)} %copy-done.10), kind=kOutput, calls=%fused_computation.40 | convolution fusion | flops 1212751872 | bytes 4207688 | tf_op jit(solution)/shard_map/conv_general_dilated | solution.py:82
  73.6 0.2 copy.31
  73.9 0.3 convert_reduce_fusion
  74.2 0.3 fusion.56
  74.5 0.2 fusion.58
  74.7 0.8 broadcast_in_dim.47
  75.5 7.5 %all-to-all-start = ((bf16[16,64,256]{2,1,0:T(8,128)(2,1)}), bf16[16,64,256]{2,1,0:T(8,128)(2,1)S(1)}, u32[]{:S(2)}, u32[]{:S(2)}) async-start(bf16[16,64,256]{2,1,0:T(8,128)(2,1)} %bitcast.11), calls=%async_computation | async-start | bytes 1048576 | tf_op jit(solution)/shard_map/all_to_all | solution.py:133
  83.0 1.2 copy.33
  84.2 0.1 dynamic_slice.7
  84.3 9.5 %all-to-all-done = bf16[16,64,256]{2,1,0:T(8,128)(2,1)S(1)} async-done(((bf16[16,64,256]{2,1,0:T(8,128)(2,1)}), bf16[16,64,256]{2,1,0:T(8,128)(2,1)S(1)}, u32[]{:S(2)}, u32[]{:S(2)}) %all-to-all-start) | async-done | bytes 524320 | tf_op jit(solution)/shard_map/all_to_all | solution.py:133
  93.8 1.3 %fusion.80 = (bf16[3,4,1024,32]{2,3,1,0:T(8,128)(2,1)}, f32[3,4,1024,32]{2,3,1,0:T(8,128)S(1)}) fusion(bf16[1024,256,1,1]{1,0,3,2:T(8,128)(2,1)S(1)} %bitcast.98, bf16[256,3,8,32]{0,3,2,1:T(8,128)(2,1)S(1)} %bitcast.101, s32[]{:T(128)S(6)} %select_n.28), kind=kOutput, calls=%fused_computation.84 | convolution fusion | flops 201719808 | bytes 3080196 | tf_op jit(solution)/shard_map/tc,cjhd->jhtd/dot_general | solution.py:137
  95.1 0.1 fusion.60
  95.2 5.5 %fusion.81 = f32[4,1024]{1,0:T(4,128)S(1)} fusion(bf16[4,1024,32]{1,2,0:T(8,128)(2,1)S(1)} %fusion.60, bf16[3,4,1024,32]{2,3,1,0:T(8,128)(2,1)} %get-tuple-element.15), kind=kOutput, calls=%fused_computation.85 | convolution fusion | flops 276825088 | bytes 540672 | tf_op jit(solution)/shard_map/sub | solution.py:145
  100.7 6.6 %fusion.48 = bf16[4,1024,32]{1,2,0:T(8,128)(2,1)S(1)} fusion(bf16[4,1024,32]{1,2,0:T(8,128)(2,1)S(1)} %fusion.60, bf16[3,4,1024,32]{2,3,1,0:T(8,128)(2,1)} %get-tuple-element.15, f32[4,1024]{1,0:T(4,128)S(1)} %fusion.81), kind=kOutput, calls=%fused_computation.43 | convolution fusion | flops 545526784 | bytes 1064960 | tf_op jit(solution)/shard_map/ist,itd->isd/dot_general | solution.py:147
  107.3 0.3 reshape.58
  107.7 0.1 copy.50
  107.8 0.4 reshape.102
  108.2 10.4 %all_to_all.10 = bf16[16,2,4096]{2,1,0:T(2,128)(2,1)S(1)} all-to-all(bf16[16,2,4096]{2,1,0:T(2,128)(2,1)S(1)} %reshape.102), channel_id=1, replica_groups=mesh['lat'=16,'lon'=16] {'lon'}, dimensions={0} | all-to-all | bytes 524288 | tf_op jit(solution)/shard_map/all_to_all | solution.py:153
  118.7 0.3 reshape.103
  119.0 1.0 fusion.42
  (36 shorter events, 0.3 us)
Async XLA Ops:
  0.0 72.2 %copy-start = (bf16[4,4,256,256]{3,2,1,0:T(8,128)(2,1)S(1)}, bf16[4,4,256,256]{3,2,1,0:T(8,128)(2,1)}, u32[]{:S(2)}) copy-start(bf16[4,4,256,256]{3,2,1,0:T(8,128)(2,1)} %param.16) | copy-start | bytes 6291460
  5.3 20.2 %collective-permute-start = (bf16[4,96,4]{1,0,2:T(4,128)(2,1)S(1)}, bf16[4,96,4]{1,0,2:T(4,128)(2,1)S(1)}, u32[]{:S(2)}, u32[]{:S(2)}) collective-permute-start(bf16[4,96,4]{1,0,2:T(4,128)(2,1)S(1)} %get-tuple-element.7), channel_id=1, source_target_pairs={{0,17},{1,18},{2,19},{3,20},{4,21},{5,22},{6,23},{7,24},{8,25},{9,... | collective-permute-start | bytes 9224 | tf_op jit(solution)/shard_map/ppermute | solution.py:40
  7.5 26.5 %collective-permute-start.2 = (bf16[4,96,4]{1,0,2:T(4,128)(2,1)S(1)}, bf16[4,96,4]{1,0,2:T(4,128)(2,1)S(1)}, u32[]{:S(2)}, u32[]{:S(2)}) collective-permute-start(bf16[4,96,4]{1,0,2:T(4,128)(2,1)S(1)} %get-tuple-element.10), channel_id=1, source_target_pairs={{0,31},{1,16},{2,17},{3,18},{4,19},{5,20},{6,21},{7,22},{8,23},{9,... | collective-permute-start | bytes 9224 | tf_op jit(solution)/shard_map/ppermute | solution.py:40
  13.5 20.6 %collective-permute-start.5 = (bf16[4,96,4]{1,0,2:T(4,128)(2,1)S(1)}, bf16[4,96,4]{1,0,2:T(4,128)(2,1)S(1)}, u32[]{:S(2)}, u32[]{:S(2)}) collective-permute-start(bf16[4,96,4]{1,0,2:T(4,128)(2,1)S(1)} %get-tuple-element.9), channel_id=1, source_target_pairs={{16,1},{17,2},{18,3},{19,4},{20,5},{21,6},{22,7},{23,8},{24,9},{25... | collective-permute-start | bytes 9224 | tf_op jit(solution)/shard_map/ppermute | solution.py:40
  16.8 22.7 %collective-permute-start.1 = (bf16[4,96,256]{1,0,2:T(4,128)(2,1)S(1)}, bf16[4,96,256]{1,0,2:T(4,128)(2,1)S(1)}, u32[]{:S(2)}, u32[]{:S(2)}) collective-permute-start(bf16[4,96,256]{1,0,2:T(4,128)(2,1)S(1)} %get-tuple-element.11), channel_id=1, source_target_pairs={{0,16},{16,32},{32,48},{48,64},{64,80},{80,96},{96,112},{112,128},... | collective-permute-start | bytes 589832 | tf_op jit(solution)/shard_map/ppermute | solution.py:43
  22.0 17.5 %collective-permute-start.6 = (bf16[4,96,256]{1,0,2:T(4,128)(2,1)S(1)}, bf16[4,96,256]{1,0,2:T(4,128)(2,1)S(1)}, u32[]{:S(2)}, u32[]{:S(2)}) collective-permute-start(bf16[4,96,256]{1,0,2:T(4,128)(2,1)S(1)} %get-tuple-element.12), channel_id=1, source_target_pairs={{16,0},{32,16},{48,32},{64,48},{80,64},{96,80},{112,96},{128,112},... | collective-permute-start | bytes 589832 | tf_op jit(solution)/shard_map/ppermute | solution.py:44
  25.5 12.4 %collective-permute-start.7 = (bf16[4,96,4]{1,0,2:T(4,128)(2,1)S(1)}, bf16[4,96,4]{1,0,2:T(4,128)(2,1)S(1)}, u32[]{:S(2)}, u32[]{:S(2)}) collective-permute-start(bf16[4,96,4]{1,0,2:T(4,128)(2,1)S(1)} %get-tuple-element.8), channel_id=1, source_target_pairs={{16,15},{17,0},{18,1},{19,2},{20,3},{21,4},{22,5},{23,6},{24,7},{2... | collective-permute-start | bytes 9224 | tf_op jit(solution)/shard_map/ppermute | solution.py:40
  34.0 5.5 %collective-permute-start.3 = (bf16[32,96,4]{1,0,2:T(8,128)(2,1)S(1)}, bf16[32,96,4]{1,0,2:T(8,128)(2,1)S(1)}, u32[]{:S(2)}, u32[]{:S(2)}) collective-permute-start(bf16[32,96,4]{1,0,2:T(8,128)(2,1)S(1)} %get-tuple-element.13), channel_id=1, source_target_pairs={{0,1},{1,2},{2,3},{3,4},{4,5},{5,6},{6,7},{7,8},{8,9},{9,10},{10,1... | collective-permute-start | bytes 73736 | tf_op jit(solution)/shard_map/ppermute | solution.py:45
  34.1 5.4 %collective-permute-start.4 = (bf16[32,96,4]{1,0,2:T(8,128)(2,1)S(1)}, bf16[32,96,4]{1,0,2:T(8,128)(2,1)S(1)}, u32[]{:S(2)}, u32[]{:S(2)}) collective-permute-start(bf16[32,96,4]{1,0,2:T(8,128)(2,1)S(1)} %get-tuple-element.14), channel_id=1, source_target_pairs={{1,0},{2,1},{3,2},{4,3},{5,4},{6,5},{7,6},{8,7},{9,8},{10,9},{11,1... | collective-permute-start | bytes 73736 | tf_op jit(solution)/shard_map/ppermute | solution.py:46
  47.0 0.9 copy-start.6
  47.0 0.9 copy-start.7
  47.1 0.9 copy-start.9
  55.2 1.2 %copy-start.5 = (bf16[4,4,128,256]{3,2,1,0:T(8,128)(2,1)S(1)}, bf16[4,4,128,256]{3,2,1,0:T(8,128)(2,1)}, u32[]{:S(2)}) copy-start(bf16[4,4,128,256]{3,2,1,0:T(8,128)(2,1)} %param.14) | copy-start | bytes 3145732
  62.1 4.2 %copy-start.2 = (f32[256]{0:T(256)S(1)}, f32[256]{0:T(256)}, u32[]{:S(2)}) copy-start(f32[256]{0:T(256)} %param.15) | copy-start | bytes 3076
  68.9 3.3 %copy-start.10 = (pred[8,9]{0,1:T(8,128)(4,1)S(1)}, pred[8,9]{0,1:T(8,128)(4,1)}, u32[]{:S(2)}) copy-start(pred[8,9]{0,1:T(8,128)(4,1)} %constant.83) | copy-start | bytes 220
  72.2 1.7 %copy-start.3 = (f32[256]{0:T(256)S(1)}, f32[256]{0:T(256)}, u32[]{:S(2)}) copy-start(f32[256]{0:T(256)} %param.17) | copy-start | bytes 3076
  73.6 0.9 copy-start.4
  73.8 10.4 %copy-start.8 = (f32[8]{0:T(128)S(1)}, f32[8]{0:T(128)}, u32[]{:S(2)}) copy-start(f32[8]{0:T(128)} %param.20) | copy-start | bytes 100
  75.5 18.3 %all-to-all-start = ((bf16[16,64,256]{2,1,0:T(8,128)(2,1)}), bf16[16,64,256]{2,1,0:T(8,128)(2,1)S(1)}, u32[]{:S(2)}, u32[]{:S(2)}) async-start(bf16[16,64,256]{2,1,0:T(8,128)(2,1)} %bitcast.11), calls=%async_computation | async-start | bytes 1048576 | tf_op jit(solution)/shard_map/all_to_all | solution.py:133
  107.3 11.7 %copy-start.1 = (bf16[256,256]{1,0:T(8,128)(2,1)S(1)}, bf16[256,256]{1,0:T(8,128)(2,1)}, u32[]{:S(2)}) copy-start(bf16[256,256]{1,0:T(8,128)(2,1)} %param.21) | copy-start | bytes 393220

commit v3 on v1

--- a/solution.py
+++ b/solution.py
@@ -11,8 +11,9 @@
     size, length = lax.axis_size("lat"), value.shape[0]
     up = [(i, i + 1) for i in range(size - 1)]
     down = [(i + 1, i) for i in range(size - 1)]
-    before = lax.ppermute(value[length - width :], "lat", up)
-    after = lax.ppermute(value[:width], "lat", down)
+    source = lax.optimization_barrier(value)
+    before = lax.ppermute(source[length - width :], "lat", up)
+    after = lax.ppermute(source[:width], "lat", down)
     return jnp.concatenate([before, value, after], axis=0)
 
 

time: 107 us -> 102 us (0.953)
  waiting for transfers between devices: 21.9 us -> 17.5 us
    ppermute x2, waiting for transfers between devices: 10.7 us -> 6.24 us  [the longest x1 6.24 us: extend_lat(): after = lax.ppermute(source[:width], 'lat', down)]
    unnamed x28 -> x30, local copies, waits for them, and re-layouts: 7.51 us -> 7.72 us
  transfers between devices with their start and end apart: 5 -> 5, of which waited for: 4 -> 3; matrix products, arithmetic and copies ran while one was open for 1% -> 6% of each run, Pallas kernels for 0% -> 0%
where the time goes in v3:
time: 102 us; the launch traced here: 101 us
  matrix products  24.9 us (24%)
  local copies, waits for them, and re-layouts  22.9 us (22%)
  waiting for transfers between devices  17.5 us (17%)
  starting transfers between devices  17.2 us (17%)
  blocking collectives  10.4 us (10%)
  other arithmetic  7.65 us (8%)
    all_to_all x1, blocking collectives, on_device(): attended = lax.all_to_all(attended, 'lon', 0, 0, tiled=True)  10.4 us
    conv_general_dilated x7, local copies, waits for them, and re-layouts, halving_filter(): lax.conv_general_dilated(extended[None], kernel, (2, 2), 'VALID', dimensi...  10.4 us
    all_to_all x1, waiting for transfers between devices, on_device(): gathered = lax.all_to_all(row_copies, 'lon', 0, 0, tiled=True)  9.54 us
    unnamed x30, local copies, waits for them, and re-layouts  7.72 us
    dot_general x1, matrix products, on_device(): jnp.einsum('ist,itd->isd', weights.astype(jnp.bfloat16), v_items, preferr...  6.59 us
    ppermute x1, waiting for transfers between devices, extend_lat(): after = lax.ppermute(source[:width], 'lat', down)  6.24 us
    conv_general_dilated x1, matrix products, first_conv(): lax.conv_general_dilated(extended[None], kernel, (1, 1), 'VALID', dimensi...  6.18 us
    all_to_all x1, starting transfers between devices, on_device(): gathered = lax.all_to_all(row_copies, 'lon', 0, 0, tiled=True)  5.95 us
  transfers between devices with their start and end apart: 5, of which 3 were waited for; matrix products, arithmetic and copies ran while one was open for 6% of the time, Pallas kernels for 0%

profile of v3, /device:TPU:112, one launch (start us, length us, event | category | flops | bytes accessed | tf_op | source)
XLA Modules:
  0.0 100.9 jit_solution(11183874542185466218)
XLA Ops:
  0.0 1.2 %fusion.77 = (bf16[4,96,256]{2,1,0:T(8,128)(2,1)S(1)}, bf16[4,96,256]{2,1,0:T(8,128)(2,1)S(1)}) fusion(bf16[32,96,256]{2,1,0:T(8,128)(2,1)} %param.11), kind=kLoop, calls=%fused_computation.84 | loop fusion | bytes 786432 | tf_op jit(solution)/shard_map/slice | solution.py:15
  1.2 0.2 copy.34
  1.4 4.8 %collective-permute-start = (bf16[4,96,256]{1,0,2:T(4,128)(2,1)S(1)}, bf16[4,96,256]{1,0,2:T(4,128)(2,1)S(1)}, u32[]{:S(2)}, u32[]{:S(2)}) collective-permute-start(bf16[4,96,256]{1,0,2:T(4,128)(2,1)S(1)} %copy.34), channel_id=1, source_target_pairs={{0,16},{16,32},{32,48},{48,64},{64,80},{80,96},{96,112},{112,128},... | collective-permute-start | bytes 589832 | tf_op jit(solution)/shard_map/ppermute | solution.py:15
  6.2 0.2 copy.35
  6.4 2.5 %collective-permute-start.1 = (bf16[4,96,256]{1,0,2:T(4,128)(2,1)S(1)}, bf16[4,96,256]{1,0,2:T(4,128)(2,1)S(1)}, u32[]{:S(2)}, u32[]{:S(2)}) collective-permute-start(bf16[4,96,256]{1,0,2:T(4,128)(2,1)S(1)} %copy.35), channel_id=1, source_target_pairs={{16,0},{32,16},{48,32},{64,48},{80,64},{96,80},{112,96},{128,112},... | collective-permute-start | bytes 589832 | tf_op jit(solution)/shard_map/ppermute | solution.py:16
  8.9 4.5 %copy.16 = bf16[32,96,256]{1,0,2:T(8,128)(2,1)} copy(bf16[32,96,256]{2,1,0:T(8,128)(2,1)} %param.11) | data formatting | bytes 3145728 | tf_op args[0]
  13.4 6.2 %collective-permute-done.1 = bf16[4,96,256]{1,0,2:T(4,128)(2,1)S(1)} collective-permute-done((bf16[4,96,256]{1,0,2:T(4,128)(2,1)S(1)}, bf16[4,96,256]{1,0,2:T(4,128)(2,1)S(1)}, u32[]{:S(2)}, u32[]{:S(2)}) %collective-permute-start.1) | collective-permute-done | bytes 196640 | tf_op jit(solution)/shard_map/ppermute | solution.py:16
  19.7 0.8 pad_maximum_fusion.3
  20.5 0.1 collective-permute-start.2
  20.6 3.8 %collective-permute-start.3 = (bf16[40,96,4]{1,0,2:T(8,128)(2,1)S(1)}, bf16[40,96,4]{1,0,2:T(8,128)(2,1)S(1)}, u32[]{:S(2)}, u32[]{:S(2)}) collective-permute-start(bf16[40,96,4]{1,0,2:T(8,128)(2,1)S(1)} %get-tuple-element.8), channel_id=1, source_target_pairs={{1,0},{2,1},{3,2},{4,3},{5,4},{6,5},{7,6},{8,7},{9,8},{10,9},{11,1... | collective-permute-start | bytes 92168 | tf_op jit(solution)/shard_map/ppermute | solution.py:27
  24.4 1.7 %collective-permute-done.2 = bf16[40,96,4]{1,0,2:T(8,128)(2,1)S(1)} collective-permute-done((bf16[40,96,4]{1,0,2:T(8,128)(2,1)S(1)}, bf16[40,96,4]{1,0,2:T(8,128)(2,1)S(1)}, u32[]{:S(2)}, u32[]{:S(2)}) %collective-permute-start.2) | collective-permute-done | bytes 30752 | tf_op jit(solution)/shard_map/ppermute | solution.py:26
  26.1 3.5 %pad_maximum_fusion = bf16[40,96,264]{1,0,2:T(8,128)(2,1)S(1)} fusion(bf16[40,96,4]{1,0,2:T(8,128)(2,1)S(1)} %collective-permute-done.3, bf16[4,96,256]{1,0,2:T(4,128)(2,1)S(1)} %collective-permute-done.1, bf16[32,96,256]{1,0,2:T(8,128)(2,1)S(1)} %copy-done.1, bf16[4,96,256]{1,0,2:T(4,128)(2,1)S(1)} %collective-permute-done, ...), kind=kLoop, calls=%fused_computation.23 | loop fusion | flops 10137600 | bytes 4055040 | tf_op jit(solution)/shard_map/concatenate | solution.py:28
  29.6 0.4 copy.18
  30.0 0.5 copy-done.7
  30.5 6.2 %select_select_fusion = bf16[38,8,33,128]{3,1,2,0:T(8,128)(2,1)S(1)} fusion(f32[128]{0:T(128)S(1)} %copy-done.8, pred[38]{0:T(512)(128)(4,1)S(1)} %compare_and_fusion, pred[8,33]{0,1:T(8,128)(4,1)S(1)} %copy-done.10, bf16[3,3,96,128]{3,2,1,0:T(8,128)(2,1)S(1)} %copy-done.7, bf16[40,96,1,7,2]{1,3,4,0,2:T(8,128)(2,1)S(1)} %slice.37, ...), kind=kOutput, calls=%fused_computation.24 | convolution fusion | flops 2236925952 | bytes 4925230 | tf_op jit(solution)/shard_map/conv_general_dilated | solution.py:40
  36.7 0.4 copy.19
  37.1 0.5 pad.1
  37.6 0.7 copy.21
  38.3 0.1 slice.38
  38.4 0.5 copy-done.6
  38.8 2.9 %fusion.8 = f32[18,8,17,256]{3,1,2,0:T(8,128)S(1)} fusion(bf16[4,4,128,256]{3,2,1,0:T(8,128)(2,1)S(1)} %copy-done.6, bf16[38,1,7,3,128]{4,2,3,0,1:T(8,128)(2,1)S(1)} %slice.38, bf16[38,1,8,34,128]{4,2,3,0,1:T(8,128)(2,1)S(1)} %copy.21), kind=kOutput, calls=%fused_computation.13 | convolution fusion | flops 2575552512 | bytes 6405632 | tf_op jit(solution)/shard_map/conv_general_dilated | solution.py:52
  41.7 2.7 %copy.22 = f32[18,8,17,256]{3,2,1,0:T(8,128)} copy(f32[18,8,17,256]{3,1,2,0:T(8,128)S(1)} %fusion.8) | data formatting | bytes 5013504 | tf_op jit(solution)/shard_map/conv_general_dilated | solution.py:52
  44.4 4.2 %reshape.74 = f32[18,1,136,256]{3,2,0,1:T(8,128)} reshape(f32[18,8,17,256]{3,2,1,0:T(8,128)} %copy.22) | data formatting | bytes 5013504 | tf_op jit(solution)/shard_map/conv_general_dilated | solution.py:52
  48.7 2.5 %fusion.38 = bf16[18,130,256]{2,1,0:T(8,128)(2,1)S(1)} fusion(f32[256]{0:T(256)S(1)} %copy-done.3, f32[18,1,136,256]{3,2,0,1:T(8,128)} %reshape.74, pred[18]{0:T(512)(128)(4,1)S(1)} %compare_and_fusion.1), kind=kLoop, calls=%fused_computation.38 | loop fusion | flops 4193280 | bytes 3595282 | tf_op jit(solution)/shard_map/jit(_where)/select_n | solution.py:36
  51.1 0.1 pad.3
  51.2 1.4 %reshape.77 = bf16[18,1,8,18,256]{4,3,2,0,1:T(8,128)(2,1)} reshape(bf16[18,1,144,256]{3,2,0,1:T(8,128)(2,1)S(1)} %pad.3) | data formatting | bytes 2654208 | tf_op jit(solution)/shard_map/conv_general_dilated | solution.py:52
  52.7 1.8 %copy.24 = bf16[18,1,8,18,256]{4,2,3,0,1:T(8,128)(2,1)S(1)} copy(bf16[18,1,8,18,256]{4,3,2,0,1:T(8,128)(2,1)} %reshape.77) | data formatting | bytes 2654208 | tf_op jit(solution)/shard_map/conv_general_dilated | solution.py:52
  54.5 0.1 slice.40
  54.6 1.4 %fusion.39 = f32[8,8,9,256]{3,1,2,0:T(8,128)S(1)} fusion(bf16[4,4,256,256]{3,2,1,0:T(8,128)(2,1)S(1)} %copy-done, bf16[18,1,7,3,256]{4,2,3,0,1:T(8,128)(2,1)S(1)} %slice.40, bf16[18,1,8,18,256]{4,2,3,0,1:T(8,128)(2,1)S(1)} %copy.24, pred[8,9]{0,1:T(8,128)(4,1)S(1)} %copy-done.11), kind=kOutput, calls=%fused_computation.40 | convolution fusion | flops 1212751872 | bytes 4207688 | tf_op jit(solution)/shard_map/conv_general_dilated | solution.py:52
  56.0 0.2 copy.25
  56.2 0.3 convert_reduce_fusion
  56.5 0.3 fusion.56
  56.8 0.2 fusion.58
  57.0 0.8 broadcast_in_dim.47
  57.9 5.9 %all-to-all-start = ((bf16[16,64,256]{2,1,0:T(8,128)(2,1)}), bf16[16,64,256]{2,1,0:T(8,128)(2,1)S(1)}, u32[]{:S(2)}, u32[]{:S(2)}) async-start(bf16[16,64,256]{2,1,0:T(8,128)(2,1)} %bitcast.11), calls=%async_computation | async-start | bytes 1048576 | tf_op jit(solution)/shard_map/all_to_all | solution.py:104
  63.9 1.2 %copy.27 = bf16[256,768]{0,1:T(8,128)(2,1)S(1)} copy(bf16[256,768]{1,0:T(8,128)(2,1)} %param.19) | data formatting | bytes 786432 | tf_op args[8]
  65.1 0.1 dynamic_slice.7
  65.1 9.5 %all-to-all-done = bf16[16,64,256]{2,1,0:T(8,128)(2,1)S(1)} async-done(((bf16[16,64,256]{2,1,0:T(8,128)(2,1)}), bf16[16,64,256]{2,1,0:T(8,128)(2,1)S(1)}, u32[]{:S(2)}, u32[]{:S(2)}) %all-to-all-start) | async-done | bytes 524320 | tf_op jit(solution)/shard_map/all_to_all | solution.py:104
  74.7 1.3 %fusion.78 = (bf16[3,4,1024,32]{2,3,1,0:T(8,128)(2,1)}, f32[3,4,1024,32]{2,3,1,0:T(8,128)S(1)}) fusion(bf16[1024,256,1,1]{1,0,3,2:T(8,128)(2,1)S(1)} %bitcast.98, bf16[256,3,8,32]{0,3,2,1:T(8,128)(2,1)S(1)} %bitcast.101, s32[]{:T(128)S(6)} %select_n.28), kind=kOutput, calls=%fused_computation.85 | convolution fusion | flops 201719808 | bytes 3080196 | tf_op jit(solution)/shard_map/tc,cjhd->jhtd/dot_general | solution.py:108
  76.0 0.1 fusion.60
  76.1 5.5 %fusion.79 = f32[4,1024]{1,0:T(4,128)S(1)} fusion(bf16[4,1024,32]{1,2,0:T(8,128)(2,1)S(1)} %fusion.60, bf16[3,4,1024,32]{2,3,1,0:T(8,128)(2,1)} %get-tuple-element.11), kind=kOutput, calls=%fused_computation.86 | convolution fusion | flops 276825088 | bytes 540672 | tf_op jit(solution)/shard_map/sub | solution.py:116
  81.6 6.6 %fusion.48 = bf16[4,1024,32]{1,2,0:T(8,128)(2,1)S(1)} fusion(bf16[4,1024,32]{1,2,0:T(8,128)(2,1)S(1)} %fusion.60, bf16[3,4,1024,32]{2,3,1,0:T(8,128)(2,1)} %get-tuple-element.11, f32[4,1024]{1,0:T(4,128)S(1)} %fusion.79), kind=kOutput, calls=%fused_computation.43 | convolution fusion | flops 545526784 | bytes 1064960 | tf_op jit(solution)/shard_map/ist,itd->isd/dot_general | solution.py:118
  88.2 0.3 reshape.58
  88.5 0.1 copy.46
  88.7 0.4 reshape.102
  89.1 10.4 %all_to_all.10 = bf16[16,2,4096]{2,1,0:T(2,128)(2,1)S(1)} all-to-all(bf16[16,2,4096]{2,1,0:T(2,128)(2,1)S(1)} %reshape.102), channel_id=1, replica_groups=mesh['lat'=16,'lon'=16] {'lon'}, dimensions={0} | all-to-all | bytes 524288 | tf_op jit(solution)/shard_map/all_to_all | solution.py:124
  99.5 0.3 reshape.103
  99.9 1.0 %fusion.42 = bf16[8,64,256]{2,1,0:T(8,128)(2,1)} fusion(bf16[8,64,256]{1,2,0:T(8,128)(2,1)S(1)} %bitcast.99, bf16[8,64,256]{2,1,0:T(8,128)(2,1)S(1)} %get-tuple-element.6, bf16[256,256]{1,0:T(8,128)(2,1)S(1)} %copy-done.2), kind=kOutput, calls=%fused_computation.41 | convolution fusion | flops 67502080 | bytes 917504 | tf_op jit(solution)/shard_map/dot_general | solution.py:127
  (31 shorter events, 0.2 us)
Async XLA Ops:
  0.0 54.5 %copy-start = (bf16[4,4,256,256]{3,2,1,0:T(8,128)(2,1)S(1)}, bf16[4,4,256,256]{3,2,1,0:T(8,128)(2,1)}, u32[]{:S(2)}) copy-start(bf16[4,4,256,256]{3,2,1,0:T(8,128)(2,1)} %param.16) | copy-start | bytes 6291460
  1.4 12.0 %collective-permute-start = (bf16[4,96,256]{1,0,2:T(4,128)(2,1)S(1)}, bf16[4,96,256]{1,0,2:T(4,128)(2,1)S(1)}, u32[]{:S(2)}, u32[]{:S(2)}) collective-permute-start(bf16[4,96,256]{1,0,2:T(4,128)(2,1)S(1)} %copy.34), channel_id=1, source_target_pairs={{0,16},{16,32},{32,48},{48,64},{64,80},{80,96},{96,112},{112,128},... | collective-permute-start | bytes 589832 | tf_op jit(solution)/shard_map/ppermute | solution.py:15
  6.4 13.3 %collective-permute-start.1 = (bf16[4,96,256]{1,0,2:T(4,128)(2,1)S(1)}, bf16[4,96,256]{1,0,2:T(4,128)(2,1)S(1)}, u32[]{:S(2)}, u32[]{:S(2)}) collective-permute-start(bf16[4,96,256]{1,0,2:T(4,128)(2,1)S(1)} %copy.35), channel_id=1, source_target_pairs={{16,0},{32,16},{48,32},{64,48},{80,64},{96,80},{112,96},{128,112},... | collective-permute-start | bytes 589832 | tf_op jit(solution)/shard_map/ppermute | solution.py:16
  13.4 12.7 %copy-start.1 = (bf16[32,96,256]{1,0,2:T(8,128)(2,1)S(1)}, bf16[32,96,256]{1,0,2:T(8,128)(2,1)}, u32[]{:S(2)}) copy-start(bf16[32,96,256]{1,0,2:T(8,128)(2,1)} %copy.16) | copy-start | bytes 4718596
  20.5 5.6 %collective-permute-start.2 = (bf16[40,96,4]{1,0,2:T(8,128)(2,1)S(1)}, bf16[40,96,4]{1,0,2:T(8,128)(2,1)S(1)}, u32[]{:S(2)}, u32[]{:S(2)}) collective-permute-start(bf16[40,96,4]{1,0,2:T(8,128)(2,1)S(1)} %get-tuple-element.7), channel_id=1, source_target_pairs={{0,1},{1,2},{2,3},{3,4},{4,5},{5,6},{6,7},{7,8},{8,9},{9,10},{10,1... | collective-permute-start | bytes 92168 | tf_op jit(solution)/shard_map/ppermute | solution.py:26
  20.6 5.5 %collective-permute-start.3 = (bf16[40,96,4]{1,0,2:T(8,128)(2,1)S(1)}, bf16[40,96,4]{1,0,2:T(8,128)(2,1)S(1)}, u32[]{:S(2)}, u32[]{:S(2)}) collective-permute-start(bf16[40,96,4]{1,0,2:T(8,128)(2,1)S(1)} %get-tuple-element.8), channel_id=1, source_target_pairs={{1,0},{2,1},{3,2},{4,3},{5,4},{6,5},{7,6},{8,7},{9,8},{10,9},{11,1... | collective-permute-start | bytes 92168 | tf_op jit(solution)/shard_map/ppermute | solution.py:27
  29.6 0.9 copy-start.7
  29.6 0.9 copy-start.8
  29.6 0.9 copy-start.10
  37.6 1.2 %copy-start.6 = (bf16[4,4,128,256]{3,2,1,0:T(8,128)(2,1)S(1)}, bf16[4,4,128,256]{3,2,1,0:T(8,128)(2,1)}, u32[]{:S(2)}) copy-start(bf16[4,4,128,256]{3,2,1,0:T(8,128)(2,1)} %param.14) | copy-start | bytes 3145732
  44.4 4.2 %copy-start.3 = (f32[256]{0:T(256)S(1)}, f32[256]{0:T(256)}, u32[]{:S(2)}) copy-start(f32[256]{0:T(256)} %param.15) | copy-start | bytes 3076
  51.2 3.3 %copy-start.11 = (pred[8,9]{0,1:T(8,128)(4,1)S(1)}, pred[8,9]{0,1:T(8,128)(4,1)}, u32[]{:S(2)}) copy-start(pred[8,9]{0,1:T(8,128)(4,1)} %constant.83) | copy-start | bytes 220
  54.6 1.7 %copy-start.4 = (f32[256]{0:T(256)S(1)}, f32[256]{0:T(256)}, u32[]{:S(2)}) copy-start(f32[256]{0:T(256)} %param.17) | copy-start | bytes 3076
  56.0 0.9 copy-start.5
  56.2 8.9 %copy-start.9 = (f32[8]{0:T(128)S(1)}, f32[8]{0:T(128)}, u32[]{:S(2)}) copy-start(f32[8]{0:T(128)} %param.20) | copy-start | bytes 100
  57.9 16.8 %all-to-all-start = ((bf16[16,64,256]{2,1,0:T(8,128)(2,1)}), bf16[16,64,256]{2,1,0:T(8,128)(2,1)S(1)}, u32[]{:S(2)}, u32[]{:S(2)}) async-start(bf16[16,64,256]{2,1,0:T(8,128)(2,1)} %bitcast.11), calls=%async_computation | async-start | bytes 1048576 | tf_op jit(solution)/shard_map/all_to_all | solution.py:104
  88.2 11.7 %copy-start.2 = (bf16[256,256]{1,0:T(8,128)(2,1)S(1)}, bf16[256,256]{1,0:T(8,128)(2,1)}, u32[]{:S(2)}) copy-start(bf16[256,256]{1,0:T(8,128)(2,1)} %param.21) | copy-start | bytes 393220

commit v4 on v3

--- a/solution.py
+++ b/solution.py
@@ -1,6 +1,7 @@
 import jax
 import jax.numpy as jnp
 from jax import lax
+from jax.experimental import pallas as pl
 from jax.sharding import PartitionSpec as P
 
 HEADS = 8
@@ -34,6 +35,32 @@
     keep = (rows >= 0) & (rows < total)
     shape = (count,) + (1,) * (value.ndim - 1)
     return jnp.where(keep.reshape(shape), value, jnp.zeros_like(value))
+
+
+def attention_block(q_ref, k_ref, v_ref, o_ref):
+    scores = lax.dot_general(
+        q_ref[0], k_ref[0], (((1,), (1,)), ((), ())), preferred_element_type=jnp.float32
+    )
+    best = jnp.max(scores, axis=-1, keepdims=True)
+    weights = jnp.exp(scores - best)
+    total = jnp.sum(weights, axis=-1, keepdims=True)
+    summed = jnp.dot(weights.astype(jnp.bfloat16), v_ref[0], preferred_element_type=jnp.float32)
+    o_ref[0] = (summed / total).astype(o_ref.dtype)
+
+
+def attend(q, k, v, block=256):
+    heads, length, d = q.shape
+    return pl.pallas_call(
+        attention_block,
+        grid=(heads, length // block),
+        in_specs=[
+            pl.BlockSpec((1, block, d), lambda h, i: (h, i, 0)),
+            pl.BlockSpec((1, length, d), lambda h, i: (h, 0, 0)),
+            pl.BlockSpec((1, length, d), lambda h, i: (h, 0, 0)),
+        ],
+        out_specs=pl.BlockSpec((1, block, d), lambda h, i: (h, i, 0)),
+        out_shape=jax.ShapeDtypeStruct(q.shape, jnp.bfloat16),
+    )(q, k, v)
 
 
 def first_conv(extended, kernel, bias):
@@ -111,14 +138,7 @@
     k_items = projected[1].astype(jnp.bfloat16)
     v_items = projected[2].astype(jnp.bfloat16)
     per_device = heads_here
-    scores = jnp.einsum("isd,itd->ist", q_items, k_items, preferred_element_type=jnp.float32)
-    best = jnp.max(scores, axis=-1, keepdims=True)
-    weights = jnp.exp(scores - best)
-    total = jnp.sum(weights, axis=-1, keepdims=True)
-    summed = jnp.einsum(
-        "ist,itd->isd", weights.astype(jnp.bfloat16), v_items, preferred_element_type=jnp.float32
-    )
-    attended = (summed / total).astype(jnp.bfloat16)
+    attended = attend(q_items, k_items, v_items)
     attended = attended.reshape(per_device, sectors, tokens, per_group_channel_count)
     attended = jnp.transpose(attended, (1, 0, 2, 3))
     attended = lax.all_to_all(attended, "lon", 0, 0, tiled=True)

time: 102 us -> 111 us (1.088)
  Pallas kernels: 0 us -> 14.4 us
  matrix products: 24.9 us -> 18.1 us
  waiting for transfers between devices: 17.5 us -> 20.1 us
    pallas_call x0 -> x1, Pallas kernels: none -> 14.4 us  [attend(): pl.pallas_call(attention_block, grid=(heads, length // block), in_specs=[...]
    dot_general x1 -> x0, matrix products: 6.59 us -> none  [on_device(): jnp.einsum('ist,itd->isd', weights.astype(jnp.bfloat16), v_items, preferr...]
    ppermute x1, waiting for transfers between devices: 6.24 us -> 0.01 us  [extend_lat(): after = lax.ppermute(source[:width], 'lat', down)]
    conv_general_dilated x2, matrix products: 4.28 us -> 9.82 us  [halving_filter(): lax.conv_general_dilated(extended[None], kernel, (2, 2), 'VALID', dimensi...]
    sub x1 -> x0, matrix products: 5.51 us -> none  [on_device(): weights = jnp.exp(scores - best)]
    ppermute x1, waiting for transfers between devices: 0.01 us -> 5.03 us  [extend_lat(): before = lax.ppermute(source[length - width:], 'lat', up)]
    conv_general_dilated x7 -> x2, local copies, waits for them, and re-layouts: 10.4 us -> 6.91 us  [halving_filter(): lax.conv_general_dilated(extended[None], kernel, (2, 2), 'VALID', dimensi...]
    ppermute x1, starting transfers between devices: 4.81 us -> 7.21 us  [extend_lat(): before = lax.ppermute(source[length - width:], 'lat', up)]
  transfers between devices with their start and end apart: 5 -> 5, of which waited for: 3 -> 4; matrix products, arithmetic and copies ran while one was open for 6% -> 5% of each run, Pallas kernels for 0% -> 0%
where the time goes in v4:
time: 111 us; the launch traced here: 110 us
  local copies, waits for them, and re-layouts  21.9 us (20%)
  waiting for transfers between devices  20.1 us (18%)
  matrix products  18.1 us (16%)
  starting transfers between devices  16.2 us (15%)
  Pallas kernels  14.4 us (13%)
  blocking collectives  10.4 us (9%)
  other arithmetic  8.69 us (8%)
    pallas_call x1, Pallas kernels, attend(): pl.pallas_call(attention_block, grid=(heads, length // block), in_specs=[...  14.4 us
    all_to_all x1, blocking collectives, on_device(): attended = lax.all_to_all(attended, 'lon', 0, 0, tiled=True)  10.4 us
    conv_general_dilated x2, matrix products, halving_filter(): lax.conv_general_dilated(extended[None], kernel, (2, 2), 'VALID', dimensi...  9.82 us
    all_to_all x1, waiting for transfers between devices, on_device(): gathered = lax.all_to_all(row_copies, 'lon', 0, 0, tiled=True)  9.5 us
    unnamed x29, local copies, waits for them, and re-layouts  7.75 us
    ppermute x1, starting transfers between devices, extend_lat(): before = lax.ppermute(source[length - width:], 'lat', up)  7.21 us
    conv_general_dilated x2, local copies, waits for them, and re-layouts, halving_filter(): lax.conv_general_dilated(extended[None], kernel, (2, 2), 'VALID', dimensi...  6.91 us
    conv_general_dilated x1, matrix products, first_conv(): lax.conv_general_dilated(extended[None], kernel, (1, 1), 'VALID', dimensi...  6.18 us
  transfers between devices with their start and end apart: 5, of which 4 were waited for; matrix products, arithmetic and copies ran while one was open for 5% of the time, Pallas kernels for 0%

profile of v4, /device:TPU:112, one launch (start us, length us, event | category | flops | bytes accessed | tf_op | source)
XLA Modules:
  0.0 110.2 jit_solution(8338119878270525649)
XLA Ops:
  0.0 1.2 %fusion.41 = (bf16[4,96,256]{2,1,0:T(8,128)(2,1)S(1)}, bf16[4,96,256]{2,1,0:T(8,128)(2,1)S(1)}) fusion(bf16[32,96,256]{2,1,0:T(8,128)(2,1)} %param.11), kind=kLoop, calls=%fused_computation.61 | loop fusion | bytes 786432 | tf_op jit(solution)/shard_map/slice | solution.py:16
  1.2 0.2 copy.33
  1.4 2.2 %collective-permute-start.1 = (bf16[4,96,256]{1,0,2:T(4,128)(2,1)S(1)}, bf16[4,96,256]{1,0,2:T(4,128)(2,1)S(1)}, u32[]{:S(2)}, u32[]{:S(2)}) collective-permute-start(bf16[4,96,256]{1,0,2:T(4,128)(2,1)S(1)} %copy.33), channel_id=1, source_target_pairs={{16,0},{32,16},{48,32},{64,48},{80,64},{96,80},{112,96},{128,112},... | collective-permute-start | bytes 589832 | tf_op jit(solution)/shard_map/ppermute | solution.py:17
  3.6 0.2 copy.32
  3.8 7.2 %collective-permute-start = (bf16[4,96,256]{1,0,2:T(4,128)(2,1)S(1)}, bf16[4,96,256]{1,0,2:T(4,128)(2,1)S(1)}, u32[]{:S(2)}, u32[]{:S(2)}) collective-permute-start(bf16[4,96,256]{1,0,2:T(4,128)(2,1)S(1)} %copy.32), channel_id=1, source_target_pairs={{0,16},{16,32},{32,48},{48,64},{64,80},{80,96},{96,112},{112,128},... | collective-permute-start | bytes 589832 | tf_op jit(solution)/shard_map/ppermute | solution.py:16
  11.0 4.5 %copy.16 = bf16[32,96,256]{1,0,2:T(8,128)(2,1)} copy(bf16[32,96,256]{2,1,0:T(8,128)(2,1)} %param.11) | data formatting | bytes 3145728 | tf_op args[0]
  15.5 5.0 %collective-permute-done = bf16[4,96,256]{1,0,2:T(4,128)(2,1)S(1)} collective-permute-done((bf16[4,96,256]{1,0,2:T(4,128)(2,1)S(1)}, bf16[4,96,256]{1,0,2:T(4,128)(2,1)S(1)}, u32[]{:S(2)}, u32[]{:S(2)}) %collective-permute-start) | collective-permute-done | bytes 196640 | tf_op jit(solution)/shard_map/ppermute | solution.py:16
  20.6 0.8 pad_maximum_fusion.3
  21.4 3.2 %collective-permute-start.3 = (bf16[40,96,4]{1,0,2:T(8,128)(2,1)S(1)}, bf16[40,96,4]{1,0,2:T(8,128)(2,1)S(1)}, u32[]{:S(2)}, u32[]{:S(2)}) collective-permute-start(bf16[40,96,4]{1,0,2:T(8,128)(2,1)S(1)} %get-tuple-element.10), channel_id=1, source_target_pairs={{1,0},{2,1},{3,2},{4,3},{5,4},{6,5},{7,6},{8,7},{9,8},{10,9},{11,1... | collective-permute-start | bytes 92168 | tf_op jit(solution)/shard_map/ppermute | solution.py:28
  24.6 1.7 %collective-permute-done.3 = bf16[40,96,4]{1,0,2:T(8,128)(2,1)S(1)} collective-permute-done((bf16[40,96,4]{1,0,2:T(8,128)(2,1)S(1)}, bf16[40,96,4]{1,0,2:T(8,128)(2,1)S(1)}, u32[]{:S(2)}, u32[]{:S(2)}) %collective-permute-start.3) | collective-permute-done | bytes 30752 | tf_op jit(solution)/shard_map/ppermute | solution.py:28
  26.2 3.9 %collective-permute-done.2 = bf16[40,96,4]{1,0,2:T(8,128)(2,1)S(1)} collective-permute-done((bf16[40,96,4]{1,0,2:T(8,128)(2,1)S(1)}, bf16[40,96,4]{1,0,2:T(8,128)(2,1)S(1)}, u32[]{:S(2)}, u32[]{:S(2)}) %collective-permute-start.2) | collective-permute-done | bytes 30752 | tf_op jit(solution)/shard_map/ppermute | solution.py:27
  30.1 3.5 %pad_maximum_fusion = bf16[40,96,264]{1,0,2:T(8,128)(2,1)S(1)} fusion(bf16[40,96,4]{1,0,2:T(8,128)(2,1)S(1)} %collective-permute-done.3, bf16[4,96,256]{1,0,2:T(4,128)(2,1)S(1)} %collective-permute-done.1, bf16[32,96,256]{1,0,2:T(8,128)(2,1)S(1)} %copy-done.1, bf16[4,96,256]{1,0,2:T(4,128)(2,1)S(1)} %collective-permute-done, ...), kind=kLoop, calls=%fused_computation.17 | loop fusion | flops 10137600 | bytes 4055040 | tf_op jit(solution)/shard_map/concatenate | solution.py:29
  33.6 0.0 copy-start.7
  33.6 0.0 copy-start.8
  33.6 0.0 copy-start.10
  33.6 0.4 copy.18
  34.0 0.5 copy-done.7
  34.5 6.2 %select_select_fusion = bf16[38,8,33,128]{3,1,2,0:T(8,128)(2,1)S(1)} fusion(f32[128]{0:T(128)S(1)} %copy-done.8, pred[38]{0:T(512)(128)(4,1)S(1)} %compare_and_fusion, pred[8,33]{0,1:T(8,128)(4,1)S(1)} %copy-done.10, bf16[3,3,96,128]{3,2,1,0:T(8,128)(2,1)S(1)} %copy-done.7, bf16[40,96,1,7,2]{1,3,4,0,2:T(8,128)(2,1)S(1)} %slice.35, ...), kind=kOutput, calls=%fused_computation.19 | convolution fusion | flops 2236925952 | bytes 4925230 | tf_op jit(solution)/shard_map/conv_general_dilated | solution.py:67
  40.7 0.4 copy.19
  41.1 0.5 pad.1
  41.6 0.0 copy-start.6
  41.6 0.7 copy.21
  42.3 0.1 slice.36
  42.4 0.5 copy-done.6
  42.8 2.9 %fusion.4 = f32[18,8,17,256]{3,1,2,0:T(8,128)S(1)} fusion(bf16[4,4,128,256]{3,2,1,0:T(8,128)(2,1)S(1)} %copy-done.6, bf16[38,1,7,3,128]{4,2,3,0,1:T(8,128)(2,1)S(1)} %slice.36, bf16[38,1,8,34,128]{4,2,3,0,1:T(8,128)(2,1)S(1)} %copy.21), kind=kOutput, calls=%fused_computation.7 | convolution fusion | flops 2575552512 | bytes 6405632 | tf_op jit(solution)/shard_map/conv_general_dilated | solution.py:79
  45.7 2.7 %copy.22 = f32[18,8,17,256]{3,2,1,0:T(8,128)} copy(f32[18,8,17,256]{3,1,2,0:T(8,128)S(1)} %fusion.4) | data formatting | bytes 5013504 | tf_op jit(solution)/shard_map/conv_general_dilated | solution.py:79
  48.4 4.2 %reshape.72 = f32[18,1,136,256]{3,2,0,1:T(8,128)} reshape(f32[18,8,17,256]{3,2,1,0:T(8,128)} %copy.22) | data formatting | bytes 5013504 | tf_op jit(solution)/shard_map/conv_general_dilated | solution.py:79
  52.6 2.5 %fusion.25 = bf16[18,130,256]{2,1,0:T(8,128)(2,1)S(1)} fusion(f32[256]{0:T(256)S(1)} %copy-done.3, f32[18,1,136,256]{3,2,0,1:T(8,128)} %reshape.72, pred[18]{0:T(512)(128)(4,1)S(1)} %compare_and_fusion.1), kind=kLoop, calls=%fused_computation.30 | loop fusion | flops 4193280 | bytes 3595282 | tf_op jit(solution)/shard_map/jit(_where)/select_n | solution.py:37
  55.1 0.0 copy-start.4
  55.1 6.9 %fusion.17 = f32[1,8,64,256]{3,0,2,1:T(1,128)S(1)} fusion(bf16[4,4,256,256]{3,2,1,0:T(8,128)(2,1)S(1)} %copy-done, bf16[1,18,130,256]{3,2,1,0:T(8,128)(2,1)S(1)} %bitcast.69), kind=kOutput, calls=%fused_computation.23 | convolution fusion | flops 1073741824 | bytes 3819520 | tf_op jit(solution)/shard_map/conv_general_dilated | solution.py:79
  62.1 0.0 copy-start.9
  62.1 0.2 convert_reduce_fusion
  62.3 0.3 fusion.29
  62.6 0.2 fusion.31
  62.8 0.9 broadcast_in_dim.45
  63.7 3.6 %all-to-all-start = ((bf16[16,64,256]{2,1,0:T(8,128)(2,1)}), bf16[16,64,256]{2,1,0:T(8,128)(2,1)S(1)}, u32[]{:S(2)}, u32[]{:S(2)}) async-start(bf16[16,64,256]{2,1,0:T(8,128)(2,1)} %bitcast.8), calls=%async_computation | async-start | bytes 1048576 | tf_op jit(solution)/shard_map/all_to_all | solution.py:131
  67.3 1.2 %copy.24 = bf16[256,768]{0,1:T(8,128)(2,1)S(1)} copy(bf16[256,768]{1,0:T(8,128)(2,1)} %param.19) | data formatting | bytes 786432 | tf_op args[8]
  68.5 0.1 dynamic_slice.7
  68.6 9.5 %all-to-all-done = bf16[16,64,256]{2,1,0:T(8,128)(2,1)S(1)} async-done(((bf16[16,64,256]{2,1,0:T(8,128)(2,1)}), bf16[16,64,256]{2,1,0:T(8,128)(2,1)S(1)}, u32[]{:S(2)}, u32[]{:S(2)}) %all-to-all-start) | async-done | bytes 524320 | tf_op jit(solution)/shard_map/all_to_all | solution.py:131
  78.1 1.1 fusion.42
  79.1 1.5 %slice_bitcast_fusion.2 = (bf16[4,1024,32]{2,1,0:T(8,128)(2,1)}, bf16[4,1024,32]{2,1,0:T(8,128)(2,1)}) fusion(bf16[3,4,1024,32]{3,2,1,0:T(8,128)(2,1)S(1)} %get-tuple-element.13), kind=kLoop, calls=%fused_computation.33 | loop fusion | bytes 1048576 | tf_op jit(solution)/shard_map/convert_element_type | solution.py:139
  80.6 1.2 %fusion.20.q_ref = bf16[4,1024,32]{2,1,0:T(8,128)(2,1)} fusion(f32[3,4,1024,32]{3,2,1,0:T(8,128)S(1)} %get-tuple-element.14, f32[4]{0:T(128)S(1)} %dynamic_slice.7), kind=kLoop, calls=%fused_computation.27 | loop fusion | flops 262144 | bytes 786448 | tf_op jit(solution)/shard_map/convert_element_type | solution.py:137
  81.8 14.4 %shard_map.109 = bf16[4,1024,32]{2,1,0:T(8,128)(2,1)} custom-call(bf16[4,1024,32]{2,1,0:T(8,128)(2,1)} %fusion.20.q_ref, bf16[4,1024,32]{2,1,0:T(8,128)(2,1)} %get-tuple-element.8.k_ref, bf16[4,1024,32]{2,1,0:T(8,128)(2,1)} %get-tuple-element.7.v_ref), custom_call_target="tpu_custom_call" | custom-call | tf_op jit(solution)/shard_map/pallas_call | solution.py:53
  96.2 1.6 %copy.26 = bf16[4,16,64,32]{2,3,0,1:T(8,128)(2,1)S(1)} copy(bf16[4,16,64,32]{3,2,1,0:T(8,128)(2,1)} %bitcast.66) | data formatting | bytes 524288 | tf_op jit(solution)/shard_map/reshape | solution.py:142
  97.9 0.4 reshape.86
  98.3 10.4 %all_to_all.10 = bf16[16,2,4096]{2,1,0:T(2,128)(2,1)S(1)} all-to-all(bf16[16,2,4096]{2,1,0:T(2,128)(2,1)S(1)} %reshape.86), channel_id=1, replica_groups=mesh['lat'=16,'lon'=16] {'lon'}, dimensions={0} | all-to-all | bytes 524288 | tf_op jit(solution)/shard_map/all_to_all | solution.py:144
  108.8 0.3 reshape.87
  109.2 1.0 fusion.26
  (23 shorter events, 0.2 us)
Async XLA Ops:
  0.0 55.1 %copy-start = (bf16[4,4,256,256]{3,2,1,0:T(8,128)(2,1)S(1)}, bf16[4,4,256,256]{3,2,1,0:T(8,128)(2,1)}, u32[]{:S(2)}) copy-start(bf16[4,4,256,256]{3,2,1,0:T(8,128)(2,1)} %param.16) | copy-start | bytes 6291460
  1.4 14.1 %collective-permute-start.1 = (bf16[4,96,256]{1,0,2:T(4,128)(2,1)S(1)}, bf16[4,96,256]{1,0,2:T(4,128)(2,1)S(1)}, u32[]{:S(2)}, u32[]{:S(2)}) collective-permute-start(bf16[4,96,256]{1,0,2:T(4,128)(2,1)S(1)} %copy.33), channel_id=1, source_target_pairs={{16,0},{32,16},{48,32},{64,48},{80,64},{96,80},{112,96},{128,112},... | collective-permute-start | bytes 589832 | tf_op jit(solution)/shard_map/ppermute | solution.py:17
  3.8 16.7 %collective-permute-start = (bf16[4,96,256]{1,0,2:T(4,128)(2,1)S(1)}, bf16[4,96,256]{1,0,2:T(4,128)(2,1)S(1)}, u32[]{:S(2)}, u32[]{:S(2)}) collective-permute-start(bf16[4,96,256]{1,0,2:T(4,128)(2,1)S(1)} %copy.32), channel_id=1, source_target_pairs={{0,16},{16,32},{32,48},{48,64},{64,80},{80,96},{96,112},{112,128},... | collective-permute-start | bytes 589832 | tf_op jit(solution)/shard_map/ppermute | solution.py:16
  15.5 14.6 %copy-start.1 = (bf16[32,96,256]{1,0,2:T(8,128)(2,1)S(1)}, bf16[32,96,256]{1,0,2:T(8,128)(2,1)}, u32[]{:S(2)}) copy-start(bf16[32,96,256]{1,0,2:T(8,128)(2,1)} %copy.16) | copy-start | bytes 4718596
  21.4 4.8 %collective-permute-start.3 = (bf16[40,96,4]{1,0,2:T(8,128)(2,1)S(1)}, bf16[40,96,4]{1,0,2:T(8,128)(2,1)S(1)}, u32[]{:S(2)}, u32[]{:S(2)}) collective-permute-start(bf16[40,96,4]{1,0,2:T(8,128)(2,1)S(1)} %get-tuple-element.10), channel_id=1, source_target_pairs={{1,0},{2,1},{3,2},{4,3},{5,4},{6,5},{7,6},{8,7},{9,8},{10,9},{11,1... | collective-permute-start | bytes 92168 | tf_op jit(solution)/shard_map/ppermute | solution.py:28
  24.6 5.5 %collective-permute-start.2 = (bf16[40,96,4]{1,0,2:T(8,128)(2,1)S(1)}, bf16[40,96,4]{1,0,2:T(8,128)(2,1)S(1)}, u32[]{:S(2)}, u32[]{:S(2)}) collective-permute-start(bf16[40,96,4]{1,0,2:T(8,128)(2,1)S(1)} %get-tuple-element.9), channel_id=1, source_target_pairs={{0,1},{1,2},{2,3},{3,4},{4,5},{5,6},{6,7},{7,8},{8,9},{9,10},{10,1... | collective-permute-start | bytes 92168 | tf_op jit(solution)/shard_map/ppermute | solution.py:27
  33.6 0.9 copy-start.7
  33.6 0.9 copy-start.8
  33.6 0.9 copy-start.10
  41.6 1.2 %copy-start.6 = (bf16[4,4,128,256]{3,2,1,0:T(8,128)(2,1)S(1)}, bf16[4,4,128,256]{3,2,1,0:T(8,128)(2,1)}, u32[]{:S(2)}) copy-start(bf16[4,4,128,256]{3,2,1,0:T(8,128)(2,1)} %param.14) | copy-start | bytes 3145732
  48.4 4.2 %copy-start.3 = (f32[256]{0:T(256)S(1)}, f32[256]{0:T(256)}, u32[]{:S(2)}) copy-start(f32[256]{0:T(256)} %param.15) | copy-start | bytes 3076
  55.1 7.0 %copy-start.4 = (f32[256]{0:T(256)S(1)}, f32[256]{0:T(256)}, u32[]{:S(2)}) copy-start(f32[256]{0:T(256)} %param.17) | copy-start | bytes 3076
  55.1 7.5 %copy-start.5 = (f32[256]{0:T(256)S(1)}, f32[256]{0:T(256)}, u32[]{:S(2)}) copy-start(f32[256]{0:T(256)} %param.18) | copy-start | bytes 3076
  62.1 6.4 %copy-start.9 = (f32[8]{0:T(128)S(1)}, f32[8]{0:T(128)}, u32[]{:S(2)}) copy-start(f32[8]{0:T(128)} %param.20) | copy-start | bytes 100
  63.7 14.4 %all-to-all-start = ((bf16[16,64,256]{2,1,0:T(8,128)(2,1)}), bf16[16,64,256]{2,1,0:T(8,128)(2,1)S(1)}, u32[]{:S(2)}, u32[]{:S(2)}) async-start(bf16[16,64,256]{2,1,0:T(8,128)(2,1)} %bitcast.8), calls=%async_computation | async-start | bytes 1048576 | tf_op jit(solution)/shard_map/all_to_all | solution.py:131
  96.2 12.9 %copy-start.2 = (bf16[256,256]{1,0:T(8,128)(2,1)S(1)}, bf16[256,256]{1,0:T(8,128)(2,1)}, u32[]{:S(2)}) copy-start(bf16[256,256]{1,0:T(8,128)(2,1)} %param.21) | copy-start | bytes 393220

commit v5 on v4

--- a/solution.py
+++ b/solution.py
@@ -39,18 +39,21 @@
 
 def attention_block(q_ref, k_ref, v_ref, o_ref):
     scores = lax.dot_general(
-        q_ref[0], k_ref[0], (((1,), (1,)), ((), ())), preferred_element_type=jnp.float32
+        k_ref[0], q_ref[0], (((1,), (1,)), ((), ())), preferred_element_type=jnp.float32
     )
-    best = jnp.max(scores, axis=-1, keepdims=True)
+    best = jnp.max(scores, axis=0, keepdims=True)
     weights = jnp.exp(scores - best)
-    total = jnp.sum(weights, axis=-1, keepdims=True)
-    summed = jnp.dot(weights.astype(jnp.bfloat16), v_ref[0], preferred_element_type=jnp.float32)
+    total = jnp.sum(weights, axis=0, keepdims=True)
+    summed = lax.dot_general(
+        v_ref[0], weights.astype(jnp.bfloat16), (((0,), (0,)), ((), ())),
+        preferred_element_type=jnp.float32,
+    )
     o_ref[0] = (summed / total).astype(o_ref.dtype)
 
 
 def attend(q, k, v, block=256):
     heads, length, d = q.shape
-    return pl.pallas_call(
+    out = pl.pallas_call(
         attention_block,
         grid=(heads, length // block),
         in_specs=[
@@ -58,9 +61,10 @@
             pl.BlockSpec((1, length, d), lambda h, i: (h, 0, 0)),
             pl.BlockSpec((1, length, d), lambda h, i: (h, 0, 0)),
         ],
-        out_specs=pl.BlockSpec((1, block, d), lambda h, i: (h, i, 0)),
-        out_shape=jax.ShapeDtypeStruct(q.shape, jnp.bfloat16),
+        out_specs=pl.BlockSpec((1, d, block), lambda h, i: (h, 0, i)),
+        out_shape=jax.ShapeDtypeStruct((heads, d, length), jnp.bfloat16),
     )(q, k, v)
+    return jnp.transpose(out, (0, 2, 1))
 
 
 def first_conv(extended, kernel, bias):

time: 111 us -> 112 us (level)
    unnamed x29 -> x28, local copies, waits for them, and re-layouts: 7.75 us -> 7.71 us
where the time goes in v5:
time: 112 us; the launch traced here: 110 us
  local copies, waits for them, and re-layouts  21.8 us (19%)
  waiting for transfers between devices  20.1 us (18%)
  matrix products  18.1 us (16%)
  starting transfers between devices  16.2 us (14%)
  Pallas kernels  14.7 us (13%)
  blocking collectives  10.4 us (9%)
  other arithmetic  8.69 us (8%)
    pallas_call x1, Pallas kernels, attend(): pl.pallas_call(attention_block, grid=(heads, length // block), in_specs=[...  14.7 us
    all_to_all x1, blocking collectives, on_device(): attended = lax.all_to_all(attended, 'lon', 0, 0, tiled=True)  10.4 us
    conv_general_dilated x2, matrix products, halving_filter(): lax.conv_general_dilated(extended[None], kernel, (2, 2), 'VALID', dimensi...  9.82 us
    all_to_all x1, waiting for transfers between devices, on_device(): gathered = lax.all_to_all(row_copies, 'lon', 0, 0, tiled=True)  9.5 us
    unnamed x28, local copies, waits for them, and re-layouts  7.71 us
    ppermute x1, starting transfers between devices, extend_lat(): before = lax.ppermute(source[length - width:], 'lat', up)  7.21 us
    conv_general_dilated x2, local copies, waits for them, and re-layouts, halving_filter(): lax.conv_general_dilated(extended[None], kernel, (2, 2), 'VALID', dimensi...  6.91 us
    conv_general_dilated x1, matrix products, first_conv(): lax.conv_general_dilated(extended[None], kernel, (1, 1), 'VALID', dimensi...  6.18 us
  transfers between devices with their start and end apart: 5, of which 4 were waited for; matrix products, arithmetic and copies ran while one was open for 5% of the time, Pallas kernels for 0%

profile of v5, /device:TPU:112, one launch (start us, length us, event | category | flops | bytes accessed | tf_op | source)
XLA Modules:
  0.0 110.3 jit_solution(5185888673474205218)
XLA Ops:
  0.0 1.2 %fusion.41 = (bf16[4,96,256]{2,1,0:T(8,128)(2,1)S(1)}, bf16[4,96,256]{2,1,0:T(8,128)(2,1)S(1)}) fusion(bf16[32,96,256]{2,1,0:T(8,128)(2,1)} %param.11), kind=kLoop, calls=%fused_computation.62 | loop fusion | bytes 786432 | tf_op jit(solution)/shard_map/slice | solution.py:16
  1.2 0.2 copy.33
  1.4 2.2 %collective-permute-start.1 = (bf16[4,96,256]{1,0,2:T(4,128)(2,1)S(1)}, bf16[4,96,256]{1,0,2:T(4,128)(2,1)S(1)}, u32[]{:S(2)}, u32[]{:S(2)}) collective-permute-start(bf16[4,96,256]{1,0,2:T(4,128)(2,1)S(1)} %copy.33), channel_id=1, source_target_pairs={{16,0},{32,16},{48,32},{64,48},{80,64},{96,80},{112,96},{128,112},... | collective-permute-start | bytes 589832 | tf_op jit(solution)/shard_map/ppermute | solution.py:17
  3.6 0.2 copy.32
  3.8 7.2 %collective-permute-start = (bf16[4,96,256]{1,0,2:T(4,128)(2,1)S(1)}, bf16[4,96,256]{1,0,2:T(4,128)(2,1)S(1)}, u32[]{:S(2)}, u32[]{:S(2)}) collective-permute-start(bf16[4,96,256]{1,0,2:T(4,128)(2,1)S(1)} %copy.32), channel_id=1, source_target_pairs={{0,16},{16,32},{32,48},{48,64},{64,80},{80,96},{96,112},{112,128},... | collective-permute-start | bytes 589832 | tf_op jit(solution)/shard_map/ppermute | solution.py:16
  11.0 4.5 %copy.16 = bf16[32,96,256]{1,0,2:T(8,128)(2,1)} copy(bf16[32,96,256]{2,1,0:T(8,128)(2,1)} %param.11) | data formatting | bytes 3145728 | tf_op args[0]
  15.5 5.0 %collective-permute-done = bf16[4,96,256]{1,0,2:T(4,128)(2,1)S(1)} collective-permute-done((bf16[4,96,256]{1,0,2:T(4,128)(2,1)S(1)}, bf16[4,96,256]{1,0,2:T(4,128)(2,1)S(1)}, u32[]{:S(2)}, u32[]{:S(2)}) %collective-permute-start) | collective-permute-done | bytes 196640 | tf_op jit(solution)/shard_map/ppermute | solution.py:16
  20.6 0.8 pad_maximum_fusion.3
  21.4 3.2 %collective-permute-start.3 = (bf16[40,96,4]{1,0,2:T(8,128)(2,1)S(1)}, bf16[40,96,4]{1,0,2:T(8,128)(2,1)S(1)}, u32[]{:S(2)}, u32[]{:S(2)}) collective-permute-start(bf16[40,96,4]{1,0,2:T(8,128)(2,1)S(1)} %get-tuple-element.10), channel_id=1, source_target_pairs={{1,0},{2,1},{3,2},{4,3},{5,4},{6,5},{7,6},{8,7},{9,8},{10,9},{11,1... | collective-permute-start | bytes 92168 | tf_op jit(solution)/shard_map/ppermute | solution.py:28
  24.6 1.7 %collective-permute-done.3 = bf16[40,96,4]{1,0,2:T(8,128)(2,1)S(1)} collective-permute-done((bf16[40,96,4]{1,0,2:T(8,128)(2,1)S(1)}, bf16[40,96,4]{1,0,2:T(8,128)(2,1)S(1)}, u32[]{:S(2)}, u32[]{:S(2)}) %collective-permute-start.3) | collective-permute-done | bytes 30752 | tf_op jit(solution)/shard_map/ppermute | solution.py:28
  26.2 3.9 %collective-permute-done.2 = bf16[40,96,4]{1,0,2:T(8,128)(2,1)S(1)} collective-permute-done((bf16[40,96,4]{1,0,2:T(8,128)(2,1)S(1)}, bf16[40,96,4]{1,0,2:T(8,128)(2,1)S(1)}, u32[]{:S(2)}, u32[]{:S(2)}) %collective-permute-start.2) | collective-permute-done | bytes 30752 | tf_op jit(solution)/shard_map/ppermute | solution.py:27
  30.1 3.5 %pad_maximum_fusion = bf16[40,96,264]{1,0,2:T(8,128)(2,1)S(1)} fusion(bf16[40,96,4]{1,0,2:T(8,128)(2,1)S(1)} %collective-permute-done.3, bf16[4,96,256]{1,0,2:T(4,128)(2,1)S(1)} %collective-permute-done.1, bf16[32,96,256]{1,0,2:T(8,128)(2,1)S(1)} %copy-done.1, bf16[4,96,256]{1,0,2:T(4,128)(2,1)S(1)} %collective-permute-done, ...), kind=kLoop, calls=%fused_computation.17 | loop fusion | flops 10137600 | bytes 4055040 | tf_op jit(solution)/shard_map/concatenate | solution.py:29
  33.6 0.0 copy-start.7
  33.6 0.0 copy-start.10
  33.6 0.4 copy.18
  34.0 0.5 copy-done.7
  34.5 6.2 %select_select_fusion = bf16[38,8,33,128]{3,1,2,0:T(8,128)(2,1)S(1)} fusion(f32[128]{0:T(128)S(1)} %copy-done.8, pred[38]{0:T(512)(128)(4,1)S(1)} %compare_and_fusion, pred[8,33]{0,1:T(8,128)(4,1)S(1)} %copy-done.10, bf16[3,3,96,128]{3,2,1,0:T(8,128)(2,1)S(1)} %copy-done.7, bf16[40,96,1,7,2]{1,3,4,0,2:T(8,128)(2,1)S(1)} %slice.35, ...), kind=kOutput, calls=%fused_computation.19 | convolution fusion | flops 2236925952 | bytes 4925230 | tf_op jit(solution)/shard_map/conv_general_dilated | solution.py:71
  40.7 0.4 copy.19
  41.1 0.5 pad.1
  41.6 0.0 copy-start.6
  41.6 0.7 copy.21
  42.3 0.1 slice.36
  42.4 0.5 copy-done.6
  42.8 2.9 %fusion.4 = f32[18,8,17,256]{3,1,2,0:T(8,128)S(1)} fusion(bf16[4,4,128,256]{3,2,1,0:T(8,128)(2,1)S(1)} %copy-done.6, bf16[38,1,7,3,128]{4,2,3,0,1:T(8,128)(2,1)S(1)} %slice.36, bf16[38,1,8,34,128]{4,2,3,0,1:T(8,128)(2,1)S(1)} %copy.21), kind=kOutput, calls=%fused_computation.7 | convolution fusion | flops 2575552512 | bytes 6405632 | tf_op jit(solution)/shard_map/conv_general_dilated | solution.py:83
  45.7 2.7 %copy.22 = f32[18,8,17,256]{3,2,1,0:T(8,128)} copy(f32[18,8,17,256]{3,1,2,0:T(8,128)S(1)} %fusion.4) | data formatting | bytes 5013504 | tf_op jit(solution)/shard_map/conv_general_dilated | solution.py:83
  48.4 4.2 %reshape.72 = f32[18,1,136,256]{3,2,0,1:T(8,128)} reshape(f32[18,8,17,256]{3,2,1,0:T(8,128)} %copy.22) | data formatting | bytes 5013504 | tf_op jit(solution)/shard_map/conv_general_dilated | solution.py:83
  52.6 2.5 %fusion.25 = bf16[18,130,256]{2,1,0:T(8,128)(2,1)S(1)} fusion(f32[256]{0:T(256)S(1)} %copy-done.3, f32[18,1,136,256]{3,2,0,1:T(8,128)} %reshape.72, pred[18]{0:T(512)(128)(4,1)S(1)} %compare_and_fusion.1), kind=kLoop, calls=%fused_computation.30 | loop fusion | flops 4193280 | bytes 3595282 | tf_op jit(solution)/shard_map/jit(_where)/select_n | solution.py:37
  55.1 0.0 copy-start.4
  55.1 6.9 %fusion.17 = f32[1,8,64,256]{3,0,2,1:T(1,128)S(1)} fusion(bf16[4,4,256,256]{3,2,1,0:T(8,128)(2,1)S(1)} %copy-done, bf16[1,18,130,256]{3,2,1,0:T(8,128)(2,1)S(1)} %bitcast.75), kind=kOutput, calls=%fused_computation.23 | convolution fusion | flops 1073741824 | bytes 3819520 | tf_op jit(solution)/shard_map/conv_general_dilated | solution.py:83
  62.1 0.0 copy-start.9
  62.1 0.2 convert_reduce_fusion
  62.3 0.3 fusion.29
  62.6 0.2 fusion.31
  62.8 0.9 broadcast_in_dim.45
  63.7 3.6 %all-to-all-start = ((bf16[16,64,256]{2,1,0:T(8,128)(2,1)}), bf16[16,64,256]{2,1,0:T(8,128)(2,1)S(1)}, u32[]{:S(2)}, u32[]{:S(2)}) async-start(bf16[16,64,256]{2,1,0:T(8,128)(2,1)} %bitcast.8), calls=%async_computation | async-start | bytes 1048576 | tf_op jit(solution)/shard_map/all_to_all | solution.py:135
  67.3 1.2 %copy.24 = bf16[256,768]{0,1:T(8,128)(2,1)S(1)} copy(bf16[256,768]{1,0:T(8,128)(2,1)} %param.19) | data formatting | bytes 786432 | tf_op args[8]
  68.5 0.1 dynamic_slice.7
  68.6 9.5 %all-to-all-done = bf16[16,64,256]{2,1,0:T(8,128)(2,1)S(1)} async-done(((bf16[16,64,256]{2,1,0:T(8,128)(2,1)}), bf16[16,64,256]{2,1,0:T(8,128)(2,1)S(1)}, u32[]{:S(2)}, u32[]{:S(2)}) %all-to-all-start) | async-done | bytes 524320 | tf_op jit(solution)/shard_map/all_to_all | solution.py:135
  78.1 1.1 fusion.42
  79.1 1.5 %slice_bitcast_fusion.2 = (bf16[4,1024,32]{2,1,0:T(8,128)(2,1)}, bf16[4,1024,32]{2,1,0:T(8,128)(2,1)}) fusion(bf16[3,4,1024,32]{3,2,1,0:T(8,128)(2,1)S(1)} %get-tuple-element.13), kind=kLoop, calls=%fused_computation.33 | loop fusion | bytes 1048576 | tf_op jit(solution)/shard_map/convert_element_type | solution.py:143
  80.6 1.2 %fusion.20.q_ref = bf16[4,1024,32]{2,1,0:T(8,128)(2,1)} fusion(f32[3,4,1024,32]{3,2,1,0:T(8,128)S(1)} %get-tuple-element.14, f32[4]{0:T(128)S(1)} %dynamic_slice.7), kind=kLoop, calls=%fused_computation.27 | loop fusion | flops 262144 | bytes 786448 | tf_op jit(solution)/shard_map/convert_element_type | solution.py:141
  81.8 14.7 %shard_map.109 = bf16[4,32,1024]{2,1,0:T(8,128)(2,1)} custom-call(bf16[4,1024,32]{2,1,0:T(8,128)(2,1)} %fusion.20.q_ref, bf16[4,1024,32]{2,1,0:T(8,128)(2,1)} %get-tuple-element.8.k_ref, bf16[4,1024,32]{2,1,0:T(8,128)(2,1)} %get-tuple-element.7.v_ref), custom_call_target="tpu_custom_call" | custom-call | tf_op jit(solution)/shard_map/pallas_call | solution.py:56
  96.6 1.4 %reshape.56 = bf16[4,16,64,32]{2,1,3,0:T(8,128)(2,1)S(1)} reshape(bf16[4,1024,32]{1,2,0:T(8,128)(2,1)} %bitcast.76) | data formatting | bytes 524288 | tf_op jit(solution)/shard_map/reshape | solution.py:146
  97.9 0.1 copy.43
  98.1 0.4 reshape.86
  98.5 10.4 %all_to_all.10 = bf16[16,2,4096]{2,1,0:T(2,128)(2,1)S(1)} all-to-all(bf16[16,2,4096]{2,1,0:T(2,128)(2,1)S(1)} %reshape.86), channel_id=1, replica_groups=mesh['lat'=16,'lon'=16] {'lon'}, dimensions={0} | all-to-all | bytes 524288 | tf_op jit(solution)/shard_map/all_to_all | solution.py:148
  108.9 0.3 reshape.87
  109.3 1.0 fusion.26
  (23 shorter events, 0.1 us)
Async XLA Ops:
  0.0 55.1 %copy-start = (bf16[4,4,256,256]{3,2,1,0:T(8,128)(2,1)S(1)}, bf16[4,4,256,256]{3,2,1,0:T(8,128)(2,1)}, u32[]{:S(2)}) copy-start(bf16[4,4,256,256]{3,2,1,0:T(8,128)(2,1)} %param.16) | copy-start | bytes 6291460
  1.4 14.1 %collective-permute-start.1 = (bf16[4,96,256]{1,0,2:T(4,128)(2,1)S(1)}, bf16[4,96,256]{1,0,2:T(4,128)(2,1)S(1)}, u32[]{:S(2)}, u32[]{:S(2)}) collective-permute-start(bf16[4,96,256]{1,0,2:T(4,128)(2,1)S(1)} %copy.33), channel_id=1, source_target_pairs={{16,0},{32,16},{48,32},{64,48},{80,64},{96,80},{112,96},{128,112},... | collective-permute-start | bytes 589832 | tf_op jit(solution)/shard_map/ppermute | solution.py:17
  3.8 16.7 %collective-permute-start = (bf16[4,96,256]{1,0,2:T(4,128)(2,1)S(1)}, bf16[4,96,256]{1,0,2:T(4,128)(2,1)S(1)}, u32[]{:S(2)}, u32[]{:S(2)}) collective-permute-start(bf16[4,96,256]{1,0,2:T(4,128)(2,1)S(1)} %copy.32), channel_id=1, source_target_pairs={{0,16},{16,32},{32,48},{48,64},{64,80},{80,96},{96,112},{112,128},... | collective-permute-start | bytes 589832 | tf_op jit(solution)/shard_map/ppermute | solution.py:16
  15.5 14.6 %copy-start.1 = (bf16[32,96,256]{1,0,2:T(8,128)(2,1)S(1)}, bf16[32,96,256]{1,0,2:T(8,128)(2,1)}, u32[]{:S(2)}) copy-start(bf16[32,96,256]{1,0,2:T(8,128)(2,1)} %copy.16) | copy-start | bytes 4718596
  21.4 4.8 %collective-permute-start.3 = (bf16[40,96,4]{1,0,2:T(8,128)(2,1)S(1)}, bf16[40,96,4]{1,0,2:T(8,128)(2,1)S(1)}, u32[]{:S(2)}, u32[]{:S(2)}) collective-permute-start(bf16[40,96,4]{1,0,2:T(8,128)(2,1)S(1)} %get-tuple-element.10), channel_id=1, source_target_pairs={{1,0},{2,1},{3,2},{4,3},{5,4},{6,5},{7,6},{8,7},{9,8},{10,9},{11,1... | collective-permute-start | bytes 92168 | tf_op jit(solution)/shard_map/ppermute | solution.py:28
  24.6 5.5 %collective-permute-start.2 = (bf16[40,96,4]{1,0,2:T(8,128)(2,1)S(1)}, bf16[40,96,4]{1,0,2:T(8,128)(2,1)S(1)}, u32[]{:S(2)}, u32[]{:S(2)}) collective-permute-start(bf16[40,96,4]{1,0,2:T(8,128)(2,1)S(1)} %get-tuple-element.9), channel_id=1, source_target_pairs={{0,1},{1,2},{2,3},{3,4},{4,5},{5,6},{6,7},{7,8},{8,9},{9,10},{10,1... | collective-permute-start | bytes 92168 | tf_op jit(solution)/shard_map/ppermute | solution.py:27
  33.6 0.9 copy-start.7
  33.6 0.9 copy-start.8
  33.6 0.9 copy-start.10
  41.6 1.2 %copy-start.6 = (bf16[4,4,128,256]{3,2,1,0:T(8,128)(2,1)S(1)}, bf16[4,4,128,256]{3,2,1,0:T(8,128)(2,1)}, u32[]{:S(2)}) copy-start(bf16[4,4,128,256]{3,2,1,0:T(8,128)(2,1)} %param.14) | copy-start | bytes 3145732
  48.4 4.2 %copy-start.3 = (f32[256]{0:T(256)S(1)}, f32[256]{0:T(256)}, u32[]{:S(2)}) copy-start(f32[256]{0:T(256)} %param.15) | copy-start | bytes 3076
  55.1 7.0 %copy-start.4 = (f32[256]{0:T(256)S(1)}, f32[256]{0:T(256)}, u32[]{:S(2)}) copy-start(f32[256]{0:T(256)} %param.17) | copy-start | bytes 3076
  55.1 7.5 %copy-start.5 = (f32[256]{0:T(256)S(1)}, f32[256]{0:T(256)}, u32[]{:S(2)}) copy-start(f32[256]{0:T(256)} %param.18) | copy-start | bytes 3076
  62.1 6.4 %copy-start.9 = (f32[8]{0:T(128)S(1)}, f32[8]{0:T(128)}, u32[]{:S(2)}) copy-start(f32[8]{0:T(128)} %param.20) | copy-start | bytes 100
  63.7 14.4 %all-to-all-start = ((bf16[16,64,256]{2,1,0:T(8,128)(2,1)}), bf16[16,64,256]{2,1,0:T(8,128)(2,1)S(1)}, u32[]{:S(2)}, u32[]{:S(2)}) async-start(bf16[16,64,256]{2,1,0:T(8,128)(2,1)} %bitcast.8), calls=%async_computation | async-start | bytes 1048576 | tf_op jit(solution)/shard_map/all_to_all | solution.py:135
  96.6 12.7 %copy-start.2 = (bf16[256,256]{1,0:T(8,128)(2,1)S(1)}, bf16[256,256]{1,0:T(8,128)(2,1)}, u32[]{:S(2)}) copy-start(bf16[256,256]{1,0:T(8,128)(2,1)} %param.21) | copy-start | bytes 393220

commit v6 on v3

--- a/solution.py
+++ b/solution.py
@@ -81,8 +81,13 @@
     opening_halved = first_conv(extended, smoothing_filter_taps, smoothing_offset_entries)
     opening_halved = clear_outside(opening_halved, base - HALO + 1, lat_total)
     closing_halved = halving_filter(opening_halved, opening_coarsen_taps, opening_coarsen_offset)
-    closing_halved = clear_outside(closing_halved, base // 2 - 1, lat_total // 2)
-    closing_halved = lax.optimization_barrier(closing_halved)
+    count = closing_halved.shape[0]
+    first_row = base // 2 - 1
+    keep_top = (first_row >= 0).astype(closing_halved.dtype)
+    keep_bottom = (first_row + count - 1 < lat_total // 2).astype(closing_halved.dtype)
+    closing_halved = jnp.concatenate(
+        [closing_halved[:1] * keep_top, closing_halved[1:-1], closing_halved[-1:] * keep_bottom], axis=0
+    )
     activation_maps = halving_filter(
         closing_halved, closing_coarsen_taps, closing_coarsen_offset
     )

time: 102 us -> 105 us (1.029)
  waiting for transfers between devices: 17.5 us -> 20.1 us
  other arithmetic: 7.65 us -> 8.97 us
    ppermute x1, waiting for transfers between devices: 6.24 us -> 0.01 us  [extend_lat(): after = lax.ppermute(source[:width], 'lat', down)]
    ppermute x1, waiting for transfers between devices: 0.01 us -> 5.05 us  [extend_lat(): before = lax.ppermute(source[length - width:], 'lat', up)]
    select_n x1 -> x0, other arithmetic: 2.46 us -> none  [clear_outside(): return jnp.where(keep.reshape(shape), value, jnp.zeros_like(value))]
    ppermute x1, starting transfers between devices: 4.81 us -> 7.21 us  [extend_lat(): before = lax.ppermute(source[length - width:], 'lat', up)]
    all_to_all x1, starting transfers between devices: 5.95 us -> 3.57 us  [on_device(): gathered = lax.all_to_all(row_copies, 'lon', 0, 0, tiled=True)]
    convert_element_type x0 -> x1, other arithmetic: none -> 2.36 us  [halving_filter(): return jax.nn.silu(total + bias).astype(jnp.bfloat16)]
    ppermute x1, waiting for transfers between devices: 1.67 us -> 3.86 us  [extend_lon(): before = lax.ppermute(last, 'lon', up)]
    ppermute x1, waiting for transfers between devices: 0.01 us -> 1.63 us  [extend_lon(): after = lax.ppermute(initial, 'lon', down)]
  transfers between devices with their start and end apart: 5 -> 5, of which waited for: 3 -> 4; matrix products, arithmetic and copies ran while one was open for 6% -> 6% of each run, Pallas kernels for 0% -> 0%
where the time goes in v6:
time: 105 us; the launch traced here: 104 us
  matrix products  24.9 us (24%)
  local copies, waits for them, and re-layouts  22.9 us (22%)
  waiting for transfers between devices  20.1 us (19%)
  starting transfers between devices  16.2 us (15%)
  blocking collectives  10.4 us (10%)
  other arithmetic  8.97 us (9%)
    all_to_all x1, blocking collectives, on_device(): attended = lax.all_to_all(attended, 'lon', 0, 0, tiled=True)  10.4 us
    conv_general_dilated x7, local copies, waits for them, and re-layouts, halving_filter(): lax.conv_general_dilated(extended[None], kernel, (2, 2), 'VALID', dimensi...  10.4 us
    all_to_all x1, waiting for transfers between devices, on_device(): gathered = lax.all_to_all(row_copies, 'lon', 0, 0, tiled=True)  9.5 us
    unnamed x28, local copies, waits for them, and re-layouts  7.72 us
    ppermute x1, starting transfers between devices, extend_lat(): before = lax.ppermute(source[length - width:], 'lat', up)  7.21 us
    dot_general x1, matrix products, on_device(): jnp.einsum('ist,itd->isd', weights.astype(jnp.bfloat16), v_items, preferr...  6.59 us
    conv_general_dilated x1, matrix products, first_conv(): lax.conv_general_dilated(extended[None], kernel, (1, 1), 'VALID', dimensi...  6.17 us
    sub x1, matrix products, on_device(): weights = jnp.exp(scores - best)  5.51 us
  transfers between devices with their start and end apart: 5, of which 4 were waited for; matrix products, arithmetic and copies ran while one was open for 6% of the time, Pallas kernels for 0%

profile of v6, /device:TPU:112, one launch (start us, length us, event | category | flops | bytes accessed | tf_op | source)
XLA Modules:
  0.0 103.9 jit_solution(10442307607589773791)
XLA Ops:
  0.0 1.2 %fusion.76 = (bf16[4,96,256]{2,1,0:T(8,128)(2,1)S(1)}, bf16[4,96,256]{2,1,0:T(8,128)(2,1)S(1)}) fusion(bf16[32,96,256]{2,1,0:T(8,128)(2,1)} %param.11), kind=kLoop, calls=%fused_computation.85 | loop fusion | bytes 786432 | tf_op jit(solution)/shard_map/slice | solution.py:15
  1.2 0.2 copy.35
  1.4 2.2 %collective-permute-start.1 = (bf16[4,96,256]{1,0,2:T(4,128)(2,1)S(1)}, bf16[4,96,256]{1,0,2:T(4,128)(2,1)S(1)}, u32[]{:S(2)}, u32[]{:S(2)}) collective-permute-start(bf16[4,96,256]{1,0,2:T(4,128)(2,1)S(1)} %copy.35), channel_id=1, source_target_pairs={{16,0},{32,16},{48,32},{64,48},{80,64},{96,80},{112,96},{128,112},... | collective-permute-start | bytes 589832 | tf_op jit(solution)/shard_map/ppermute | solution.py:16
  3.6 0.2 copy.34
  3.8 7.2 %collective-permute-start = (bf16[4,96,256]{1,0,2:T(4,128)(2,1)S(1)}, bf16[4,96,256]{1,0,2:T(4,128)(2,1)S(1)}, u32[]{:S(2)}, u32[]{:S(2)}) collective-permute-start(bf16[4,96,256]{1,0,2:T(4,128)(2,1)S(1)} %copy.34), channel_id=1, source_target_pairs={{0,16},{16,32},{32,48},{48,64},{64,80},{80,96},{96,112},{112,128},... | collective-permute-start | bytes 589832 | tf_op jit(solution)/shard_map/ppermute | solution.py:15
  11.0 4.5 %copy.16 = bf16[32,96,256]{1,0,2:T(8,128)(2,1)} copy(bf16[32,96,256]{2,1,0:T(8,128)(2,1)} %param.11) | data formatting | bytes 3145728 | tf_op args[0]
  15.5 5.1 %collective-permute-done = bf16[4,96,256]{1,0,2:T(4,128)(2,1)S(1)} collective-permute-done((bf16[4,96,256]{1,0,2:T(4,128)(2,1)S(1)}, bf16[4,96,256]{1,0,2:T(4,128)(2,1)S(1)}, u32[]{:S(2)}, u32[]{:S(2)}) %collective-permute-start) | collective-permute-done | bytes 196640 | tf_op jit(solution)/shard_map/ppermute | solution.py:15
  20.6 0.8 pad_maximum_fusion.3
  21.4 3.2 %collective-permute-start.3 = (bf16[40,96,4]{1,0,2:T(8,128)(2,1)S(1)}, bf16[40,96,4]{1,0,2:T(8,128)(2,1)S(1)}, u32[]{:S(2)}, u32[]{:S(2)}) collective-permute-start(bf16[40,96,4]{1,0,2:T(8,128)(2,1)S(1)} %get-tuple-element.8), channel_id=1, source_target_pairs={{1,0},{2,1},{3,2},{4,3},{5,4},{6,5},{7,6},{8,7},{9,8},{10,9},{11,1... | collective-permute-start | bytes 92168 | tf_op jit(solution)/shard_map/ppermute | solution.py:27
  24.6 1.6 %collective-permute-done.3 = bf16[40,96,4]{1,0,2:T(8,128)(2,1)S(1)} collective-permute-done((bf16[40,96,4]{1,0,2:T(8,128)(2,1)S(1)}, bf16[40,96,4]{1,0,2:T(8,128)(2,1)S(1)}, u32[]{:S(2)}, u32[]{:S(2)}) %collective-permute-start.3) | collective-permute-done | bytes 30752 | tf_op jit(solution)/shard_map/ppermute | solution.py:27
  26.2 3.9 %collective-permute-done.2 = bf16[40,96,4]{1,0,2:T(8,128)(2,1)S(1)} collective-permute-done((bf16[40,96,4]{1,0,2:T(8,128)(2,1)S(1)}, bf16[40,96,4]{1,0,2:T(8,128)(2,1)S(1)}, u32[]{:S(2)}, u32[]{:S(2)}) %collective-permute-start.2) | collective-permute-done | bytes 30752 | tf_op jit(solution)/shard_map/ppermute | solution.py:26
  30.1 4.7 %pad_maximum_fusion = bf16[40,96,264]{1,0,2:T(8,128)(2,1)S(1)} fusion(bf16[40,96,4]{1,0,2:T(8,128)(2,1)S(1)} %collective-permute-done.3, bf16[4,96,256]{1,0,2:T(4,128)(2,1)S(1)} %collective-permute-done.1, bf16[32,96,256]{1,0,2:T(8,128)(2,1)} %copy.16, bf16[4,96,256]{1,0,2:T(4,128)(2,1)S(1)} %collective-permute-done, ...), kind=kLoop, calls=%fused_computation.23 | loop fusion | flops 10137600 | bytes 4055040 | tf_op jit(solution)/shard_map/concatenate | solution.py:28
  34.9 0.4 copy.18
  35.3 0.5 copy-done.6
  35.8 6.2 %select_select_fusion = bf16[38,8,33,128]{3,1,2,0:T(8,128)(2,1)S(1)} fusion(f32[128]{0:T(128)S(1)} %copy-done.7, pred[38]{0:T(512)(128)(4,1)S(1)} %compare_and_fusion, pred[8,33]{0,1:T(8,128)(4,1)S(1)} %copy-done.9, bf16[3,3,96,128]{3,2,1,0:T(8,128)(2,1)S(1)} %copy-done.6, bf16[40,96,1,7,2]{1,3,4,0,2:T(8,128)(2,1)S(1)} %slice.49, ...), kind=kOutput, calls=%fused_computation.24 | convolution fusion | flops 2236925952 | bytes 4925230 | tf_op jit(solution)/shard_map/conv_general_dilated | solution.py:40
  41.9 0.4 copy.19
  42.3 0.5 pad.1
  42.8 0.7 copy.21
  43.6 0.5 copy-done.5
  44.1 2.9 %fusion.8 = f32[18,8,17,256]{3,1,2,0:T(8,128)S(1)} fusion(bf16[4,4,128,256]{3,2,1,0:T(8,128)(2,1)S(1)} %copy-done.5, bf16[38,1,7,3,128]{4,2,3,0,1:T(8,128)(2,1)S(1)} %slice.50, bf16[38,1,8,34,128]{4,2,3,0,1:T(8,128)(2,1)S(1)} %copy.21), kind=kOutput, calls=%fused_computation.13 | convolution fusion | flops 2575552512 | bytes 6405632 | tf_op jit(solution)/shard_map/conv_general_dilated | solution.py:52
  47.0 2.7 %copy.22 = f32[18,8,17,256]{3,2,1,0:T(8,128)} copy(f32[18,8,17,256]{3,1,2,0:T(8,128)S(1)} %fusion.8) | data formatting | bytes 5013504 | tf_op jit(solution)/shard_map/conv_general_dilated | solution.py:52
  49.7 4.2 %reshape.66 = f32[18,1,136,256]{3,2,0,1:T(8,128)} reshape(f32[18,8,17,256]{3,2,1,0:T(8,128)} %copy.22) | data formatting | bytes 5013504 | tf_op jit(solution)/shard_map/conv_general_dilated | solution.py:52
  53.9 2.4 %multiply_convert_fusion.1 = bf16[18,130,256]{2,1,0:T(8,128)(2,1)S(1)} fusion(f32[18,1,136,256]{3,2,0,1:T(8,128)} %reshape.66, f32[256]{0:T(256)S(1)} %copy-done.4), kind=kLoop, calls=%fused_computation.27 | loop fusion | flops 3594240 | bytes 3595264 | tf_op jit(solution)/shard_map/convert_element_type | solution.py:60
  56.3 0.1 slice.53
  56.4 0.2 maximum_bitcast_fusion
  56.5 0.1 pad.3
  56.7 1.4 %reshape.69 = bf16[18,1,8,18,256]{4,3,2,0,1:T(8,128)(2,1)} reshape(bf16[18,1,144,256]{3,2,0,1:T(8,128)(2,1)S(1)} %pad.3) | data formatting | bytes 2654208 | tf_op jit(solution)/shard_map/conv_general_dilated | solution.py:52
  58.1 1.8 %copy.24 = bf16[18,1,8,18,256]{4,2,3,0,1:T(8,128)(2,1)S(1)} copy(bf16[18,1,8,18,256]{4,3,2,0,1:T(8,128)(2,1)} %reshape.69) | data formatting | bytes 2654208 | tf_op jit(solution)/shard_map/conv_general_dilated | solution.py:52
  60.0 1.4 %fusion.38 = f32[8,8,9,256]{3,1,2,0:T(8,128)S(1)} fusion(bf16[4,4,256,256]{3,2,1,0:T(8,128)(2,1)S(1)} %copy-done, bf16[18,1,7,3,256]{4,2,3,0,1:T(8,128)(2,1)S(1)} %slice.55, bf16[18,1,8,18,256]{4,2,3,0,1:T(8,128)(2,1)S(1)} %copy.24, pred[8,9]{0,1:T(8,128)(4,1)S(1)} %copy-done.10), kind=kOutput, calls=%fused_computation.40 | convolution fusion | flops 1212751872 | bytes 4207688 | tf_op jit(solution)/shard_map/conv_general_dilated | solution.py:52
  61.4 0.2 copy.25
  61.6 0.3 convert_reduce_fusion
  61.9 0.3 fusion.55
  62.2 0.2 fusion.57
  62.5 0.8 broadcast_in_dim.34
  63.3 3.6 %all-to-all-start = ((bf16[16,64,256]{2,1,0:T(8,128)(2,1)}), bf16[16,64,256]{2,1,0:T(8,128)(2,1)S(1)}, u32[]{:S(2)}, u32[]{:S(2)}) async-start(bf16[16,64,256]{2,1,0:T(8,128)(2,1)} %bitcast.11), calls=%async_computation | async-start | bytes 1048576 | tf_op jit(solution)/shard_map/all_to_all | solution.py:109
  66.9 1.2 %copy.27 = bf16[256,768]{0,1:T(8,128)(2,1)S(1)} copy(bf16[256,768]{1,0:T(8,128)(2,1)} %param.19) | data formatting | bytes 786432 | tf_op args[8]
  68.1 0.1 dynamic_slice.7
  68.2 9.5 %all-to-all-done = bf16[16,64,256]{2,1,0:T(8,128)(2,1)S(1)} async-done(((bf16[16,64,256]{2,1,0:T(8,128)(2,1)}), bf16[16,64,256]{2,1,0:T(8,128)(2,1)S(1)}, u32[]{:S(2)}, u32[]{:S(2)}) %all-to-all-start) | async-done | bytes 524320 | tf_op jit(solution)/shard_map/all_to_all | solution.py:109
  77.7 1.3 %fusion.77 = (bf16[3,4,1024,32]{2,3,1,0:T(8,128)(2,1)}, f32[3,4,1024,32]{2,3,1,0:T(8,128)S(1)}) fusion(bf16[1024,256,1,1]{1,0,3,2:T(8,128)(2,1)S(1)} %bitcast.96, bf16[256,3,8,32]{0,3,2,1:T(8,128)(2,1)S(1)} %bitcast.99, s32[]{:T(128)S(6)} %select_n.23), kind=kOutput, calls=%fused_computation.86 | convolution fusion | flops 201719808 | bytes 3080196 | tf_op jit(solution)/shard_map/tc,cjhd->jhtd/dot_general | solution.py:113
  79.0 0.1 fusion.59
  79.1 5.5 %fusion.78 = f32[4,1024]{1,0:T(4,128)S(1)} fusion(bf16[4,1024,32]{1,2,0:T(8,128)(2,1)S(1)} %fusion.59, bf16[3,4,1024,32]{2,3,1,0:T(8,128)(2,1)} %get-tuple-element.13), kind=kOutput, calls=%fused_computation.87 | convolution fusion | flops 276825088 | bytes 540672 | tf_op jit(solution)/shard_map/sub | solution.py:121
  84.6 6.6 %fusion.47 = bf16[4,1024,32]{1,2,0:T(8,128)(2,1)S(1)} fusion(bf16[4,1024,32]{1,2,0:T(8,128)(2,1)S(1)} %fusion.59, bf16[3,4,1024,32]{2,3,1,0:T(8,128)(2,1)} %get-tuple-element.13, f32[4,1024]{1,0:T(4,128)S(1)} %fusion.78), kind=kOutput, calls=%fused_computation.43 | convolution fusion | flops 545526784 | bytes 1064960 | tf_op jit(solution)/shard_map/ist,itd->isd/dot_general | solution.py:123
  91.2 0.3 reshape.50
  91.5 0.1 copy.46
  91.7 0.4 reshape.94
  92.1 10.4 %all_to_all.10 = bf16[16,2,4096]{2,1,0:T(2,128)(2,1)S(1)} all-to-all(bf16[16,2,4096]{2,1,0:T(2,128)(2,1)S(1)} %reshape.94), channel_id=1, replica_groups=mesh['lat'=16,'lon'=16] {'lon'}, dimensions={0} | all-to-all | bytes 524288 | tf_op jit(solution)/shard_map/all_to_all | solution.py:129
  102.5 0.3 reshape.95
  102.9 1.0 fusion.41
  (31 shorter events, 0.3 us)
Async XLA Ops:
  0.0 59.9 %copy-start = (bf16[4,4,256,256]{3,2,1,0:T(8,128)(2,1)S(1)}, bf16[4,4,256,256]{3,2,1,0:T(8,128)(2,1)}, u32[]{:S(2)}) copy-start(bf16[4,4,256,256]{3,2,1,0:T(8,128)(2,1)} %param.16) | copy-start | bytes 6291460
  1.4 14.1 %collective-permute-start.1 = (bf16[4,96,256]{1,0,2:T(4,128)(2,1)S(1)}, bf16[4,96,256]{1,0,2:T(4,128)(2,1)S(1)}, u32[]{:S(2)}, u32[]{:S(2)}) collective-permute-start(bf16[4,96,256]{1,0,2:T(4,128)(2,1)S(1)} %copy.35), channel_id=1, source_target_pairs={{16,0},{32,16},{48,32},{64,48},{80,64},{96,80},{112,96},{128,112},... | collective-permute-start | bytes 589832 | tf_op jit(solution)/shard_map/ppermute | solution.py:16
  3.8 16.7 %collective-permute-start = (bf16[4,96,256]{1,0,2:T(4,128)(2,1)S(1)}, bf16[4,96,256]{1,0,2:T(4,128)(2,1)S(1)}, u32[]{:S(2)}, u32[]{:S(2)}) collective-permute-start(bf16[4,96,256]{1,0,2:T(4,128)(2,1)S(1)} %copy.34), channel_id=1, source_target_pairs={{0,16},{16,32},{32,48},{48,64},{64,80},{80,96},{96,112},{112,128},... | collective-permute-start | bytes 589832 | tf_op jit(solution)/shard_map/ppermute | solution.py:15
  21.4 4.8 %collective-permute-start.3 = (bf16[40,96,4]{1,0,2:T(8,128)(2,1)S(1)}, bf16[40,96,4]{1,0,2:T(8,128)(2,1)S(1)}, u32[]{:S(2)}, u32[]{:S(2)}) collective-permute-start(bf16[40,96,4]{1,0,2:T(8,128)(2,1)S(1)} %get-tuple-element.8), channel_id=1, source_target_pairs={{1,0},{2,1},{3,2},{4,3},{5,4},{6,5},{7,6},{8,7},{9,8},{10,9},{11,1... | collective-permute-start | bytes 92168 | tf_op jit(solution)/shard_map/ppermute | solution.py:27
  24.6 5.5 %collective-permute-start.2 = (bf16[40,96,4]{1,0,2:T(8,128)(2,1)S(1)}, bf16[40,96,4]{1,0,2:T(8,128)(2,1)S(1)}, u32[]{:S(2)}, u32[]{:S(2)}) collective-permute-start(bf16[40,96,4]{1,0,2:T(8,128)(2,1)S(1)} %get-tuple-element.7), channel_id=1, source_target_pairs={{0,1},{1,2},{2,3},{3,4},{4,5},{5,6},{6,7},{7,8},{8,9},{9,10},{10,1... | collective-permute-start | bytes 92168 | tf_op jit(solution)/shard_map/ppermute | solution.py:26
  34.8 0.9 copy-start.6
  34.8 0.9 copy-start.7
  34.8 0.9 copy-start.9
  42.8 1.2 %copy-start.5 = (bf16[4,4,128,256]{3,2,1,0:T(8,128)(2,1)S(1)}, bf16[4,4,128,256]{3,2,1,0:T(8,128)(2,1)}, u32[]{:S(2)}) copy-start(bf16[4,4,128,256]{3,2,1,0:T(8,128)(2,1)} %param.14) | copy-start | bytes 3145732
  49.7 4.2 %copy-start.4 = (f32[256]{0:T(256)S(1)}, f32[256]{0:T(256)}, u32[]{:S(2)}) copy-start(f32[256]{0:T(256)} %param.15) | copy-start | bytes 3076
  56.6 3.3 %copy-start.10 = (pred[8,9]{0,1:T(8,128)(4,1)S(1)}, pred[8,9]{0,1:T(8,128)(4,1)}, u32[]{:S(2)}) copy-start(pred[8,9]{0,1:T(8,128)(4,1)} %constant.86) | copy-start | bytes 220
  60.0 1.7 %copy-start.2 = (f32[256]{0:T(256)S(1)}, f32[256]{0:T(256)}, u32[]{:S(2)}) copy-start(f32[256]{0:T(256)} %param.17) | copy-start | bytes 3076
  61.4 0.9 copy-start.3
  61.6 6.5 %copy-start.8 = (f32[8]{0:T(128)S(1)}, f32[8]{0:T(128)}, u32[]{:S(2)}) copy-start(f32[8]{0:T(128)} %param.20) | copy-start | bytes 100
  63.3 14.4 %all-to-all-start = ((bf16[16,64,256]{2,1,0:T(8,128)(2,1)}), bf16[16,64,256]{2,1,0:T(8,128)(2,1)S(1)}, u32[]{:S(2)}, u32[]{:S(2)}) async-start(bf16[16,64,256]{2,1,0:T(8,128)(2,1)} %bitcast.11), calls=%async_computation | async-start | bytes 1048576 | tf_op jit(solution)/shard_map/all_to_all | solution.py:109
  91.2 11.7 %copy-start.1 = (bf16[256,256]{1,0:T(8,128)(2,1)S(1)}, bf16[256,256]{1,0:T(8,128)(2,1)}, u32[]{:S(2)}) copy-start(bf16[256,256]{1,0:T(8,128)(2,1)} %param.21) | copy-start | bytes 393220

commit v7 on v3

--- a/solution.py
+++ b/solution.py
@@ -76,9 +76,18 @@
     band = meridian_slab_data.shape[0]
     lat_total = band * lax.axis_size("lat")
     base = lax.axis_index("lat") * band
-    extended = extend_lat(meridian_slab_data, HALO)
-    extended = extend_lon(extended, HALO, 2)
-    opening_halved = first_conv(extended, smoothing_filter_taps, smoothing_offset_entries)
+    n_lat, n_lon = lax.axis_size("lat"), lax.axis_size("lon")
+    width = meridian_slab_data.shape[2]
+    source = lax.optimization_barrier(meridian_slab_data)
+    left = lax.ppermute(source[:, :, width - HALO :], "lon", [(i, (i + 1) % n_lon) for i in range(n_lon)])
+    right = lax.ppermute(source[:, :, :HALO], "lon", [((i + 1) % n_lon, i) for i in range(n_lon)])
+    wide = jnp.concatenate([left, meridian_slab_data, right], axis=2)
+    top = lax.ppermute(wide[band - HALO :], "lat", [(i, i + 1) for i in range(n_lat - 1)])
+    bottom = lax.ppermute(wide[:HALO], "lat", [(i + 1, i) for i in range(n_lat - 1)])
+    middle = first_conv(wide, smoothing_filter_taps, smoothing_offset_entries)
+    upper = first_conv(jnp.concatenate([top, wide[:2]], axis=0), smoothing_filter_taps, smoothing_offset_entries)
+    lower = first_conv(jnp.concatenate([wide[band - 2 :], bottom], axis=0), smoothing_filter_taps, smoothing_offset_entries)
+    opening_halved = jnp.concatenate([upper, middle, lower], axis=0)
     opening_halved = clear_outside(opening_halved, base - HALO + 1, lat_total)
     closing_halved = halving_filter(opening_halved, opening_coarsen_taps, opening_coarsen_offset)
     closing_halved = clear_outside(closing_halved, base // 2 - 1, lat_total // 2)

time: 102 us -> 101 us (level)
  waiting for transfers between devices: 17.5 us -> 12 us
  local copies, waits for them, and re-layouts: 22.9 us -> 27.1 us
    ppermute x4, waiting for transfers between devices: 7.92 us -> 2.44 us  [the longest x1 2.43 us: on_device(): lax.ppermute(wide[:HALO], 'lat', [(i + 1, i) for i in range(n_lat - 1)])]
    slice x1 -> x3, local copies, waits for them, and re-layouts: 1.2 us -> 3.13 us  [the longest x1 2.7 us: on_device(): source[:, :, width - HALO:]]
    select_n x1 -> x2, other arithmetic: 2.46 us -> 4.08 us  [clear_outside(): return jnp.where(keep.reshape(shape), value, jnp.zeros_like(value))]
    convert_element_type x0 -> x6, local copies, waits for them, and re-layouts: none -> 1.15 us  [first_conv(): return jax.nn.silu(total + bias).astype(jnp.bfloat16)]
    select_n x4 -> x1, local copies, waits for them, and re-layouts: 1.62 us -> 0.48 us  [clear_outside(): return jnp.where(keep.reshape(shape), value, jnp.zeros_like(value))]
    conv_general_dilated x7 -> x9, local copies, waits for them, and re-layouts: 10.4 us -> 11.2 us  [halving_filter(): lax.conv_general_dilated(extended[None], kernel, (2, 2), 'VALID', dimensi...]
    concatenate x1 -> x2, other arithmetic: 3.48 us -> 2.79 us  [the longest x1 2.08 us: on_device(): wide = jnp.concatenate([left, meridian_slab_data, right], axis=2)]
    conv_general_dilated x1 -> x3, matrix products: 6.18 us -> 6.59 us  [first_conv(): lax.conv_general_dilated(extended[None], kernel, (1, 1), 'VALID', dimensi...]
  transfers between devices with their start and end apart: 5 -> 5, of which waited for: 3 -> 2; matrix products, arithmetic and copies ran while one was open for 6% -> 13% of each run, Pallas kernels for 0% -> 0%
where the time goes in v7:
time: 101 us; the launch traced here: 99.7 us
  local copies, waits for them, and re-layouts  27.1 us (27%)
  matrix products  25.3 us (25%)
  starting transfers between devices  16.6 us (16%)
  waiting for transfers between devices  12 us (12%)
  blocking collectives  10.4 us (10%)
  other arithmetic  7.76 us (8%)
    conv_general_dilated x9, local copies, waits for them, and re-layouts, halving_filter(): lax.conv_general_dilated(extended[None], kernel, (2, 2), 'VALID', dimensi...  11.2 us
    all_to_all x1, blocking collectives, on_device(): attended = lax.all_to_all(attended, 'lon', 0, 0, tiled=True)  10.4 us
    all_to_all x1, waiting for transfers between devices, on_device(): gathered = lax.all_to_all(row_copies, 'lon', 0, 0, tiled=True)  9.54 us
    unnamed x30, local copies, waits for them, and re-layouts  8.66 us
    conv_general_dilated x3, matrix products, first_conv(): lax.conv_general_dilated(extended[None], kernel, (1, 1), 'VALID', dimensi...  6.59 us
    dot_general x1, matrix products, on_device(): jnp.einsum('ist,itd->isd', weights.astype(jnp.bfloat16), v_items, preferr...  6.58 us
    sub x1, matrix products, on_device(): weights = jnp.exp(scores - best)  5.52 us
    all_to_all x1, starting transfers between devices, on_device(): gathered = lax.all_to_all(row_copies, 'lon', 0, 0, tiled=True)  5.17 us
  transfers between devices with their start and end apart: 5, of which 2 were waited for; matrix products, arithmetic and copies ran while one was open for 13% of the time, Pallas kernels for 0%

profile of v7, /device:TPU:112, one launch (start us, length us, event | category | flops | bytes accessed | tf_op | source)
XLA Modules:
  0.0 99.7 jit_solution(18203717532315291271)
XLA Ops:
  0.0 2.7 %fusion.107 = (bf16[32,96,4]{2,1,0:T(8,128)(2,1)}, bf16[32,96,4]{2,1,0:T(8,128)(2,1)S(1)}) fusion(bf16[32,96,256]{2,1,0:T(8,128)(2,1)} %param.11), kind=kLoop, calls=%fused_computation.117 | loop fusion | bytes 98304 | tf_op jit(solution)/shard_map/slice | solution.py:82
  2.7 1.5 %copy.48 = bf16[32,96,4]{1,0,2:T(8,128)(2,1)S(1)} copy(bf16[32,96,4]{2,1,0:T(8,128)(2,1)} %get-tuple-element.11) | data formatting | bytes 49152
  4.3 0.3 copy.49
  4.6 3.9 %collective-permute-start.1 = (bf16[32,96,4]{1,0,2:T(8,128)(2,1)S(1)}, bf16[32,96,4]{1,0,2:T(8,128)(2,1)S(1)}, u32[]{:S(2)}, u32[]{:S(2)}) collective-permute-start(bf16[32,96,4]{1,0,2:T(8,128)(2,1)S(1)} %copy.49), channel_id=1, source_target_pairs={{1,0},{2,1},{3,2},{4,3},{5,4},{6,5},{7,6},{8,7},{9,8},{10,9},{11,1... | collective-permute-start | bytes 73736 | tf_op jit(solution)/shard_map/ppermute | solution.py:83
  8.5 4.4 %copy.16 = bf16[32,96,256]{1,0,2:T(8,128)(2,1)} copy(bf16[32,96,256]{2,1,0:T(8,128)(2,1)} %param.11) | data formatting | bytes 3145728 | tf_op args[0]
  13.0 2.1 %pad_maximum_fusion = bf16[32,96,264]{1,0,2:T(8,128)(2,1)S(1)} fusion(bf16[32,96,4]{1,0,2:T(8,128)(2,1)S(1)} %collective-permute-done.1, bf16[32,96,256]{1,0,2:T(8,128)(2,1)} %copy.16, bf16[32,96,4]{1,0,2:T(8,128)(2,1)S(1)} %collective-permute-done), kind=kLoop, calls=%fused_computation.28 | loop fusion | flops 1622016 | bytes 3244032 | tf_op jit(solution)/shard_map/concatenate | solution.py:84
  15.1 0.2 fusion.105
  15.3 4.9 %collective-permute-start.2 = (bf16[4,96,264]{1,0,2:T(4,128)(2,1)S(1)}, bf16[4,96,264]{1,0,2:T(4,128)(2,1)S(1)}, u32[]{:S(2)}, u32[]{:S(2)}) collective-permute-start(bf16[4,96,264]{1,0,2:T(4,128)(2,1)S(1)} %get-tuple-element.7), channel_id=1, source_target_pairs={{0,16},{16,32},{32,48},{48,64},{64,80},{80,96},{96,112},{112,128},... | collective-permute-start | bytes 608264 | tf_op jit(solution)/shard_map/ppermute | solution.py:85
  20.3 2.5 %collective-permute-start.3 = (bf16[4,96,264]{1,0,2:T(4,128)(2,1)S(1)}, bf16[4,96,264]{1,0,2:T(4,128)(2,1)S(1)}, u32[]{:S(2)}, u32[]{:S(2)}) collective-permute-start(bf16[4,96,264]{1,0,2:T(4,128)(2,1)S(1)} %get-tuple-element.8), channel_id=1, source_target_pairs={{16,0},{32,16},{48,32},{64,48},{80,64},{96,80},{112,96},{128,112},... | collective-permute-start | bytes 608264 | tf_op jit(solution)/shard_map/ppermute | solution.py:86
  22.8 0.8 copy.22
  23.7 5.1 %multiply_convert_fusion = bf16[30,8,33,128]{3,1,2,0:T(8,128)(2,1)S(1)} fusion(f32[128]{0:T(128)S(1)} %copy-done.7, pred[8,33]{0,1:T(8,128)(4,1)S(1)} %copy-done.9, bf16[3,3,96,128]{3,2,1,0:T(8,128)(2,1)S(1)} %copy-done.6, bf16[32,96,1,7,2]{1,3,4,0,2:T(8,128)(2,1)S(1)} %slice.54, bf16[32,96,1,8,33]{1,3,4,0,2:T(8,128)(2,1)S(1)} %copy.22), kind=kOutput, calls=%fused_computation.8 | convolution fusion | flops 1764034560 | bytes 3957512 | tf_op jit(solution)/shard_map/conv_general_dilated | solution.py:40
  28.8 0.4 copy.23
  29.2 0.4 slice_bitcast_fusion.1
  29.6 0.2 fusion.106
  29.8 2.4 %collective-permute-done.3 = bf16[4,96,264]{1,0,2:T(4,128)(2,1)S(1)} collective-permute-done((bf16[4,96,264]{1,0,2:T(4,128)(2,1)S(1)}, bf16[4,96,264]{1,0,2:T(4,128)(2,1)S(1)}, u32[]{:S(2)}, u32[]{:S(2)}) %collective-permute-start.3) | collective-permute-done | bytes 202784 | tf_op jit(solution)/shard_map/ppermute | solution.py:86
  32.2 0.7 pad_maximum_fusion.1
  33.0 0.8 multiply_convert_fusion.3
  33.8 0.1 copy.20
  34.1 0.8 multiply_convert_fusion.2
  34.9 0.1 copy.27
  35.1 1.6 %fusion.13 = bf16[38,1,262,128]{3,0,2,1:T(8,128)(2,1)S(1)} fusion(bf16[1,4,262,128]{3,1,2,0:T(4,128)(2,1)S(1)} %slice_bitcast_fusion.3, bf16[1,30,262,128]{3,1,2,0:T(8,128)(2,1)S(1)} %slice_bitcast_fusion.1, bf16[1,4,262,128]{3,1,2,0:T(4,128)(2,1)S(1)} %slice_bitcast_fusion.4, pred[38]{0:T(512)(128)(4,1)S(1)} %compare_and_fusion), kind=kLoop, calls=%fused_computation.18 | loop fusion | flops 8920576 | bytes 5097510 | tf_op jit(solution)/shard_map/jit(_where)/select_n | solution.py:36
  36.7 0.5 pad.3
  37.2 0.7 copy.29
  38.0 0.4 copy-done.5
  38.4 2.9 %fusion.24 = f32[18,8,17,256]{3,1,2,0:T(8,128)S(1)} fusion(bf16[4,4,128,256]{3,2,1,0:T(8,128)(2,1)S(1)} %copy-done.5, bf16[38,1,7,3,128]{4,2,3,0,1:T(8,128)(2,1)S(1)} %slice.60, bf16[38,1,8,34,128]{4,2,3,0,1:T(8,128)(2,1)S(1)} %copy.29, pred[8,17]{0,1:T(8,128)(4,1)S(1)} %copy-done.10), kind=kOutput, calls=%fused_computation.31 | convolution fusion | flops 2576179200 | bytes 6405768 | tf_op jit(solution)/shard_map/conv_general_dilated | solution.py:52
  41.3 2.7 %copy.30 = f32[18,8,17,256]{3,2,1,0:T(8,128)} copy(f32[18,8,17,256]{3,1,2,0:T(8,128)S(1)} %fusion.24) | data formatting | bytes 5013504 | tf_op jit(solution)/shard_map/conv_general_dilated | solution.py:52
  44.0 4.2 %reshape.115 = f32[18,1,136,256]{3,2,0,1:T(8,128)} reshape(f32[18,8,17,256]{3,2,1,0:T(8,128)} %copy.30) | data formatting | bytes 5013504 | tf_op jit(solution)/shard_map/conv_general_dilated | solution.py:52
  48.3 2.5 %fusion.39 = bf16[18,130,256]{2,1,0:T(8,128)(2,1)S(1)} fusion(f32[256]{0:T(256)S(1)} %copy-done.2, f32[18,1,136,256]{3,2,0,1:T(8,128)} %reshape.115, pred[18]{0:T(512)(128)(4,1)S(1)} %compare_and_fusion.1), kind=kLoop, calls=%fused_computation.40 | loop fusion | flops 4193280 | bytes 3595282 | tf_op jit(solution)/shard_map/jit(_where)/select_n | solution.py:36
  50.8 1.4 %reshape.118 = bf16[18,1,8,18,256]{4,3,2,0,1:T(8,128)(2,1)} reshape(bf16[18,1,144,256]{3,2,0,1:T(8,128)(2,1)S(1)} %pad.5) | data formatting | bytes 2654208 | tf_op jit(solution)/shard_map/conv_general_dilated | solution.py:52
  52.3 1.8 %copy.32 = bf16[18,1,8,18,256]{4,2,3,0,1:T(8,128)(2,1)S(1)} copy(bf16[18,1,8,18,256]{4,3,2,0,1:T(8,128)(2,1)} %reshape.118) | data formatting | bytes 2654208 | tf_op jit(solution)/shard_map/conv_general_dilated | solution.py:52
  54.2 1.4 %fusion.42 = f32[8,8,9,256]{3,1,2,0:T(8,128)S(1)} fusion(bf16[4,4,256,256]{3,2,1,0:T(8,128)(2,1)S(1)} %copy-done, bf16[18,1,7,3,256]{4,2,3,0,1:T(8,128)(2,1)S(1)} %slice.62, bf16[18,1,8,18,256]{4,2,3,0,1:T(8,128)(2,1)S(1)} %copy.32, pred[8,9]{0,1:T(8,128)(4,1)S(1)} %copy-done.11), kind=kOutput, calls=%fused_computation.46 | convolution fusion | flops 1212751872 | bytes 4207688 | tf_op jit(solution)/shard_map/conv_general_dilated | solution.py:52
  55.6 0.2 copy.33
  55.8 0.3 convert_reduce_fusion
  56.1 0.3 fusion.64
  56.4 0.2 fusion.66
  56.6 0.9 broadcast_in_dim.57
  57.5 5.2 %all-to-all-start = ((bf16[16,64,256]{2,1,0:T(8,128)(2,1)}), bf16[16,64,256]{2,1,0:T(8,128)(2,1)S(1)}, u32[]{:S(2)}, u32[]{:S(2)}) async-start(bf16[16,64,256]{2,1,0:T(8,128)(2,1)} %bitcast.21), calls=%async_computation | async-start | bytes 1048576 | tf_op jit(solution)/shard_map/all_to_all | solution.py:113
  62.7 1.2 %copy.35 = bf16[256,768]{0,1:T(8,128)(2,1)S(1)} copy(bf16[256,768]{1,0:T(8,128)(2,1)} %param.19) | data formatting | bytes 786432 | tf_op args[8]
  64.0 9.5 %all-to-all-done = bf16[16,64,256]{2,1,0:T(8,128)(2,1)S(1)} async-done(((bf16[16,64,256]{2,1,0:T(8,128)(2,1)}), bf16[16,64,256]{2,1,0:T(8,128)(2,1)S(1)}, u32[]{:S(2)}, u32[]{:S(2)}) %all-to-all-start) | async-done | bytes 524320 | tf_op jit(solution)/shard_map/all_to_all | solution.py:113
  73.5 1.3 %fusion.108 = (bf16[3,4,1024,32]{2,3,1,0:T(8,128)(2,1)}, f32[3,4,1024,32]{2,3,1,0:T(8,128)S(1)}) fusion(bf16[1024,256,1,1]{1,0,3,2:T(8,128)(2,1)S(1)} %bitcast.122, bf16[256,3,8,32]{0,3,2,1:T(8,128)(2,1)S(1)} %bitcast.127, s32[]{:T(128)S(6)} %select_n.34), kind=kOutput, calls=%fused_computation.118 | convolution fusion | flops 201719808 | bytes 3080196 | tf_op jit(solution)/shard_map/tc,cjhd->jhtd/dot_general | solution.py:117
  74.9 5.5 %fusion.109 = f32[4,1024]{1,0:T(4,128)S(1)} fusion(bf16[4,1024,32]{1,2,0:T(8,128)(2,1)S(1)} %fusion.68, bf16[3,4,1024,32]{2,3,1,0:T(8,128)(2,1)} %get-tuple-element.13), kind=kOutput, calls=%fused_computation.119 | convolution fusion | flops 276825088 | bytes 540672 | tf_op jit(solution)/shard_map/sub | solution.py:125
  80.4 6.6 %fusion.54 = bf16[4,1024,32]{1,2,0:T(8,128)(2,1)S(1)} fusion(bf16[4,1024,32]{1,2,0:T(8,128)(2,1)S(1)} %fusion.68, bf16[3,4,1024,32]{2,3,1,0:T(8,128)(2,1)} %get-tuple-element.13, f32[4,1024]{1,0:T(4,128)S(1)} %fusion.109), kind=kOutput, calls=%fused_computation.50 | convolution fusion | flops 545526784 | bytes 1064960 | tf_op jit(solution)/shard_map/ist,itd->isd/dot_general | solution.py:127
  87.0 0.3 reshape.91
  87.4 0.1 copy.60
  87.5 0.4 reshape.165
  87.9 10.4 %all_to_all.10 = bf16[16,2,4096]{2,1,0:T(2,128)(2,1)S(1)} all-to-all(bf16[16,2,4096]{2,1,0:T(2,128)(2,1)S(1)} %reshape.165), channel_id=1, replica_groups=mesh['lat'=16,'lon'=16] {'lon'}, dimensions={0} | all-to-all | bytes 524288 | tf_op jit(solution)/shard_map/all_to_all | solution.py:133
  98.4 0.3 reshape.166
  98.7 1.0 %fusion.45 = bf16[8,64,256]{2,1,0:T(8,128)(2,1)} fusion(bf16[8,64,256]{1,2,0:T(8,128)(2,1)S(1)} %bitcast.123, bf16[8,64,256]{2,1,0:T(8,128)(2,1)S(1)} %get-tuple-element.6, bf16[256,256]{1,0:T(8,128)(2,1)S(1)} %copy-done.1), kind=kOutput, calls=%fused_computation.47 | convolution fusion | flops 67502080 | bytes 917504 | tf_op jit(solution)/shard_map/dot_general | solution.py:136
  (45 shorter events, 1.0 us)
Async XLA Ops:
  0.0 54.1 %copy-start = (bf16[4,4,256,256]{3,2,1,0:T(8,128)(2,1)S(1)}, bf16[4,4,256,256]{3,2,1,0:T(8,128)(2,1)}, u32[]{:S(2)}) copy-start(bf16[4,4,256,256]{3,2,1,0:T(8,128)(2,1)} %param.16) | copy-start | bytes 6291460
  4.2 8.8 %collective-permute-start = (bf16[32,96,4]{1,0,2:T(8,128)(2,1)S(1)}, bf16[32,96,4]{1,0,2:T(8,128)(2,1)S(1)}, u32[]{:S(2)}, u32[]{:S(2)}) collective-permute-start(bf16[32,96,4]{1,0,2:T(8,128)(2,1)S(1)} %copy.48), channel_id=1, source_target_pairs={{0,1},{1,2},{2,3},{3,4},{4,5},{5,6},{6,7},{7,8},{8,9},{9,10},{10,1... | collective-permute-start | bytes 73736 | tf_op jit(solution)/shard_map/ppermute | solution.py:82
  4.6 8.4 %collective-permute-start.1 = (bf16[32,96,4]{1,0,2:T(8,128)(2,1)S(1)}, bf16[32,96,4]{1,0,2:T(8,128)(2,1)S(1)}, u32[]{:S(2)}, u32[]{:S(2)}) collective-permute-start(bf16[32,96,4]{1,0,2:T(8,128)(2,1)S(1)} %copy.49), channel_id=1, source_target_pairs={{1,0},{2,1},{3,2},{4,3},{5,4},{6,5},{7,6},{8,7},{9,8},{10,9},{11,1... | collective-permute-start | bytes 73736 | tf_op jit(solution)/shard_map/ppermute | solution.py:83
  15.3 8.4 %copy-start.6 = (bf16[3,3,96,128]{3,2,1,0:T(8,128)(2,1)S(1)}, bf16[3,3,96,128]{3,2,1,0:T(8,128)(2,1)}, u32[]{:S(2)}) copy-start(bf16[3,3,96,128]{3,2,1,0:T(8,128)(2,1)} %param.12) | copy-start | bytes 663556
  15.3 8.4 %copy-start.7 = (f32[128]{0:T(128)S(1)}, f32[128]{0:T(128)}, u32[]{:S(2)}) copy-start(f32[128]{0:T(128)} %param.13) | copy-start | bytes 1540
  15.3 8.4 %copy-start.9 = (pred[8,33]{0,1:T(8,128)(4,1)S(1)}, pred[8,33]{0,1:T(8,128)(4,1)}, u32[]{:S(2)}) copy-start(pred[8,33]{0,1:T(8,128)(4,1)} %constant.94) | copy-start | bytes 796
  15.3 14.5 %collective-permute-start.2 = (bf16[4,96,264]{1,0,2:T(4,128)(2,1)S(1)}, bf16[4,96,264]{1,0,2:T(4,128)(2,1)S(1)}, u32[]{:S(2)}, u32[]{:S(2)}) collective-permute-start(bf16[4,96,264]{1,0,2:T(4,128)(2,1)S(1)} %get-tuple-element.7), channel_id=1, source_target_pairs={{0,16},{16,32},{32,48},{48,64},{64,80},{80,96},{96,112},{112,128},... | collective-permute-start | bytes 608264 | tf_op jit(solution)/shard_map/ppermute | solution.py:85
  20.3 12.0 %collective-permute-start.3 = (bf16[4,96,264]{1,0,2:T(4,128)(2,1)S(1)}, bf16[4,96,264]{1,0,2:T(4,128)(2,1)S(1)}, u32[]{:S(2)}, u32[]{:S(2)}) collective-permute-start(bf16[4,96,264]{1,0,2:T(4,128)(2,1)S(1)} %get-tuple-element.8), channel_id=1, source_target_pairs={{16,0},{32,16},{48,32},{64,48},{80,64},{96,80},{112,96},{128,112},... | collective-permute-start | bytes 608264 | tf_op jit(solution)/shard_map/ppermute | solution.py:86
  37.2 1.2 %copy-start.5 = (bf16[4,4,128,256]{3,2,1,0:T(8,128)(2,1)S(1)}, bf16[4,4,128,256]{3,2,1,0:T(8,128)(2,1)}, u32[]{:S(2)}) copy-start(bf16[4,4,128,256]{3,2,1,0:T(8,128)(2,1)} %param.14) | copy-start | bytes 3145732
  37.2 1.2 %copy-start.10 = (pred[8,17]{0,1:T(8,128)(4,1)S(1)}, pred[8,17]{0,1:T(8,128)(4,1)}, u32[]{:S(2)}) copy-start(pred[8,17]{0,1:T(8,128)(4,1)} %constant.93) | copy-start | bytes 412
  44.0 4.2 %copy-start.2 = (f32[256]{0:T(256)S(1)}, f32[256]{0:T(256)}, u32[]{:S(2)}) copy-start(f32[256]{0:T(256)} %param.15) | copy-start | bytes 3076
  52.3 1.9 %copy-start.11 = (pred[8,9]{0,1:T(8,128)(4,1)S(1)}, pred[8,9]{0,1:T(8,128)(4,1)}, u32[]{:S(2)}) copy-start(pred[8,9]{0,1:T(8,128)(4,1)} %constant.92) | copy-start | bytes 220
  54.2 1.7 %copy-start.3 = (f32[256]{0:T(256)S(1)}, f32[256]{0:T(256)}, u32[]{:S(2)}) copy-start(f32[256]{0:T(256)} %param.17) | copy-start | bytes 3076
  55.6 0.9 copy-start.4
  55.8 8.1 %copy-start.8 = (f32[8]{0:T(128)S(1)}, f32[8]{0:T(128)}, u32[]{:S(2)}) copy-start(f32[8]{0:T(128)} %param.20) | copy-start | bytes 100
  57.5 16.0 %all-to-all-start = ((bf16[16,64,256]{2,1,0:T(8,128)(2,1)}), bf16[16,64,256]{2,1,0:T(8,128)(2,1)S(1)}, u32[]{:S(2)}, u32[]{:S(2)}) async-start(bf16[16,64,256]{2,1,0:T(8,128)(2,1)} %bitcast.21), calls=%async_computation | async-start | bytes 1048576 | tf_op jit(solution)/shard_map/all_to_all | solution.py:113
  87.0 11.7 %copy-start.1 = (bf16[256,256]{1,0:T(8,128)(2,1)S(1)}, bf16[256,256]{1,0:T(8,128)(2,1)}, u32[]{:S(2)}) copy-start(bf16[256,256]{1,0:T(8,128)(2,1)} %param.21) | copy-start | bytes 393220

commit v8 on v7

--- a/solution.py
+++ b/solution.py
@@ -87,8 +87,9 @@
     middle = first_conv(wide, smoothing_filter_taps, smoothing_offset_entries)
     upper = first_conv(jnp.concatenate([top, wide[:2]], axis=0), smoothing_filter_taps, smoothing_offset_entries)
     lower = first_conv(jnp.concatenate([wide[band - 2 :], bottom], axis=0), smoothing_filter_taps, smoothing_offset_entries)
+    upper = clear_outside(upper, base - HALO + 1, lat_total)
+    lower = clear_outside(lower, base + band - 1, lat_total)
     opening_halved = jnp.concatenate([upper, middle, lower], axis=0)
-    opening_halved = clear_outside(opening_halved, base - HALO + 1, lat_total)
     closing_halved = halving_filter(opening_halved, opening_coarsen_taps, opening_coarsen_offset)
     closing_halved = clear_outside(closing_halved, base // 2 - 1, lat_total // 2)
     closing_halved = lax.optimization_barrier(closing_halved)

time: 101 us -> 102 us (level)
  other arithmetic: 7.76 us -> 9.69 us
  matrix products: 25.3 us -> 24.2 us
    broadcast_in_dim x0 -> x1, other arithmetic: none -> 1.75 us  [halving_filter(): extended[None]]
    conv_general_dilated x3, matrix products: 6.59 us -> 5.43 us  [first_conv(): lax.conv_general_dilated(extended[None], kernel, (1, 1), 'VALID', dimensi...]
    convert_element_type x6 -> x0, local copies, waits for them, and re-layouts: 1.15 us -> none  [first_conv(): return jax.nn.silu(total + bias).astype(jnp.bfloat16)]
    convert_element_type x0 -> x1, other arithmetic: none -> 1.12 us  [first_conv(): return jax.nn.silu(total + bias).astype(jnp.bfloat16)]
    conv_general_dilated x6 -> x9, local copies, waits for them, and re-layouts: 1.01 us -> 2.12 us  [first_conv(): lax.conv_general_dilated(extended[None], kernel, (1, 1), 'VALID', dimensi...]
where the time goes in v8:
time: 102 us; the launch traced here: 100 us
  local copies, waits for them, and re-layouts  27.1 us (27%)
  matrix products  24.2 us (24%)
  starting transfers between devices  16.8 us (16%)
  waiting for transfers between devices  11.6 us (11%)
  blocking collectives  10.4 us (10%)
  other arithmetic  9.69 us (10%)
    conv_general_dilated x9, local copies, waits for them, and re-layouts, halving_filter(): lax.conv_general_dilated(extended[None], kernel, (2, 2), 'VALID', dimensi...  11.2 us
    all_to_all x1, blocking collectives, on_device(): attended = lax.all_to_all(attended, 'lon', 0, 0, tiled=True)  10.4 us
    all_to_all x1, waiting for transfers between devices, on_device(): gathered = lax.all_to_all(row_copies, 'lon', 0, 0, tiled=True)  9.53 us
    unnamed x30, local copies, waits for them, and re-layouts  8.65 us
    dot_general x1, matrix products, on_device(): jnp.einsum('ist,itd->isd', weights.astype(jnp.bfloat16), v_items, preferr...  6.59 us
    sub x1, matrix products, on_device(): weights = jnp.exp(scores - best)  5.51 us
    conv_general_dilated x3, matrix products, first_conv(): lax.conv_general_dilated(extended[None], kernel, (1, 1), 'VALID', dimensi...  5.43 us
    all_to_all x1, starting transfers between devices, on_device(): gathered = lax.all_to_all(row_copies, 'lon', 0, 0, tiled=True)  5.17 us
  transfers between devices with their start and end apart: 5, of which 2 were waited for; matrix products, arithmetic and copies ran while one was open for 13% of the time, Pallas kernels for 0%

profile of v8, /device:TPU:112, one launch (start us, length us, event | category | flops | bytes accessed | tf_op | source)
XLA Modules:
  0.0 100.3 jit_solution(1816651187869409221)
XLA Ops:
  0.0 2.7 %fusion.109 = (bf16[32,96,4]{2,1,0:T(8,128)(2,1)}, bf16[32,96,4]{2,1,0:T(8,128)(2,1)S(1)}) fusion(bf16[32,96,256]{2,1,0:T(8,128)(2,1)} %param.11), kind=kLoop, calls=%fused_computation.123 | loop fusion | bytes 98304 | tf_op jit(solution)/shard_map/slice | solution.py:82
  2.7 1.5 %copy.48 = bf16[32,96,4]{1,0,2:T(8,128)(2,1)S(1)} copy(bf16[32,96,4]{2,1,0:T(8,128)(2,1)} %get-tuple-element.11) | data formatting | bytes 49152
  4.3 0.3 copy.49
  4.6 3.9 %collective-permute-start.1 = (bf16[32,96,4]{1,0,2:T(8,128)(2,1)S(1)}, bf16[32,96,4]{1,0,2:T(8,128)(2,1)S(1)}, u32[]{:S(2)}, u32[]{:S(2)}) collective-permute-start(bf16[32,96,4]{1,0,2:T(8,128)(2,1)S(1)} %copy.49), channel_id=1, source_target_pairs={{1,0},{2,1},{3,2},{4,3},{5,4},{6,5},{7,6},{8,7},{9,8},{10,9},{11,1... | collective-permute-start | bytes 73736 | tf_op jit(solution)/shard_map/ppermute | solution.py:83
  8.5 4.4 %copy.16 = bf16[32,96,256]{1,0,2:T(8,128)(2,1)} copy(bf16[32,96,256]{2,1,0:T(8,128)(2,1)} %param.11) | data formatting | bytes 3145728 | tf_op args[0]
  13.0 2.1 %pad_maximum_fusion = bf16[32,96,264]{1,0,2:T(8,128)(2,1)S(1)} fusion(bf16[32,96,4]{1,0,2:T(8,128)(2,1)S(1)} %collective-permute-done.1, bf16[32,96,256]{1,0,2:T(8,128)(2,1)} %copy.16, bf16[32,96,4]{1,0,2:T(8,128)(2,1)S(1)} %collective-permute-done), kind=kLoop, calls=%fused_computation.29 | loop fusion | flops 1622016 | bytes 3244032 | tf_op jit(solution)/shard_map/concatenate | solution.py:84
  15.1 0.2 fusion.107
  15.3 4.9 %collective-permute-start.2 = (bf16[4,96,264]{1,0,2:T(4,128)(2,1)S(1)}, bf16[4,96,264]{1,0,2:T(4,128)(2,1)S(1)}, u32[]{:S(2)}, u32[]{:S(2)}) collective-permute-start(bf16[4,96,264]{1,0,2:T(4,128)(2,1)S(1)} %get-tuple-element.7), channel_id=1, source_target_pairs={{0,16},{16,32},{32,48},{48,64},{64,80},{80,96},{96,112},{112,128},... | collective-permute-start | bytes 608264 | tf_op jit(solution)/shard_map/ppermute | solution.py:85
  20.3 2.7 %collective-permute-start.3 = (bf16[4,96,264]{1,0,2:T(4,128)(2,1)S(1)}, bf16[4,96,264]{1,0,2:T(4,128)(2,1)S(1)}, u32[]{:S(2)}, u32[]{:S(2)}) collective-permute-start(bf16[4,96,264]{1,0,2:T(4,128)(2,1)S(1)} %get-tuple-element.8), channel_id=1, source_target_pairs={{16,0},{32,16},{48,32},{64,48},{80,64},{96,80},{112,96},{128,112},... | collective-permute-start | bytes 608264 | tf_op jit(solution)/shard_map/ppermute | solution.py:86
  23.0 0.8 copy.22
  23.9 4.0 %broadcast_select_fusion = f32[30,8,33,128]{3,1,2,0:T(8,128)S(1)} fusion(pred[8,33]{0,1:T(8,128)(4,1)S(1)} %copy-done.9, bf16[3,3,96,128]{3,2,1,0:T(8,128)(2,1)S(1)} %copy-done.7, bf16[32,96,1,7,2]{1,3,4,0,2:T(8,128)(2,1)S(1)} %slice.54, bf16[32,96,1,8,33]{1,3,4,0,2:T(8,128)(2,1)S(1)} %copy.22), kind=kOutput, calls=%fused_computation.31 | convolution fusion | flops 1757952000 | bytes 5984520 | tf_op jit(solution)/shard_map/conv_general_dilated | solution.py:40
  27.9 0.8 copy.23
  28.8 1.1 %multiply_convert_fusion = bf16[30,262,128]{2,0,1:T(8,128)(2,1)S(1)} fusion(f32[30,1,264,128]{3,0,2,1:T(8,128)S(1)} %bitcast.135, f32[128]{0:T(128)S(1)} %copy-done.2), kind=kLoop, calls=%fused_computation.10 | loop fusion | flops 6036480 | bytes 6036992 | tf_op jit(solution)/shard_map/convert_element_type | solution.py:48
  29.9 0.2 fusion.108
  30.1 2.1 %collective-permute-done.3 = bf16[4,96,264]{1,0,2:T(4,128)(2,1)S(1)} collective-permute-done((bf16[4,96,264]{1,0,2:T(4,128)(2,1)S(1)}, bf16[4,96,264]{1,0,2:T(4,128)(2,1)S(1)}, u32[]{:S(2)}, u32[]{:S(2)}) %collective-permute-start.3) | collective-permute-done | bytes 202784 | tf_op jit(solution)/shard_map/ppermute | solution.py:86
  32.2 0.7 pad_maximum_fusion.1
  33.0 0.7 convolution_select_fusion
  33.7 0.1 copy.27
  34.0 0.7 convolution_select_fusion.1
  34.7 0.1 copy.20
  34.8 0.7 broadcast_select_fusion.2
  35.5 1.8 %maximum_bitcast_fusion = bf16[38,1,262,128]{3,0,2,1:T(8,128)(2,1)S(1)} fusion(bf16[4,262,128]{2,0,1:T(4,128)(2,1)S(1)} %get-tuple-element.14, bf16[30,262,128]{2,0,1:T(8,128)(2,1)S(1)} %multiply_convert_fusion, bf16[4,262,128]{2,0,1:T(4,128)(2,1)S(1)} %get-tuple-element.13), kind=kLoop, calls=%fused_computation.19 | loop fusion | flops 7646208 | bytes 5097472 | tf_op jit(solution)/shard_map/broadcast_in_dim | solution.py:53
  37.3 0.5 pad.3
  37.8 0.7 copy.29
  38.5 0.4 copy-done.6
  39.0 2.9 %fusion.26 = f32[18,8,17,256]{3,1,2,0:T(8,128)S(1)} fusion(bf16[4,4,128,256]{3,2,1,0:T(8,128)(2,1)S(1)} %copy-done.6, bf16[38,1,7,3,128]{4,2,3,0,1:T(8,128)(2,1)S(1)} %slice.60, bf16[38,1,8,34,128]{4,2,3,0,1:T(8,128)(2,1)S(1)} %copy.29, pred[8,17]{0,1:T(8,128)(4,1)S(1)} %copy-done.10), kind=kOutput, calls=%fused_computation.32 | convolution fusion | flops 2576179200 | bytes 6405768 | tf_op jit(solution)/shard_map/conv_general_dilated | solution.py:52
  41.9 2.7 %copy.30 = f32[18,8,17,256]{3,2,1,0:T(8,128)} copy(f32[18,8,17,256]{3,1,2,0:T(8,128)S(1)} %fusion.26) | data formatting | bytes 5013504 | tf_op jit(solution)/shard_map/conv_general_dilated | solution.py:52
  44.6 4.2 %reshape.96 = f32[18,1,136,256]{3,2,0,1:T(8,128)} reshape(f32[18,8,17,256]{3,2,1,0:T(8,128)} %copy.30) | data formatting | bytes 5013504 | tf_op jit(solution)/shard_map/conv_general_dilated | solution.py:52
  48.8 2.5 %fusion.41 = bf16[18,130,256]{2,1,0:T(8,128)(2,1)S(1)} fusion(f32[256]{0:T(256)S(1)} %copy-done.3, f32[18,1,136,256]{3,2,0,1:T(8,128)} %reshape.96, pred[18]{0:T(512)(128)(4,1)S(1)} %compare_and_fusion.2), kind=kLoop, calls=%fused_computation.41 | loop fusion | flops 4193280 | bytes 3595282 | tf_op jit(solution)/shard_map/jit(_where)/select_n | solution.py:36
  51.4 1.4 %reshape.99 = bf16[18,1,8,18,256]{4,3,2,0,1:T(8,128)(2,1)} reshape(bf16[18,1,144,256]{3,2,0,1:T(8,128)(2,1)S(1)} %pad.5) | data formatting | bytes 2654208 | tf_op jit(solution)/shard_map/conv_general_dilated | solution.py:52
  52.8 1.8 %copy.32 = bf16[18,1,8,18,256]{4,2,3,0,1:T(8,128)(2,1)S(1)} copy(bf16[18,1,8,18,256]{4,3,2,0,1:T(8,128)(2,1)} %reshape.99) | data formatting | bytes 2654208 | tf_op jit(solution)/shard_map/conv_general_dilated | solution.py:52
  54.7 1.4 %fusion.42 = f32[8,8,9,256]{3,1,2,0:T(8,128)S(1)} fusion(bf16[4,4,256,256]{3,2,1,0:T(8,128)(2,1)S(1)} %copy-done, bf16[18,1,7,3,256]{4,2,3,0,1:T(8,128)(2,1)S(1)} %slice.62, bf16[18,1,8,18,256]{4,2,3,0,1:T(8,128)(2,1)S(1)} %copy.32, pred[8,9]{0,1:T(8,128)(4,1)S(1)} %copy-done.11), kind=kOutput, calls=%fused_computation.45 | convolution fusion | flops 1212751872 | bytes 4207688 | tf_op jit(solution)/shard_map/conv_general_dilated | solution.py:52
  56.1 0.2 copy.33
  56.4 0.3 convert_reduce_fusion
  56.7 0.3 fusion.66
  57.0 0.2 fusion.68
  57.2 0.8 broadcast_in_dim.62
  58.1 5.2 %all-to-all-start = ((bf16[16,64,256]{2,1,0:T(8,128)(2,1)}), bf16[16,64,256]{2,1,0:T(8,128)(2,1)S(1)}, u32[]{:S(2)}, u32[]{:S(2)}) async-start(bf16[16,64,256]{2,1,0:T(8,128)(2,1)} %bitcast.21), calls=%async_computation | async-start | bytes 1048576 | tf_op jit(solution)/shard_map/all_to_all | solution.py:114
  63.3 1.2 %copy.35 = bf16[256,768]{0,1:T(8,128)(2,1)S(1)} copy(bf16[256,768]{1,0:T(8,128)(2,1)} %param.19) | data formatting | bytes 786432 | tf_op args[8]
  64.5 9.5 %all-to-all-done = bf16[16,64,256]{2,1,0:T(8,128)(2,1)S(1)} async-done(((bf16[16,64,256]{2,1,0:T(8,128)(2,1)}), bf16[16,64,256]{2,1,0:T(8,128)(2,1)S(1)}, u32[]{:S(2)}, u32[]{:S(2)}) %all-to-all-start) | async-done | bytes 524320 | tf_op jit(solution)/shard_map/all_to_all | solution.py:114
  74.1 1.3 %fusion.110 = (bf16[3,4,1024,32]{2,3,1,0:T(8,128)(2,1)}, f32[3,4,1024,32]{2,3,1,0:T(8,128)S(1)}) fusion(bf16[1024,256,1,1]{1,0,3,2:T(8,128)(2,1)S(1)} %bitcast.144, bf16[256,3,8,32]{0,3,2,1:T(8,128)(2,1)S(1)} %bitcast.147, s32[]{:T(128)S(6)} %select_n.31), kind=kOutput, calls=%fused_computation.124 | convolution fusion | flops 201719808 | bytes 3080196 | tf_op jit(solution)/shard_map/tc,cjhd->jhtd/dot_general | solution.py:118
  75.5 5.5 %fusion.111 = f32[4,1024]{1,0:T(4,128)S(1)} fusion(bf16[4,1024,32]{1,2,0:T(8,128)(2,1)S(1)} %fusion.70, bf16[3,4,1024,32]{2,3,1,0:T(8,128)(2,1)} %get-tuple-element.15), kind=kOutput, calls=%fused_computation.125 | convolution fusion | flops 276825088 | bytes 540672 | tf_op jit(solution)/shard_map/sub | solution.py:126
  81.0 6.6 %fusion.52 = bf16[4,1024,32]{1,2,0:T(8,128)(2,1)S(1)} fusion(bf16[4,1024,32]{1,2,0:T(8,128)(2,1)S(1)} %fusion.70, bf16[3,4,1024,32]{2,3,1,0:T(8,128)(2,1)} %get-tuple-element.15, f32[4,1024]{1,0:T(4,128)S(1)} %fusion.111), kind=kOutput, calls=%fused_computation.49 | convolution fusion | flops 545526784 | bytes 1064960 | tf_op jit(solution)/shard_map/ist,itd->isd/dot_general | solution.py:128
  87.6 0.3 reshape.66
  88.1 0.4 reshape.144
  88.5 10.4 %all_to_all.10 = bf16[16,2,4096]{2,1,0:T(2,128)(2,1)S(1)} all-to-all(bf16[16,2,4096]{2,1,0:T(2,128)(2,1)S(1)} %reshape.144), channel_id=1, replica_groups=mesh['lat'=16,'lon'=16] {'lon'}, dimensions={0} | all-to-all | bytes 524288 | tf_op jit(solution)/shard_map/all_to_all | solution.py:134
  98.9 0.3 reshape.145
  99.3 1.0 %fusion.45 = bf16[8,64,256]{2,1,0:T(8,128)(2,1)} fusion(bf16[8,64,256]{1,2,0:T(8,128)(2,1)S(1)} %bitcast.145, bf16[8,64,256]{2,1,0:T(8,128)(2,1)S(1)} %get-tuple-element.6, bf16[256,256]{1,0:T(8,128)(2,1)S(1)} %copy-done.1), kind=kOutput, calls=%fused_computation.46 | convolution fusion | flops 67502080 | bytes 917504 | tf_op jit(solution)/shard_map/dot_general | solution.py:137
  (44 shorter events, 0.9 us)
Async XLA Ops:
  0.0 54.7 %copy-start = (bf16[4,4,256,256]{3,2,1,0:T(8,128)(2,1)S(1)}, bf16[4,4,256,256]{3,2,1,0:T(8,128)(2,1)}, u32[]{:S(2)}) copy-start(bf16[4,4,256,256]{3,2,1,0:T(8,128)(2,1)} %param.16) | copy-start | bytes 6291460
  4.2 8.8 %collective-permute-start = (bf16[32,96,4]{1,0,2:T(8,128)(2,1)S(1)}, bf16[32,96,4]{1,0,2:T(8,128)(2,1)S(1)}, u32[]{:S(2)}, u32[]{:S(2)}) collective-permute-start(bf16[32,96,4]{1,0,2:T(8,128)(2,1)S(1)} %copy.48), channel_id=1, source_target_pairs={{0,1},{1,2},{2,3},{3,4},{4,5},{5,6},{6,7},{7,8},{8,9},{9,10},{10,1... | collective-permute-start | bytes 73736 | tf_op jit(solution)/shard_map/ppermute | solution.py:82
  4.6 8.4 %collective-permute-start.1 = (bf16[32,96,4]{1,0,2:T(8,128)(2,1)S(1)}, bf16[32,96,4]{1,0,2:T(8,128)(2,1)S(1)}, u32[]{:S(2)}, u32[]{:S(2)}) collective-permute-start(bf16[32,96,4]{1,0,2:T(8,128)(2,1)S(1)} %copy.49), channel_id=1, source_target_pairs={{1,0},{2,1},{3,2},{4,3},{5,4},{6,5},{7,6},{8,7},{9,8},{10,9},{11,1... | collective-permute-start | bytes 73736 | tf_op jit(solution)/shard_map/ppermute | solution.py:83
  15.3 8.6 %copy-start.7 = (bf16[3,3,96,128]{3,2,1,0:T(8,128)(2,1)S(1)}, bf16[3,3,96,128]{3,2,1,0:T(8,128)(2,1)}, u32[]{:S(2)}) copy-start(bf16[3,3,96,128]{3,2,1,0:T(8,128)(2,1)} %param.12) | copy-start | bytes 663556
  15.3 8.6 %copy-start.9 = (pred[8,33]{0,1:T(8,128)(4,1)S(1)}, pred[8,33]{0,1:T(8,128)(4,1)}, u32[]{:S(2)}) copy-start(pred[8,33]{0,1:T(8,128)(4,1)} %constant.97) | copy-start | bytes 796
  15.3 14.8 %collective-permute-start.2 = (bf16[4,96,264]{1,0,2:T(4,128)(2,1)S(1)}, bf16[4,96,264]{1,0,2:T(4,128)(2,1)S(1)}, u32[]{:S(2)}, u32[]{:S(2)}) collective-permute-start(bf16[4,96,264]{1,0,2:T(4,128)(2,1)S(1)} %get-tuple-element.7), channel_id=1, source_target_pairs={{0,16},{16,32},{32,48},{48,64},{64,80},{80,96},{96,112},{112,128},... | collective-permute-start | bytes 608264 | tf_op jit(solution)/shard_map/ppermute | solution.py:85
  20.3 12.0 %collective-permute-start.3 = (bf16[4,96,264]{1,0,2:T(4,128)(2,1)S(1)}, bf16[4,96,264]{1,0,2:T(4,128)(2,1)S(1)}, u32[]{:S(2)}, u32[]{:S(2)}) collective-permute-start(bf16[4,96,264]{1,0,2:T(4,128)(2,1)S(1)} %get-tuple-element.8), channel_id=1, source_target_pairs={{16,0},{32,16},{48,32},{64,48},{80,64},{96,80},{112,96},{128,112},... | collective-permute-start | bytes 608264 | tf_op jit(solution)/shard_map/ppermute | solution.py:86
  27.9 0.9 copy-start.2
  37.8 1.2 %copy-start.6 = (bf16[4,4,128,256]{3,2,1,0:T(8,128)(2,1)S(1)}, bf16[4,4,128,256]{3,2,1,0:T(8,128)(2,1)}, u32[]{:S(2)}) copy-start(bf16[4,4,128,256]{3,2,1,0:T(8,128)(2,1)} %param.14) | copy-start | bytes 3145732
  37.8 1.2 %copy-start.10 = (pred[8,17]{0,1:T(8,128)(4,1)S(1)}, pred[8,17]{0,1:T(8,128)(4,1)}, u32[]{:S(2)}) copy-start(pred[8,17]{0,1:T(8,128)(4,1)} %constant.96) | copy-start | bytes 412
  44.6 4.2 %copy-start.3 = (f32[256]{0:T(256)S(1)}, f32[256]{0:T(256)}, u32[]{:S(2)}) copy-start(f32[256]{0:T(256)} %param.15) | copy-start | bytes 3076
  52.8 1.9 %copy-start.11 = (pred[8,9]{0,1:T(8,128)(4,1)S(1)}, pred[8,9]{0,1:T(8,128)(4,1)}, u32[]{:S(2)}) copy-start(pred[8,9]{0,1:T(8,128)(4,1)} %constant.95) | copy-start | bytes 220
  54.7 1.7 %copy-start.4 = (f32[256]{0:T(256)S(1)}, f32[256]{0:T(256)}, u32[]{:S(2)}) copy-start(f32[256]{0:T(256)} %param.17) | copy-start | bytes 3076
  56.1 0.9 copy-start.5
  56.3 8.1 %copy-start.8 = (f32[8]{0:T(128)S(1)}, f32[8]{0:T(128)}, u32[]{:S(2)}) copy-start(f32[8]{0:T(128)} %param.20) | copy-start | bytes 100
  58.1 16.0 %all-to-all-start = ((bf16[16,64,256]{2,1,0:T(8,128)(2,1)}), bf16[16,64,256]{2,1,0:T(8,128)(2,1)S(1)}, u32[]{:S(2)}, u32[]{:S(2)}) async-start(bf16[16,64,256]{2,1,0:T(8,128)(2,1)} %bitcast.21), calls=%async_computation | async-start | bytes 1048576 | tf_op jit(solution)/shard_map/all_to_all | solution.py:114
  87.6 11.7 %copy-start.1 = (bf16[256,256]{1,0:T(8,128)(2,1)S(1)}, bf16[256,256]{1,0:T(8,128)(2,1)}, u32[]{:S(2)}) copy-start(bf16[256,256]{1,0:T(8,128)(2,1)} %param.21) | copy-start | bytes 393220

commit v9 on v7

--- a/solution.py
+++ b/solution.py
@@ -78,9 +78,8 @@
     base = lax.axis_index("lat") * band
     n_lat, n_lon = lax.axis_size("lat"), lax.axis_size("lon")
     width = meridian_slab_data.shape[2]
-    source = lax.optimization_barrier(meridian_slab_data)
-    left = lax.ppermute(source[:, :, width - HALO :], "lon", [(i, (i + 1) % n_lon) for i in range(n_lon)])
-    right = lax.ppermute(source[:, :, :HALO], "lon", [((i + 1) % n_lon, i) for i in range(n_lon)])
+    left = lax.ppermute(meridian_slab_data[:, :, width - HALO :], "lon", [(i, (i + 1) % n_lon) for i in range(n_lon)])
+    right = lax.ppermute(meridian_slab_data[:, :, :HALO], "lon", [((i + 1) % n_lon, i) for i in range(n_lon)])
     wide = jnp.concatenate([left, meridian_slab_data, right], axis=2)
     top = lax.ppermute(wide[band - HALO :], "lat", [(i, i + 1) for i in range(n_lat - 1)])
     bottom = lax.ppermute(wide[:HALO], "lat", [(i + 1, i) for i in range(n_lat - 1)])

time: 101 us -> 100 us (0.990)
  local copies, waits for them, and re-layouts: 27.1 us -> 23.5 us
  waiting for transfers between devices: 12 us -> 15 us
    slice x1, local copies, waits for them, and re-layouts: 2.7 us -> 0.78 us  [on_device(): meridian_slab_data[:, :, width - HALO:]]
    unnamed x30 -> x28, local copies, waits for them, and re-layouts: 8.66 us -> 7 us
    ppermute x2, waiting for transfers between devices: 0.01 us -> 1.58 us  [the longest x1 1.58 us: on_device(): lax.ppermute(meridian_slab_data[:, :, width - HALO:], 'lon', [(i, (i + 1)...]
    ppermute x1, waiting for transfers between devices: 2.43 us -> 3.86 us  [on_device(): lax.ppermute(wide[:HALO], 'lat', [(i + 1, i) for i in range(n_lat - 1)])]
  transfers between devices with their start and end apart: 5 -> 5, of which waited for: 2 -> 3; matrix products, arithmetic and copies ran while one was open for 13% -> 8% of each run, Pallas kernels for 0% -> 0%
where the time goes in v9:
time: 100 us; the launch traced here: 99.2 us
  matrix products  25.3 us (25%)
  local copies, waits for them, and re-layouts  23.5 us (24%)
  starting transfers between devices  16.6 us (17%)
  waiting for transfers between devices  15 us (15%)
  blocking collectives  10.4 us (10%)
  other arithmetic  7.76 us (8%)
    conv_general_dilated x9, local copies, waits for them, and re-layouts, halving_filter(): lax.conv_general_dilated(extended[None], kernel, (2, 2), 'VALID', dimensi...  11.2 us
    all_to_all x1, blocking collectives, on_device(): attended = lax.all_to_all(attended, 'lon', 0, 0, tiled=True)  10.4 us
    all_to_all x1, waiting for transfers between devices, on_device(): gathered = lax.all_to_all(row_copies, 'lon', 0, 0, tiled=True)  9.54 us
    unnamed x28, local copies, waits for them, and re-layouts  7 us
    conv_general_dilated x3, matrix products, first_conv(): lax.conv_general_dilated(extended[None], kernel, (1, 1), 'VALID', dimensi...  6.6 us
    dot_general x1, matrix products, on_device(): jnp.einsum('ist,itd->isd', weights.astype(jnp.bfloat16), v_items, preferr...  6.58 us
    sub x1, matrix products, on_device(): weights = jnp.exp(scores - best)  5.52 us
    all_to_all x1, starting transfers between devices, on_device(): gathered = lax.all_to_all(row_copies, 'lon', 0, 0, tiled=True)  5.31 us
  transfers between devices with their start and end apart: 5, of which 3 were waited for; matrix products, arithmetic and copies ran while one was open for 8% of the time, Pallas kernels for 0%

profile of v9, /device:TPU:112, one launch (start us, length us, event | category | flops | bytes accessed | tf_op | source)
XLA Modules:
  0.0 99.2 jit_solution(2054849868651189169)
XLA Ops:
  0.0 4.6 %copy.14 = bf16[32,96,256]{1,0,2:T(8,128)(2,1)} copy(bf16[32,96,256]{2,1,0:T(8,128)(2,1)} %param.11) | data formatting | bytes 3145728 | tf_op args[0]
  4.6 0.8 fusion.107
  5.4 3.9 %collective-permute-start.1 = (bf16[32,96,4]{1,0,2:T(8,128)(2,1)S(1)}, bf16[32,96,4]{1,0,2:T(8,128)(2,1)S(1)}, u32[]{:S(2)}, u32[]{:S(2)}) collective-permute-start(bf16[32,96,4]{1,0,2:T(8,128)(2,1)S(1)} %get-tuple-element.12), channel_id=1, source_target_pairs={{1,0},{2,1},{3,2},{4,3},{5,4},{6,5},{7,6},{8,7},{9,8},{10,9},{11,1... | collective-permute-start | bytes 73736 | tf_op jit(solution)/shard_map/ppermute | solution.py:82
  9.2 1.6 %collective-permute-done = bf16[32,96,4]{1,0,2:T(8,128)(2,1)S(1)} collective-permute-done((bf16[32,96,4]{1,0,2:T(8,128)(2,1)S(1)}, bf16[32,96,4]{1,0,2:T(8,128)(2,1)S(1)}, u32[]{:S(2)}, u32[]{:S(2)}) %collective-permute-start) | collective-permute-done | bytes 24608 | tf_op jit(solution)/shard_map/ppermute | solution.py:81
  10.8 2.1 %pad_maximum_fusion = bf16[32,96,264]{1,0,2:T(8,128)(2,1)S(1)} fusion(bf16[32,96,4]{1,0,2:T(8,128)(2,1)S(1)} %collective-permute-done.1, bf16[32,96,256]{1,0,2:T(8,128)(2,1)} %copy.14, bf16[32,96,4]{1,0,2:T(8,128)(2,1)S(1)} %collective-permute-done), kind=kLoop, calls=%fused_computation.28 | loop fusion | flops 1622016 | bytes 3244032 | tf_op jit(solution)/shard_map/concatenate | solution.py:83
  12.9 0.2 fusion.105
  13.2 4.9 %collective-permute-start.2 = (bf16[4,96,264]{1,0,2:T(4,128)(2,1)S(1)}, bf16[4,96,264]{1,0,2:T(4,128)(2,1)S(1)}, u32[]{:S(2)}, u32[]{:S(2)}) collective-permute-start(bf16[4,96,264]{1,0,2:T(4,128)(2,1)S(1)} %get-tuple-element.7), channel_id=1, source_target_pairs={{0,16},{16,32},{32,48},{48,64},{64,80},{80,96},{96,112},{112,128},... | collective-permute-start | bytes 608264 | tf_op jit(solution)/shard_map/ppermute | solution.py:84
  18.1 2.5 %collective-permute-start.3 = (bf16[4,96,264]{1,0,2:T(4,128)(2,1)S(1)}, bf16[4,96,264]{1,0,2:T(4,128)(2,1)S(1)}, u32[]{:S(2)}, u32[]{:S(2)}) collective-permute-start(bf16[4,96,264]{1,0,2:T(4,128)(2,1)S(1)} %get-tuple-element.8), channel_id=1, source_target_pairs={{16,0},{32,16},{48,32},{64,48},{80,64},{96,80},{112,96},{128,112},... | collective-permute-start | bytes 608264 | tf_op jit(solution)/shard_map/ppermute | solution.py:85
  20.7 0.8 copy.22
  21.6 5.1 %multiply_convert_fusion = bf16[30,8,33,128]{3,1,2,0:T(8,128)(2,1)S(1)} fusion(f32[128]{0:T(128)S(1)} %copy-done.7, pred[8,33]{0,1:T(8,128)(4,1)S(1)} %copy-done.9, bf16[3,3,96,128]{3,2,1,0:T(8,128)(2,1)S(1)} %copy-done.6, bf16[32,96,1,7,2]{1,3,4,0,2:T(8,128)(2,1)S(1)} %slice.54, bf16[32,96,1,8,33]{1,3,4,0,2:T(8,128)(2,1)S(1)} %copy.22), kind=kOutput, calls=%fused_computation.8 | convolution fusion | flops 1764034560 | bytes 3957512 | tf_op jit(solution)/shard_map/conv_general_dilated | solution.py:40
  26.7 0.4 copy.23
  27.0 0.4 slice_bitcast_fusion.1
  27.4 0.2 fusion.106
  27.7 3.9 %collective-permute-done.3 = bf16[4,96,264]{1,0,2:T(4,128)(2,1)S(1)} collective-permute-done((bf16[4,96,264]{1,0,2:T(4,128)(2,1)S(1)}, bf16[4,96,264]{1,0,2:T(4,128)(2,1)S(1)}, u32[]{:S(2)}, u32[]{:S(2)}) %collective-permute-start.3) | collective-permute-done | bytes 202784 | tf_op jit(solution)/shard_map/ppermute | solution.py:85
  31.5 0.7 pad_maximum_fusion.1
  32.3 0.8 multiply_convert_fusion.3
  33.1 0.1 copy.20
  33.4 0.8 multiply_convert_fusion.2
  34.1 0.1 copy.27
  34.4 1.6 %fusion.13 = bf16[38,1,262,128]{3,0,2,1:T(8,128)(2,1)S(1)} fusion(bf16[1,4,262,128]{3,1,2,0:T(4,128)(2,1)S(1)} %slice_bitcast_fusion.3, bf16[1,30,262,128]{3,1,2,0:T(8,128)(2,1)S(1)} %slice_bitcast_fusion.1, bf16[1,4,262,128]{3,1,2,0:T(4,128)(2,1)S(1)} %slice_bitcast_fusion.4, pred[38]{0:T(512)(128)(4,1)S(1)} %compare_and_fusion), kind=kLoop, calls=%fused_computation.18 | loop fusion | flops 8920576 | bytes 5097510 | tf_op jit(solution)/shard_map/jit(_where)/select_n | solution.py:36
  36.0 0.5 pad.3
  36.5 0.7 copy.29
  37.3 0.4 copy-done.5
  37.7 2.9 %fusion.24 = f32[18,8,17,256]{3,1,2,0:T(8,128)S(1)} fusion(bf16[4,4,128,256]{3,2,1,0:T(8,128)(2,1)S(1)} %copy-done.5, bf16[38,1,7,3,128]{4,2,3,0,1:T(8,128)(2,1)S(1)} %slice.60, bf16[38,1,8,34,128]{4,2,3,0,1:T(8,128)(2,1)S(1)} %copy.29, pred[8,17]{0,1:T(8,128)(4,1)S(1)} %copy-done.10), kind=kOutput, calls=%fused_computation.31 | convolution fusion | flops 2576179200 | bytes 6405768 | tf_op jit(solution)/shard_map/conv_general_dilated | solution.py:52
  40.6 2.7 %copy.30 = f32[18,8,17,256]{3,2,1,0:T(8,128)} copy(f32[18,8,17,256]{3,1,2,0:T(8,128)S(1)} %fusion.24) | data formatting | bytes 5013504 | tf_op jit(solution)/shard_map/conv_general_dilated | solution.py:52
  43.3 4.2 %reshape.115 = f32[18,1,136,256]{3,2,0,1:T(8,128)} reshape(f32[18,8,17,256]{3,2,1,0:T(8,128)} %copy.30) | data formatting | bytes 5013504 | tf_op jit(solution)/shard_map/conv_general_dilated | solution.py:52
  47.5 2.5 %fusion.39 = bf16[18,130,256]{2,1,0:T(8,128)(2,1)S(1)} fusion(f32[256]{0:T(256)S(1)} %copy-done.2, f32[18,1,136,256]{3,2,0,1:T(8,128)} %reshape.115, pred[18]{0:T(512)(128)(4,1)S(1)} %compare_and_fusion.1), kind=kLoop, calls=%fused_computation.40 | loop fusion | flops 4193280 | bytes 3595282 | tf_op jit(solution)/shard_map/jit(_where)/select_n | solution.py:36
  50.1 1.4 %reshape.118 = bf16[18,1,8,18,256]{4,3,2,0,1:T(8,128)(2,1)} reshape(bf16[18,1,144,256]{3,2,0,1:T(8,128)(2,1)S(1)} %pad.5) | data formatting | bytes 2654208 | tf_op jit(solution)/shard_map/conv_general_dilated | solution.py:52
  51.5 1.8 %copy.32 = bf16[18,1,8,18,256]{4,2,3,0,1:T(8,128)(2,1)S(1)} copy(bf16[18,1,8,18,256]{4,3,2,0,1:T(8,128)(2,1)} %reshape.118) | data formatting | bytes 2654208 | tf_op jit(solution)/shard_map/conv_general_dilated | solution.py:52
  53.4 1.4 %fusion.42 = f32[8,8,9,256]{3,1,2,0:T(8,128)S(1)} fusion(bf16[4,4,256,256]{3,2,1,0:T(8,128)(2,1)S(1)} %copy-done, bf16[18,1,7,3,256]{4,2,3,0,1:T(8,128)(2,1)S(1)} %slice.62, bf16[18,1,8,18,256]{4,2,3,0,1:T(8,128)(2,1)S(1)} %copy.32, pred[8,9]{0,1:T(8,128)(4,1)S(1)} %copy-done.11), kind=kOutput, calls=%fused_computation.46 | convolution fusion | flops 1212751872 | bytes 4207688 | tf_op jit(solution)/shard_map/conv_general_dilated | solution.py:52
  54.9 0.2 copy.33
  55.1 0.3 convert_reduce_fusion
  55.4 0.3 fusion.64
  55.7 0.2 fusion.66
  55.9 0.9 broadcast_in_dim.57
  56.8 5.3 %all-to-all-start = ((bf16[16,64,256]{2,1,0:T(8,128)(2,1)}), bf16[16,64,256]{2,1,0:T(8,128)(2,1)S(1)}, u32[]{:S(2)}, u32[]{:S(2)}) async-start(bf16[16,64,256]{2,1,0:T(8,128)(2,1)} %bitcast.21), calls=%async_computation | async-start | bytes 1048576 | tf_op jit(solution)/shard_map/all_to_all | solution.py:112
  62.1 1.2 %copy.35 = bf16[256,768]{0,1:T(8,128)(2,1)S(1)} copy(bf16[256,768]{1,0:T(8,128)(2,1)} %param.19) | data formatting | bytes 786432 | tf_op args[8]
  63.4 9.5 %all-to-all-done = bf16[16,64,256]{2,1,0:T(8,128)(2,1)S(1)} async-done(((bf16[16,64,256]{2,1,0:T(8,128)(2,1)}), bf16[16,64,256]{2,1,0:T(8,128)(2,1)S(1)}, u32[]{:S(2)}, u32[]{:S(2)}) %all-to-all-start) | async-done | bytes 524320 | tf_op jit(solution)/shard_map/all_to_all | solution.py:112
  72.9 1.3 %fusion.108 = (bf16[3,4,1024,32]{2,3,1,0:T(8,128)(2,1)}, f32[3,4,1024,32]{2,3,1,0:T(8,128)S(1)}) fusion(bf16[1024,256,1,1]{1,0,3,2:T(8,128)(2,1)S(1)} %bitcast.122, bf16[256,3,8,32]{0,3,2,1:T(8,128)(2,1)S(1)} %bitcast.127, s32[]{:T(128)S(6)} %select_n.34), kind=kOutput, calls=%fused_computation.118 | convolution fusion | flops 201719808 | bytes 3080196 | tf_op jit(solution)/shard_map/tc,cjhd->jhtd/dot_general | solution.py:116
  74.2 0.1 fusion.68
  74.3 5.5 %fusion.109 = f32[4,1024]{1,0:T(4,128)S(1)} fusion(bf16[4,1024,32]{1,2,0:T(8,128)(2,1)S(1)} %fusion.68, bf16[3,4,1024,32]{2,3,1,0:T(8,128)(2,1)} %get-tuple-element.13), kind=kOutput, calls=%fused_computation.119 | convolution fusion | flops 276825088 | bytes 540672 | tf_op jit(solution)/shard_map/sub | solution.py:124
  79.8 6.6 %fusion.54 = bf16[4,1024,32]{1,2,0:T(8,128)(2,1)S(1)} fusion(bf16[4,1024,32]{1,2,0:T(8,128)(2,1)S(1)} %fusion.68, bf16[3,4,1024,32]{2,3,1,0:T(8,128)(2,1)} %get-tuple-element.13, f32[4,1024]{1,0:T(4,128)S(1)} %fusion.109), kind=kOutput, calls=%fused_computation.50 | convolution fusion | flops 545526784 | bytes 1064960 | tf_op jit(solution)/shard_map/ist,itd->isd/dot_general | solution.py:126
  86.4 0.3 reshape.91
  86.8 0.1 copy.58
  86.9 0.4 reshape.165
  87.3 10.4 %all_to_all.10 = bf16[16,2,4096]{2,1,0:T(2,128)(2,1)S(1)} all-to-all(bf16[16,2,4096]{2,1,0:T(2,128)(2,1)S(1)} %reshape.165), channel_id=1, replica_groups=mesh['lat'=16,'lon'=16] {'lon'}, dimensions={0} | all-to-all | bytes 524288 | tf_op jit(solution)/shard_map/all_to_all | solution.py:132
  97.8 0.3 reshape.166
  98.1 1.0 %fusion.45 = bf16[8,64,256]{2,1,0:T(8,128)(2,1)} fusion(bf16[8,64,256]{1,2,0:T(8,128)(2,1)S(1)} %bitcast.123, bf16[8,64,256]{2,1,0:T(8,128)(2,1)S(1)} %get-tuple-element.6, bf16[256,256]{1,0:T(8,128)(2,1)S(1)} %copy-done.1), kind=kOutput, calls=%fused_computation.47 | convolution fusion | flops 67502080 | bytes 917504 | tf_op jit(solution)/shard_map/dot_general | solution.py:135
  (43 shorter events, 0.8 us)
Async XLA Ops:
  0.0 53.4 %copy-start = (bf16[4,4,256,256]{3,2,1,0:T(8,128)(2,1)S(1)}, bf16[4,4,256,256]{3,2,1,0:T(8,128)(2,1)}, u32[]{:S(2)}) copy-start(bf16[4,4,256,256]{3,2,1,0:T(8,128)(2,1)} %param.16) | copy-start | bytes 6291460
  5.4 5.4 %collective-permute-start = (bf16[32,96,4]{1,0,2:T(8,128)(2,1)S(1)}, bf16[32,96,4]{1,0,2:T(8,128)(2,1)S(1)}, u32[]{:S(2)}, u32[]{:S(2)}) collective-permute-start(bf16[32,96,4]{1,0,2:T(8,128)(2,1)S(1)} %get-tuple-element.11), channel_id=1, source_target_pairs={{0,1},{1,2},{2,3},{3,4},{4,5},{5,6},{6,7},{7,8},{8,9},{9,10},{10,1... | collective-permute-start | bytes 73736 | tf_op jit(solution)/shard_map/ppermute | solution.py:81
  5.4 5.4 %collective-permute-start.1 = (bf16[32,96,4]{1,0,2:T(8,128)(2,1)S(1)}, bf16[32,96,4]{1,0,2:T(8,128)(2,1)S(1)}, u32[]{:S(2)}, u32[]{:S(2)}) collective-permute-start(bf16[32,96,4]{1,0,2:T(8,128)(2,1)S(1)} %get-tuple-element.12), channel_id=1, source_target_pairs={{1,0},{2,1},{3,2},{4,3},{5,4},{6,5},{7,6},{8,7},{9,8},{10,9},{11,1... | collective-permute-start | bytes 73736 | tf_op jit(solution)/shard_map/ppermute | solution.py:82
  13.1 8.4 %copy-start.6 = (bf16[3,3,96,128]{3,2,1,0:T(8,128)(2,1)S(1)}, bf16[3,3,96,128]{3,2,1,0:T(8,128)(2,1)}, u32[]{:S(2)}) copy-start(bf16[3,3,96,128]{3,2,1,0:T(8,128)(2,1)} %param.12) | copy-start | bytes 663556
  13.1 8.4 %copy-start.7 = (f32[128]{0:T(128)S(1)}, f32[128]{0:T(128)}, u32[]{:S(2)}) copy-start(f32[128]{0:T(128)} %param.13) | copy-start | bytes 1540
  13.2 8.4 %copy-start.9 = (pred[8,33]{0,1:T(8,128)(4,1)S(1)}, pred[8,33]{0,1:T(8,128)(4,1)}, u32[]{:S(2)}) copy-start(pred[8,33]{0,1:T(8,128)(4,1)} %constant.94) | copy-start | bytes 796
  13.2 14.5 %collective-permute-start.2 = (bf16[4,96,264]{1,0,2:T(4,128)(2,1)S(1)}, bf16[4,96,264]{1,0,2:T(4,128)(2,1)S(1)}, u32[]{:S(2)}, u32[]{:S(2)}) collective-permute-start(bf16[4,96,264]{1,0,2:T(4,128)(2,1)S(1)} %get-tuple-element.7), channel_id=1, source_target_pairs={{0,16},{16,32},{32,48},{48,64},{64,80},{80,96},{96,112},{112,128},... | collective-permute-start | bytes 608264 | tf_op jit(solution)/shard_map/ppermute | solution.py:84
  18.1 13.4 %collective-permute-start.3 = (bf16[4,96,264]{1,0,2:T(4,128)(2,1)S(1)}, bf16[4,96,264]{1,0,2:T(4,128)(2,1)S(1)}, u32[]{:S(2)}, u32[]{:S(2)}) collective-permute-start(bf16[4,96,264]{1,0,2:T(4,128)(2,1)S(1)} %get-tuple-element.8), channel_id=1, source_target_pairs={{16,0},{32,16},{48,32},{64,48},{80,64},{96,80},{112,96},{128,112},... | collective-permute-start | bytes 608264 | tf_op jit(solution)/shard_map/ppermute | solution.py:85
  36.5 1.2 %copy-start.5 = (bf16[4,4,128,256]{3,2,1,0:T(8,128)(2,1)S(1)}, bf16[4,4,128,256]{3,2,1,0:T(8,128)(2,1)}, u32[]{:S(2)}) copy-start(bf16[4,4,128,256]{3,2,1,0:T(8,128)(2,1)} %param.14) | copy-start | bytes 3145732
  36.5 1.2 %copy-start.10 = (pred[8,17]{0,1:T(8,128)(4,1)S(1)}, pred[8,17]{0,1:T(8,128)(4,1)}, u32[]{:S(2)}) copy-start(pred[8,17]{0,1:T(8,128)(4,1)} %constant.93) | copy-start | bytes 412
  43.3 4.2 %copy-start.2 = (f32[256]{0:T(256)S(1)}, f32[256]{0:T(256)}, u32[]{:S(2)}) copy-start(f32[256]{0:T(256)} %param.15) | copy-start | bytes 3076
  51.5 1.9 %copy-start.11 = (pred[8,9]{0,1:T(8,128)(4,1)S(1)}, pred[8,9]{0,1:T(8,128)(4,1)}, u32[]{:S(2)}) copy-start(pred[8,9]{0,1:T(8,128)(4,1)} %constant.92) | copy-start | bytes 220
  53.4 1.7 %copy-start.3 = (f32[256]{0:T(256)S(1)}, f32[256]{0:T(256)}, u32[]{:S(2)}) copy-start(f32[256]{0:T(256)} %param.17) | copy-start | bytes 3076
  54.8 0.9 copy-start.4
  55.0 8.2 %copy-start.8 = (f32[8]{0:T(128)S(1)}, f32[8]{0:T(128)}, u32[]{:S(2)}) copy-start(f32[8]{0:T(128)} %param.20) | copy-start | bytes 100
  56.8 16.1 %all-to-all-start = ((bf16[16,64,256]{2,1,0:T(8,128)(2,1)}), bf16[16,64,256]{2,1,0:T(8,128)(2,1)S(1)}, u32[]{:S(2)}, u32[]{:S(2)}) async-start(bf16[16,64,256]{2,1,0:T(8,128)(2,1)} %bitcast.21), calls=%async_computation | async-start | bytes 1048576 | tf_op jit(solution)/shard_map/all_to_all | solution.py:112
  86.4 11.7 %copy-start.1 = (bf16[256,256]{1,0:T(8,128)(2,1)S(1)}, bf16[256,256]{1,0:T(8,128)(2,1)}, u32[]{:S(2)}) copy-start(bf16[256,256]{1,0:T(8,128)(2,1)} %param.21) | copy-start | bytes 393220
